TPU v7x, 256 devices: a whole 4x4x8 slice. The times are simulated.
256 devices in a mesh: sub: 16 (over y, z_lo), grp: 16 (over x, z_hi, core).
Axes of the slice: x: 4, y: 4, z: 8 (z_hi: 2, z_lo: 4; z = z_hi * 4 + z_lo), core: 2. Of those that a mesh axis runs over, the one named last changes fastest.
Arguments:
- facies: int32 [256, 128, 128], P('sub', 'grp'), may hold values from 0 to 7
- facies_perm: float32 [8], replicated, may hold values from 0.2 to 5
- perm_scale: float32 [256, 128, 128], P('sub', 'grp'), may hold values from 0.5 to 2
- source: float32 [256, 128, 128], P('sub', 'grp'), may hold values from -6 to 6
- pressure_start: float32 [256, 128, 128], P('sub', 'grp'), may hold values from -4 to 4
- intersection_depth: int32 [15], replicated, may hold values from 1 to 4, as said below
Outputs:
- pressure: float32 [256, 128, 128], P('sub', 'grp')
Inputs may be any that keep to these rules, and one draw needn't show every extreme that they name: `intersection_depth`: every entry is a margin depth; some entry equals 4 in every draw.
All inputs are finite; a program needn't handle non-finite values.
Results may differ from a plain program's by a relative error of at most 0.0003.
Values sent between devices are 32-bit elements; how exact they have to be, the bound alone decides.
No kernel may reach another device: no remote copies, remote signals or barrier semaphores. Data moves between devices by JAX's collectives and lax.ppermute only.
A program may use at most 64 MiB of HBM per device.

v0:
```python
import math

import jax
import jax.numpy as jnp
from jax import lax
from jax.sharding import PartitionSpec as P
from jax.experimental import pallas as pl
from jax.experimental.pallas import tpu as pltpu

OV = 4
BL = 8
ROUNDS = 4
OUTER = 2
FACIES = 8


STORE = 0.02


def relax_weight(round_index):
    return 1.0 / (1.4 + 0.6 * math.cos(math.pi * (2 * round_index + 1) / (2 * ROUNDS)))


def harmonic(former, second):
    inside = jnp.where((former > 0) & (second > 0), 1.0, 0.0)
    safe_former = jnp.where(former > 0, former, 1.0)
    safe_second = jnp.where(second > 0, second, 1.0)
    return inside * (2.0 * safe_former * safe_second / (safe_former + safe_second))


def lower_nb(field, axis, fill=0.0):
    extent = field.shape[axis]
    plane = jnp.full_like(lax.slice_in_dim(field, 0, 1, axis=axis), fill)
    return jnp.concatenate([plane, lax.slice_in_dim(field, 0, extent - 1, axis=axis)], axis=axis)


def upper_nb(field, axis, fill=0.0):
    extent = field.shape[axis]
    plane = jnp.full_like(lax.slice_in_dim(field, 0, 1, axis=axis), fill)
    return jnp.concatenate([lax.slice_in_dim(field, 1, extent, axis=axis), plane], axis=axis)


def apply_operator(coeffs, center):
    diagonal, face_below, face_above, face_left, face_right, face_front, face_back = coeffs
    coupled = (
        face_below * lower_nb(center, 0)
        + face_above * upper_nb(center, 0)
        + face_left * lower_nb(center, 1)
        + face_right * upper_nb(center, 1)
        + face_front * lower_nb(center, 2)
        + face_back * upper_nb(center, 2)
    )
    return diagonal * center - coupled


def block_position(shape, axis):
    broadcast_shape = [1] * len(shape)
    broadcast_shape[axis] = shape[axis]
    return (jnp.arange(shape[axis], dtype=jnp.int32) % BL).reshape(broadcast_shape)


def factor_lines(lower_band, middle, upper_band, axis):
    upper_prev = lower_nb(upper_band, axis)
    pivots = middle
    for _ in range(BL - 1):
        pivots = middle - (lower_band / lower_nb(pivots, axis, 1.0)) * upper_prev
    multipliers = lower_band / lower_nb(pivots, axis, 1.0)
    return (multipliers, 1.0 / pivots, upper_band, axis)


def solve_lines(factors, rhs):
    multipliers, inverse, upper_band, axis = factors
    forward = rhs
    for _ in range(BL - 1):
        forward = rhs - multipliers * lower_nb(forward, axis)
    result = forward * inverse
    for _ in range(BL - 1):
        result = (forward - upper_band * upper_nb(result, axis)) * inverse
    return result


def line_factors(coeffs, active, axis):
    diagonal = coeffs[0]
    line_axis = {0: 0, 1: 1, 2: 2}[axis]
    face_low = coeffs[2 * line_axis + 1]
    face_high = coeffs[2 * line_axis + 2]
    position = block_position(diagonal.shape, axis)
    if axis == 0:
        active_low = lower_nb(active, 0)
        active_high = upper_nb(active, 0)
    else:
        active_low = active
        active_high = active
    lower_band = jnp.where(position != 0, -face_low * active * active_low, 0.0)
    upper_band = jnp.where(position != BL - 1, -face_high * active * active_high, 0.0)
    middle = jnp.where(active > 0, diagonal, 1.0)
    return factor_lines(lower_band, middle, upper_band, axis)


def make_round_kernel(weight_now, weight_next, last, own_cols):
    def kernel(
        e_ref, t_ref, d_ref, fb_ref, fa_ref, fl_ref, fr_ref, ff_ref, fk_ref, act_ref,
        ym_ref, yi_ref, yu_ref, zm_ref, zi_ref, zu_ref, xm_ref, xi_ref, xu_ref,
        o_ref, s_ref, f_ref,
    ):
        rows, cols, lanes = e_ref.shape

        def row_lower(x):
            return jnp.concatenate([jnp.zeros_like(x[:1]), x[:-1]], axis=0)

        def row_upper(x):
            return jnp.concatenate([x[1:], jnp.zeros_like(x[:1])], axis=0)

        def operate(e):
            coupled = (
                fb_ref[...] * row_lower(e)
                + fa_ref[...] * row_upper(e)
                + fl_ref[...] * pltpu.roll(e, 1, 1)
                + fr_ref[...] * pltpu.roll(e, cols - 1, 1)
                + ff_ref[...] * pltpu.roll(e, 1, 2)
                + fk_ref[...] * pltpu.roll(e, lanes - 1, 2)
            )
            return d_ref[...] * e - coupled

        def roll_solve(rhs, m, inv, u, axis, extent):
            forward = rhs
            for _ in range(BL - 1):
                forward = rhs - m * pltpu.roll(forward, 1, axis)
            result = forward * inv
            for _ in range(BL - 1):
                result = (forward - u * pltpu.roll(result, extent - 1, axis)) * inv
            return result

        act = act_ref[...]
        target = t_ref[...]
        e = e_ref[...]
        update = act * (target - operate(e))
        e = e + weight_now * roll_solve(update, ym_ref[...], yi_ref[...], yu_ref[...], 2, lanes)
        s_ref[...] = act * (target - operate(e))
        for block in range(rows // BL):
            base = block * BL
            forward = s_ref[base]
            f_ref[base] = forward
            for position in range(1, BL):
                r = base + position
                forward = s_ref[r] - zm_ref[r] * forward
                f_ref[r] = forward
            result = forward * zi_ref[base + BL - 1]
            s_ref[base + BL - 1] = result
            for position in range(BL - 2, -1, -1):
                r = base + position
                result = (f_ref[r] - zu_ref[r] * result) * zi_ref[r]
                s_ref[r] = result
        e = e + weight_now * s_ref[...]
        if last:
            o_ref[...] = e
        else:
            update = (act * (target - operate(e)))[:, own_cols]
            o_ref[...] = e[:, own_cols] + weight_next * roll_solve(
                update, xm_ref[...], xi_ref[...], xu_ref[...], 1, BL
            )

    return kernel


def round_call(weight_now, weight_next, last, tile_cols, estimate, target, coeffs, active, fy, fz, fx):
    own_cols = slice(tile_cols, 2 * tile_cols)
    shape = estimate.shape
    out_shape = shape if last else (shape[0], tile_cols, shape[2])
    return pl.pallas_call(
        make_round_kernel(weight_now, weight_next, last, own_cols),
        out_shape=jax.ShapeDtypeStruct(out_shape, jnp.float32),
        scratch_shapes=[pltpu.VMEM(shape, jnp.float32), pltpu.VMEM(shape, jnp.float32)],
    )(estimate, target, *coeffs, active, *fy[:3], *fz[:3], *fx[:3])


def grp_pairs(axis, by):
    devices = lax.axis_size(axis)
    return [(i, i + by) for i in range(devices) if 0 <= i + by < devices]


def with_sides(value, axis, dim):
    from_left = lax.ppermute(value, axis, grp_pairs(axis, 1))
    from_right = lax.ppermute(value, axis, grp_pairs(axis, -1))
    return jnp.concatenate([from_left, value, from_right], axis=dim)


def with_rows(value, axis, dim, width):
    length = value.shape[dim]
    below = lax.ppermute(
        lax.slice_in_dim(value, length - width, length, axis=dim), axis, grp_pairs(axis, 1)
    )
    above = lax.ppermute(lax.slice_in_dim(value, 0, width, axis=dim), axis, grp_pairs(axis, -1))
    return jnp.concatenate([below, value, above], axis=dim)


def on_device(facies, facies_perm, perm_scale, source, pressure_start, intersection_depth):
    slab_rows, tile_cols, line_cells = source.shape
    margin_rows = slab_rows + 2 * OV
    perm_local = jnp.zeros(source.shape, jnp.float32)
    for facies_kind in range(FACIES):
        perm_local = perm_local + jnp.where(facies == facies_kind, facies_perm[facies_kind], 0.0)
    perm_local = perm_local * perm_scale

    stacked = jnp.stack([perm_local, pressure_start, source])
    stacked = with_rows(stacked, "sub", 1, OV + 1)
    stacked = with_sides(stacked, "grp", 2)
    perm_wide = stacked[0]
    pressure_wide = stacked[1]
    source_wide = stacked[2][1:-1]

    faces_vertical = harmonic(perm_wide[:-1], perm_wide[1:])
    middle_block = perm_wide[1:-1]
    faces_across = harmonic(middle_block[:, :-1], middle_block[:, 1:])
    faces_along = harmonic(middle_block[:, :, :-1], middle_block[:, :, 1:])
    zero_col = jnp.zeros_like(middle_block[:, :1])
    zero_lane = jnp.zeros_like(middle_block[:, :, :1])
    face_below = faces_vertical[:-1]
    face_above = faces_vertical[1:]
    face_left = jnp.concatenate([zero_col, faces_across], axis=1)
    face_right = jnp.concatenate([faces_across, zero_col], axis=1)
    face_front = jnp.concatenate([zero_lane, faces_along], axis=2)
    face_back = jnp.concatenate([faces_along, zero_lane], axis=2)
    diagonal = STORE + face_below + face_above + face_left + face_right + face_front + face_back
    coeffs = (diagonal, face_below, face_above, face_left, face_right, face_front, face_back)
    own = slice(tile_cols, 2 * tile_cols)
    own_coeffs = tuple(member[:, own] for member in coeffs)

    slab_index = lax.axis_index("sub")
    bounds = jnp.concatenate(
        [jnp.zeros((1,), jnp.int32), intersection_depth, jnp.zeros((1,), jnp.int32)]
    )
    depth_low = bounds[slab_index]
    depth_high = bounds[slab_index + 1]
    offsets = jnp.arange(margin_rows, dtype=jnp.int32) - OV
    inside_slab = (offsets >= -depth_low) & (offsets < slab_rows + depth_high)
    band_rows = (offsets < depth_low) | (offsets >= slab_rows - depth_high)
    active = jnp.where(inside_slab, 1.0, 0.0).reshape(margin_rows, 1, 1)
    weight = jnp.where(inside_slab & band_rows, 0.5, jnp.where(inside_slab, 1.0, 0.0)).reshape(
        margin_rows, 1, 1
    )
    full_active = jnp.broadcast_to(active, diagonal.shape)
    own_active = jnp.broadcast_to(active, own_coeffs[0].shape)
    factors_x = line_factors(own_coeffs, own_active, 1)
    factors_y = line_factors(coeffs, full_active, 2)
    factors_z = line_factors(coeffs, full_active, 0)

    rows_pad = jnp.zeros_like(pressure_wide[:1])
    for outer_turn in range(OUTER):
        center = pressure_wide[1:-1]
        coupled = (
            face_below * pressure_wide[:-2]
            + face_above * pressure_wide[2:]
            + face_left * lower_nb(center, 1)
            + face_right * upper_nb(center, 1)
            + face_front * lower_nb(center, 2)
            + face_back * upper_nb(center, 2)
        )
        residual = source_wide - (diagonal * center - coupled)
        target = residual * active
        estimate_own = relax_weight(0) * solve_lines(factors_x, target[:, own])
        for round_index in range(ROUNDS):
            estimate = with_sides(estimate_own, "grp", 1)
            last = round_index + 1 == ROUNDS
            estimate = round_call(
                relax_weight(round_index),
                0.0 if last else relax_weight(round_index + 1),
                last,
                tile_cols,
                estimate,
                target,
                coeffs,
                full_active,
                factors_y,
                factors_z,
                factors_x,
            )
            estimate_own = estimate
        correction = weight * estimate
        if outer_turn + 1 < OUTER:
            span = 2 * OV + 1
            from_below = lax.ppermute(
                correction[margin_rows - span :], "sub", grp_pairs("sub", 1)
            )
            from_above = lax.ppermute(correction[:span], "sub", grp_pairs("sub", -1))
            filler = jnp.zeros(
                (margin_rows + 2 - span,) + correction.shape[1:], jnp.float32
            )
            pressure_wide = (
                pressure_wide
                + jnp.concatenate([rows_pad, correction, rows_pad], axis=0)
                + jnp.concatenate([from_below, filler], axis=0)
                + jnp.concatenate([filler, from_above], axis=0)
            )
        else:
            own_corr = correction[:, own]
            from_below = lax.ppermute(
                own_corr[margin_rows - OV :], "sub", grp_pairs("sub", 1)
            )
            from_above = lax.ppermute(own_corr[:OV], "sub", grp_pairs("sub", -1))
            filler = jnp.zeros((slab_rows - OV, tile_cols, line_cells), jnp.float32)
            combined = (
                own_corr[OV : OV + slab_rows]
                + jnp.concatenate([from_below, filler], axis=0)
                + jnp.concatenate([filler, from_above], axis=0)
            )
            return pressure_wide[OV + 1 : OV + 1 + slab_rows, own] + combined


def solution(mesh):
    return jax.shard_map(
        on_device,
        mesh=mesh,
        in_specs=(
            P("sub", "grp", None),
            P(),
            P("sub", "grp", None),
            P("sub", "grp", None),
            P("sub", "grp", None),
            P(),
        ),
        out_specs=P("sub", "grp", None),
        check_vma=False,
    )
```

profile of v0, /device:TPU:225, one launch (start us, length us, event | category | flops | bytes accessed | tf_op | source)
XLA Modules:
  0.0 233.7 jit_solution(14575171591635947033)
XLA Ops:
  1.6 6.0 %multiply_bitcast_fusion = f32[1,16,8,128]{3,2,1,0:T(8,128)S(1)} fusion(f32[16,8,128]{2,1,0:T(8,128)} %param.8, s32[16,8,128]{2,1,0:T(8,128)} %param.6, f32[]{:T(128)} %bitcast.7, f32[]{:T(128)} %bitcast.6, f32[]{:T(128)} %bitcast.5, f32[]{:T(128)} %bitcast.4, f32[]{:T(128)} %bitcast.3, f32[]{:T(128)} %bitcast.2, f32[]{:T(128)} %bitcast.1, f32[]{:T(128)} %bitcast), kind=kLoop, calls=%fused_computation.201 | loop fusion | flops 393216 | bytes 196640 | tf_op jit(solution)/shard_map/stack | solution.py:205
  7.6 4.5 %collective-permute-start = (f32[3,5,8,128]{3,2,1,0:T(8,128)S(1)}, f32[3,5,8,128]{3,2,1,0:T(8,128)S(1)}, u32[]{:S(2)}, u32[]{:S(2)}) collective-permute-start(f32[3,5,8,128]{3,2,1,0:T(8,128)S(1)} %get-tuple-element.41), channel_id=1, source_target_pairs={{0,16},{16,32},{32,48},{48,64},{64,80},{80,96},{96,112},{112,128},... | collective-permute-start | bytes 184328 | tf_op jit(solution)/shard_map/ppermute | solution.py:190
  25.9 4.6 %collective-permute-done.2 = f32[3,26,8,128]{3,2,1,0:T(8,128)S(1)} collective-permute-done((f32[3,26,8,128]{3,2,1,0:T(8,128)S(1)}, f32[3,26,8,128]{3,2,1,0:T(8,128)S(1)}, u32[]{:S(2)}, u32[]{:S(2)}) %collective-permute-start.2) | collective-permute-done | bytes 319520 | tf_op jit(solution)/shard_map/ppermute | solution.py:183
  30.5 10.8 %collective-permute-done.3 = f32[3,26,8,128]{3,2,1,0:T(8,128)S(1)} collective-permute-done((f32[3,26,8,128]{3,2,1,0:T(8,128)S(1)}, f32[3,26,8,128]{3,2,1,0:T(8,128)S(1)}, u32[]{:S(2)}, u32[]{:S(2)}) %collective-permute-start.3) | collective-permute-done | bytes 319520 | tf_op jit(solution)/shard_map/ppermute | solution.py:184
  59.6 4.8 %shard_map.64 = f32[24,8,128]{2,1,0:T(8,128)} custom-call(f32[24,24,128]{2,1,0:T(8,128)} %pad_maximum_fusion.2.e_ref, f32[24,24,128]{2,1,0:T(8,128)} %copy-done.9, f32[24,24,128]{2,1,0:T(8,128)} %copy-done.8, f32[24,24,128]{2,1,0:T(8,128)} %get-tuple-element.21.fb_ref, f32[24,24,128]{2,1,0:T(8,128)} %get-tuple-element.20.fa_ref, ...), custom_call_target="tpu_custom_call" | custom-call | tf_op jit(solution)/shard_map/pallas_call | solution.py:170
  64.4 6.2 %collective-permute-start.6 = (f32[24,8,128]{2,1,0:T(8,128)}, f32[24,8,128]{2,1,0:T(8,128)S(1)}, u32[]{:S(2)}, u32[]{:S(2)}) collective-permute-start(f32[24,8,128]{2,1,0:T(8,128)} %shard_map.64), channel_id=1, source_target_pairs={{0,1},{1,2},{2,3},{3,4},{4,5},{5,6},{6,7},{7,8},{8,9},{9,10},{10,1... | collective-permute-start | bytes 294920 | tf_op jit(solution)/shard_map/ppermute | solution.py:183
  72.6 9.0 %collective-permute-done.7 = f32[24,8,128]{2,1,0:T(8,128)S(1)} collective-permute-done((f32[24,8,128]{2,1,0:T(8,128)}, f32[24,8,128]{2,1,0:T(8,128)S(1)}, u32[]{:S(2)}, u32[]{:S(2)}) %collective-permute-start.7) | collective-permute-done | bytes 98336 | tf_op jit(solution)/shard_map/ppermute | solution.py:184
  83.2 4.8 %shard_map.65 = f32[24,8,128]{2,1,0:T(8,128)} custom-call(f32[24,24,128]{2,1,0:T(8,128)} %pad_maximum_fusion.3.e_ref, f32[24,24,128]{2,1,0:T(8,128)} %copy-done.9, f32[24,24,128]{2,1,0:T(8,128)} %copy-done.8, f32[24,24,128]{2,1,0:T(8,128)} %get-tuple-element.21.fb_ref, f32[24,24,128]{2,1,0:T(8,128)} %get-tuple-element.20.fa_ref, ...), custom_call_target="tpu_custom_call" | custom-call | tf_op jit(solution)/shard_map/pallas_call | solution.py:170
  93.1 7.7 %collective-permute-done.9 = f32[24,8,128]{2,1,0:T(8,128)S(1)} collective-permute-done((f32[24,8,128]{2,1,0:T(8,128)}, f32[24,8,128]{2,1,0:T(8,128)S(1)}, u32[]{:S(2)}, u32[]{:S(2)}) %collective-permute-start.9) | collective-permute-done | bytes 98336 | tf_op jit(solution)/shard_map/ppermute | solution.py:184
  102.5 4.8 %shard_map.66 = f32[24,8,128]{2,1,0:T(8,128)} custom-call(f32[24,24,128]{2,1,0:T(8,128)} %pad_maximum_fusion.4.e_ref, f32[24,24,128]{2,1,0:T(8,128)} %copy-done.9, f32[24,24,128]{2,1,0:T(8,128)} %copy-done.8, f32[24,24,128]{2,1,0:T(8,128)} %get-tuple-element.21.fb_ref, f32[24,24,128]{2,1,0:T(8,128)} %get-tuple-element.20.fa_ref, ...), custom_call_target="tpu_custom_call" | custom-call | tf_op jit(solution)/shard_map/pallas_call | solution.py:170
  112.3 7.9 %collective-permute-done.11 = f32[24,8,128]{2,1,0:T(8,128)S(1)} collective-permute-done((f32[24,8,128]{2,1,0:T(8,128)}, f32[24,8,128]{2,1,0:T(8,128)S(1)}, u32[]{:S(2)}, u32[]{:S(2)}) %collective-permute-start.11) | collective-permute-done | bytes 98336 | tf_op jit(solution)/shard_map/ppermute | solution.py:184
  121.8 4.7 %shard_map.67 = f32[24,24,128]{2,1,0:T(8,128)} custom-call(f32[24,24,128]{2,1,0:T(8,128)} %pad_maximum_fusion.5.e_ref, f32[24,24,128]{2,1,0:T(8,128)} %copy-done.9, f32[24,24,128]{2,1,0:T(8,128)} %copy-done.8, f32[24,24,128]{2,1,0:T(8,128)} %get-tuple-element.21.fb_ref, f32[24,24,128]{2,1,0:T(8,128)} %get-tuple-element.20.fa_ref, ...), custom_call_target="tpu_custom_call" | custom-call | tf_op jit(solution)/shard_map/pallas_call | solution.py:170
  127.6 5.1 %collective-permute-start.12 = (f32[9,24,128]{2,1,0:T(8,128)S(1)}, f32[9,24,128]{2,1,0:T(8,128)S(1)}, u32[]{:S(2)}, u32[]{:S(2)}) collective-permute-start(f32[9,24,128]{2,1,0:T(8,128)S(1)} %get-tuple-element.28), channel_id=1, source_target_pairs={{0,16},{16,32},{32,48},{48,64},{64,80},{80,96},{96,112},{112,128},... | collective-permute-start | bytes 331784 | tf_op jit(solution)/shard_map/ppermute | solution.py:282
  134.6 6.3 %collective-permute-done.13 = f32[9,24,128]{2,1,0:T(8,128)S(1)} collective-permute-done((f32[9,24,128]{2,1,0:T(8,128)S(1)}, f32[9,24,128]{2,1,0:T(8,128)S(1)}, u32[]{:S(2)}, u32[]{:S(2)}) %collective-permute-start.13) | collective-permute-done | bytes 110624 | tf_op jit(solution)/shard_map/ppermute | solution.py:285
  144.8 4.0 %collective-permute-start.14 = (f32[24,8,128]{2,1,0:T(8,128)S(1)}, f32[24,8,128]{2,1,0:T(8,128)S(1)}, u32[]{:S(2)}, u32[]{:S(2)}) collective-permute-start(f32[24,8,128]{2,1,0:T(8,128)S(1)} %multiply_multiply_fusion), channel_id=1, source_target_pairs={{0,1},{1,2},{2,3},{3,4},{4,5},{5,6},{6,7},{7,8},{8,9},{9,10},{10,1... | collective-permute-start | bytes 294920 | tf_op jit(solution)/shard_map/ppermute | solution.py:183
  150.8 8.8 %collective-permute-done.15 = f32[24,8,128]{2,1,0:T(8,128)S(1)} collective-permute-done((f32[24,8,128]{2,1,0:T(8,128)S(1)}, f32[24,8,128]{2,1,0:T(8,128)S(1)}, u32[]{:S(2)}, u32[]{:S(2)}) %collective-permute-start.15) | collective-permute-done | bytes 98336 | tf_op jit(solution)/shard_map/ppermute | solution.py:184
  160.3 4.8 %shard_map.68 = f32[24,8,128]{2,1,0:T(8,128)} custom-call(f32[24,24,128]{2,1,0:T(8,128)} %pad_maximum_fusion.6.e_ref, f32[24,24,128]{2,1,0:T(8,128)} %copy-done.10, f32[24,24,128]{2,1,0:T(8,128)} %copy-done.8, f32[24,24,128]{2,1,0:T(8,128)} %get-tuple-element.21.fb_ref, f32[24,24,128]{2,1,0:T(8,128)} %get-tuple-element.20.fa_ref, ...), custom_call_target="tpu_custom_call" | custom-call | tf_op jit(solution)/shard_map/pallas_call | solution.py:170
  169.5 8.5 %collective-permute-done.17 = f32[24,8,128]{2,1,0:T(8,128)S(1)} collective-permute-done((f32[24,8,128]{2,1,0:T(8,128)}, f32[24,8,128]{2,1,0:T(8,128)S(1)}, u32[]{:S(2)}, u32[]{:S(2)}) %collective-permute-start.17) | collective-permute-done | bytes 98336 | tf_op jit(solution)/shard_map/ppermute | solution.py:184
  179.6 4.8 %shard_map.69 = f32[24,8,128]{2,1,0:T(8,128)} custom-call(f32[24,24,128]{2,1,0:T(8,128)} %pad_maximum_fusion.7.e_ref, f32[24,24,128]{2,1,0:T(8,128)} %copy-done.10, f32[24,24,128]{2,1,0:T(8,128)} %copy-done.8, f32[24,24,128]{2,1,0:T(8,128)} %get-tuple-element.21.fb_ref, f32[24,24,128]{2,1,0:T(8,128)} %get-tuple-element.20.fa_ref, ...), custom_call_target="tpu_custom_call" | custom-call | tf_op jit(solution)/shard_map/pallas_call | solution.py:170
  188.8 8.5 %collective-permute-done.19 = f32[24,8,128]{2,1,0:T(8,128)S(1)} collective-permute-done((f32[24,8,128]{2,1,0:T(8,128)}, f32[24,8,128]{2,1,0:T(8,128)S(1)}, u32[]{:S(2)}, u32[]{:S(2)}) %collective-permute-start.19) | collective-permute-done | bytes 98336 | tf_op jit(solution)/shard_map/ppermute | solution.py:184
  198.9 4.8 %shard_map.70 = f32[24,8,128]{2,1,0:T(8,128)} custom-call(f32[24,24,128]{2,1,0:T(8,128)} %pad_maximum_fusion.8.e_ref, f32[24,24,128]{2,1,0:T(8,128)} %copy-done.10, f32[24,24,128]{2,1,0:T(8,128)} %copy-done.8, f32[24,24,128]{2,1,0:T(8,128)} %get-tuple-element.21.fb_ref, f32[24,24,128]{2,1,0:T(8,128)} %get-tuple-element.20.fa_ref, ...), custom_call_target="tpu_custom_call" | custom-call | tf_op jit(solution)/shard_map/pallas_call | solution.py:170
  208.1 8.5 %collective-permute-done.21 = f32[24,8,128]{2,1,0:T(8,128)S(1)} collective-permute-done((f32[24,8,128]{2,1,0:T(8,128)}, f32[24,8,128]{2,1,0:T(8,128)S(1)}, u32[]{:S(2)}, u32[]{:S(2)}) %collective-permute-start.21) | collective-permute-done | bytes 98336 | tf_op jit(solution)/shard_map/ppermute | solution.py:184
  218.3 4.7 %shard_map.71 = f32[24,24,128]{2,1,0:T(8,128)} custom-call(f32[24,24,128]{2,1,0:T(8,128)} %pad_maximum_fusion.9.e_ref, f32[24,24,128]{2,1,0:T(8,128)} %copy-done.10, f32[24,24,128]{2,1,0:T(8,128)} %copy-done.8, f32[24,24,128]{2,1,0:T(8,128)} %get-tuple-element.21.fb_ref, f32[24,24,128]{2,1,0:T(8,128)} %get-tuple-element.20.fa_ref, ...), custom_call_target="tpu_custom_call" | custom-call | tf_op jit(solution)/shard_map/pallas_call | solution.py:170
  229.3 3.8 %collective-permute-done.23 = f32[4,8,128]{2,1,0:T(8,128)S(1)} collective-permute-done((f32[4,8,128]{2,1,0:T(8,128)S(1)}, f32[4,8,128]{2,1,0:T(8,128)S(1)}, u32[]{:S(2)}, u32[]{:S(2)}) %collective-permute-start.23) | collective-permute-done | bytes 16416 | tf_op jit(solution)/shard_map/ppermute | solution.py:300
  (167 shorter events, 82.5 us)
Async XLA Ops:
  7.6 9.3 %collective-permute-start = (f32[3,5,8,128]{3,2,1,0:T(8,128)S(1)}, f32[3,5,8,128]{3,2,1,0:T(8,128)S(1)}, u32[]{:S(2)}, u32[]{:S(2)}) collective-permute-start(f32[3,5,8,128]{3,2,1,0:T(8,128)S(1)} %get-tuple-element.41), channel_id=1, source_target_pairs={{0,16},{16,32},{32,48},{48,64},{64,80},{80,96},{96,112},{112,128},... | collective-permute-start | bytes 184328 | tf_op jit(solution)/shard_map/ppermute | solution.py:190
  12.2 7.7 %collective-permute-start.1 = (f32[3,5,8,128]{3,2,1,0:T(8,128)S(1)}, f32[3,5,8,128]{3,2,1,0:T(8,128)S(1)}, u32[]{:S(2)}, u32[]{:S(2)}) collective-permute-start(f32[3,5,8,128]{3,2,1,0:T(8,128)S(1)} %get-tuple-element.42), channel_id=1, source_target_pairs={{16,0},{32,16},{48,32},{64,48},{80,64},{96,80},{112,96},{128,112},... | collective-permute-start | bytes 184328 | tf_op jit(solution)/shard_map/ppermute | solution.py:193
  19.9 10.6 %collective-permute-start.2 = (f32[3,26,8,128]{3,2,1,0:T(8,128)S(1)}, f32[3,26,8,128]{3,2,1,0:T(8,128)S(1)}, u32[]{:S(2)}, u32[]{:S(2)}) collective-permute-start(f32[3,26,8,128]{3,2,1,0:T(8,128)S(1)} %pad_maximum_fusion.1), channel_id=1, source_target_pairs={{0,1},{1,2},{2,3},{3,4},{4,5},{5,6},{6,7},{7,8},{8,9},{9,10},{10,1... | collective-permute-start | bytes 958472 | tf_op jit(solution)/shard_map/ppermute | solution.py:183
  23.2 18.2 %collective-permute-start.3 = (f32[3,26,8,128]{3,2,1,0:T(8,128)S(1)}, f32[3,26,8,128]{3,2,1,0:T(8,128)S(1)}, u32[]{:S(2)}, u32[]{:S(2)}) collective-permute-start(f32[3,26,8,128]{3,2,1,0:T(8,128)S(1)} %pad_maximum_fusion.1), channel_id=1, source_target_pairs={{1,0},{2,1},{3,2},{4,3},{5,4},{6,5},{7,6},{8,7},{9,8},{10,9},{11,1... | collective-permute-start | bytes 958472 | tf_op jit(solution)/shard_map/ppermute | solution.py:184
  45.3 11.0 %collective-permute-start.4 = (f32[24,8,128]{2,1,0:T(8,128)S(1)}, f32[24,8,128]{2,1,0:T(8,128)S(1)}, u32[]{:S(2)}, u32[]{:S(2)}) collective-permute-start(f32[24,8,128]{2,1,0:T(8,128)S(1)} %multiply_multiply_fusion.1), channel_id=1, source_target_pairs={{0,1},{1,2},{2,3},{3,4},{4,5},{5,6},{6,7},{7,8},{8,9},{9,10},{10,1... | collective-permute-start | bytes 294920 | tf_op jit(solution)/shard_map/ppermute | solution.py:183
  47.2 10.7 %collective-permute-start.5 = (f32[24,8,128]{2,1,0:T(8,128)S(1)}, f32[24,8,128]{2,1,0:T(8,128)S(1)}, u32[]{:S(2)}, u32[]{:S(2)}) collective-permute-start(f32[24,8,128]{2,1,0:T(8,128)S(1)} %multiply_multiply_fusion.1), channel_id=1, source_target_pairs={{1,0},{2,1},{3,2},{4,3},{5,4},{6,5},{7,6},{8,7},{9,8},{10,9},{11,1... | collective-permute-start | bytes 294920 | tf_op jit(solution)/shard_map/ppermute | solution.py:184
  64.4 8.2 %collective-permute-start.6 = (f32[24,8,128]{2,1,0:T(8,128)}, f32[24,8,128]{2,1,0:T(8,128)S(1)}, u32[]{:S(2)}, u32[]{:S(2)}) collective-permute-start(f32[24,8,128]{2,1,0:T(8,128)} %shard_map.64), channel_id=1, source_target_pairs={{0,1},{1,2},{2,3},{3,4},{4,5},{5,6},{6,7},{7,8},{8,9},{9,10},{10,1... | collective-permute-start | bytes 294920 | tf_op jit(solution)/shard_map/ppermute | solution.py:183
  70.6 11.0 %collective-permute-start.7 = (f32[24,8,128]{2,1,0:T(8,128)}, f32[24,8,128]{2,1,0:T(8,128)S(1)}, u32[]{:S(2)}, u32[]{:S(2)}) collective-permute-start(f32[24,8,128]{2,1,0:T(8,128)} %shard_map.64), channel_id=1, source_target_pairs={{1,0},{2,1},{3,2},{4,3},{5,4},{6,5},{7,6},{8,7},{9,8},{10,9},{11,1... | collective-permute-start | bytes 294920 | tf_op jit(solution)/shard_map/ppermute | solution.py:184
  88.0 5.1 %collective-permute-start.8 = (f32[24,8,128]{2,1,0:T(8,128)}, f32[24,8,128]{2,1,0:T(8,128)S(1)}, u32[]{:S(2)}, u32[]{:S(2)}) collective-permute-start(f32[24,8,128]{2,1,0:T(8,128)} %shard_map.65), channel_id=1, source_target_pairs={{0,1},{1,2},{2,3},{3,4},{4,5},{5,6},{6,7},{7,8},{8,9},{9,10},{10,1... | collective-permute-start | bytes 294920 | tf_op jit(solution)/shard_map/ppermute | solution.py:183
  89.9 11.0 %collective-permute-start.9 = (f32[24,8,128]{2,1,0:T(8,128)}, f32[24,8,128]{2,1,0:T(8,128)S(1)}, u32[]{:S(2)}, u32[]{:S(2)}) collective-permute-start(f32[24,8,128]{2,1,0:T(8,128)} %shard_map.65), channel_id=1, source_target_pairs={{1,0},{2,1},{3,2},{4,3},{5,4},{6,5},{7,6},{8,7},{9,8},{10,9},{11,1... | collective-permute-start | bytes 294920 | tf_op jit(solution)/shard_map/ppermute | solution.py:184
  107.3 5.0 %collective-permute-start.10 = (f32[24,8,128]{2,1,0:T(8,128)}, f32[24,8,128]{2,1,0:T(8,128)S(1)}, u32[]{:S(2)}, u32[]{:S(2)}) collective-permute-start(f32[24,8,128]{2,1,0:T(8,128)} %shard_map.66), channel_id=1, source_target_pairs={{0,1},{1,2},{2,3},{3,4},{4,5},{5,6},{6,7},{7,8},{8,9},{9,10},{10,1... | collective-permute-start | bytes 294920 | tf_op jit(solution)/shard_map/ppermute | solution.py:183
  109.2 11.0 %collective-permute-start.11 = (f32[24,8,128]{2,1,0:T(8,128)}, f32[24,8,128]{2,1,0:T(8,128)S(1)}, u32[]{:S(2)}, u32[]{:S(2)}) collective-permute-start(f32[24,8,128]{2,1,0:T(8,128)} %shard_map.66), channel_id=1, source_target_pairs={{1,0},{2,1},{3,2},{4,3},{5,4},{6,5},{7,6},{8,7},{9,8},{10,9},{11,1... | collective-permute-start | bytes 294920 | tf_op jit(solution)/shard_map/ppermute | solution.py:184
  127.6 7.0 %collective-permute-start.12 = (f32[9,24,128]{2,1,0:T(8,128)S(1)}, f32[9,24,128]{2,1,0:T(8,128)S(1)}, u32[]{:S(2)}, u32[]{:S(2)}) collective-permute-start(f32[9,24,128]{2,1,0:T(8,128)S(1)} %get-tuple-element.28), channel_id=1, source_target_pairs={{0,16},{16,32},{32,48},{48,64},{64,80},{80,96},{96,112},{112,128},... | collective-permute-start | bytes 331784 | tf_op jit(solution)/shard_map/ppermute | solution.py:282
  132.6 8.2 %collective-permute-start.13 = (f32[9,24,128]{2,1,0:T(8,128)S(1)}, f32[9,24,128]{2,1,0:T(8,128)S(1)}, u32[]{:S(2)}, u32[]{:S(2)}) collective-permute-start(f32[9,24,128]{2,1,0:T(8,128)S(1)} %get-tuple-element.29), channel_id=1, source_target_pairs={{16,0},{32,16},{48,32},{64,48},{80,64},{96,80},{112,96},{128,112},... | collective-permute-start | bytes 331784 | tf_op jit(solution)/shard_map/ppermute | solution.py:285
  144.8 6.0 %collective-permute-start.14 = (f32[24,8,128]{2,1,0:T(8,128)S(1)}, f32[24,8,128]{2,1,0:T(8,128)S(1)}, u32[]{:S(2)}, u32[]{:S(2)}) collective-permute-start(f32[24,8,128]{2,1,0:T(8,128)S(1)} %multiply_multiply_fusion), channel_id=1, source_target_pairs={{0,1},{1,2},{2,3},{3,4},{4,5},{5,6},{6,7},{7,8},{8,9},{9,10},{10,1... | collective-permute-start | bytes 294920 | tf_op jit(solution)/shard_map/ppermute | solution.py:183
  148.8 10.7 %collective-permute-start.15 = (f32[24,8,128]{2,1,0:T(8,128)S(1)}, f32[24,8,128]{2,1,0:T(8,128)S(1)}, u32[]{:S(2)}, u32[]{:S(2)}) collective-permute-start(f32[24,8,128]{2,1,0:T(8,128)S(1)} %multiply_multiply_fusion), channel_id=1, source_target_pairs={{1,0},{2,1},{3,2},{4,3},{5,4},{6,5},{7,6},{8,7},{9,8},{10,9},{11,1... | collective-permute-start | bytes 294920 | tf_op jit(solution)/shard_map/ppermute | solution.py:184
  165.1 4.3 %collective-permute-start.16 = (f32[24,8,128]{2,1,0:T(8,128)}, f32[24,8,128]{2,1,0:T(8,128)S(1)}, u32[]{:S(2)}, u32[]{:S(2)}) collective-permute-start(f32[24,8,128]{2,1,0:T(8,128)} %shard_map.68), channel_id=1, source_target_pairs={{0,1},{1,2},{2,3},{3,4},{4,5},{5,6},{6,7},{7,8},{8,9},{9,10},{10,1... | collective-permute-start | bytes 294920 | tf_op jit(solution)/shard_map/ppermute | solution.py:183
  167.0 11.0 %collective-permute-start.17 = (f32[24,8,128]{2,1,0:T(8,128)}, f32[24,8,128]{2,1,0:T(8,128)S(1)}, u32[]{:S(2)}, u32[]{:S(2)}) collective-permute-start(f32[24,8,128]{2,1,0:T(8,128)} %shard_map.68), channel_id=1, source_target_pairs={{1,0},{2,1},{3,2},{4,3},{5,4},{6,5},{7,6},{8,7},{9,8},{10,9},{11,1... | collective-permute-start | bytes 294920 | tf_op jit(solution)/shard_map/ppermute | solution.py:184
  184.4 4.3 %collective-permute-start.18 = (f32[24,8,128]{2,1,0:T(8,128)}, f32[24,8,128]{2,1,0:T(8,128)S(1)}, u32[]{:S(2)}, u32[]{:S(2)}) collective-permute-start(f32[24,8,128]{2,1,0:T(8,128)} %shard_map.69), channel_id=1, source_target_pairs={{0,1},{1,2},{2,3},{3,4},{4,5},{5,6},{6,7},{7,8},{8,9},{9,10},{10,1... | collective-permute-start | bytes 294920 | tf_op jit(solution)/shard_map/ppermute | solution.py:183
  186.4 11.0 %collective-permute-start.19 = (f32[24,8,128]{2,1,0:T(8,128)}, f32[24,8,128]{2,1,0:T(8,128)S(1)}, u32[]{:S(2)}, u32[]{:S(2)}) collective-permute-start(f32[24,8,128]{2,1,0:T(8,128)} %shard_map.69), channel_id=1, source_target_pairs={{1,0},{2,1},{3,2},{4,3},{5,4},{6,5},{7,6},{8,7},{9,8},{10,9},{11,1... | collective-permute-start | bytes 294920 | tf_op jit(solution)/shard_map/ppermute | solution.py:184
  203.7 4.3 %collective-permute-start.20 = (f32[24,8,128]{2,1,0:T(8,128)}, f32[24,8,128]{2,1,0:T(8,128)S(1)}, u32[]{:S(2)}, u32[]{:S(2)}) collective-permute-start(f32[24,8,128]{2,1,0:T(8,128)} %shard_map.70), channel_id=1, source_target_pairs={{0,1},{1,2},{2,3},{3,4},{4,5},{5,6},{6,7},{7,8},{8,9},{9,10},{10,1... | collective-permute-start | bytes 294920 | tf_op jit(solution)/shard_map/ppermute | solution.py:183
  205.7 11.0 %collective-permute-start.21 = (f32[24,8,128]{2,1,0:T(8,128)}, f32[24,8,128]{2,1,0:T(8,128)S(1)}, u32[]{:S(2)}, u32[]{:S(2)}) collective-permute-start(f32[24,8,128]{2,1,0:T(8,128)} %shard_map.70), channel_id=1, source_target_pairs={{1,0},{2,1},{3,2},{4,3},{5,4},{6,5},{7,6},{8,7},{9,8},{10,9},{11,1... | collective-permute-start | bytes 294920 | tf_op jit(solution)/shard_map/ppermute | solution.py:184
  224.0 5.3 %collective-permute-start.22 = (f32[4,8,128]{2,1,0:T(8,128)S(1)}, f32[4,8,128]{2,1,0:T(8,128)S(1)}, u32[]{:S(2)}, u32[]{:S(2)}) collective-permute-start(f32[4,8,128]{2,1,0:T(8,128)S(1)} %get-tuple-element.26), channel_id=1, source_target_pairs={{0,16},{16,32},{32,48},{48,64},{64,80},{80,96},{96,112},{112,128},... | collective-permute-start | bytes 49160 | tf_op jit(solution)/shard_map/ppermute | solution.py:297
  225.9 7.2 %collective-permute-start.23 = (f32[4,8,128]{2,1,0:T(8,128)S(1)}, f32[4,8,128]{2,1,0:T(8,128)S(1)}, u32[]{:S(2)}, u32[]{:S(2)}) collective-permute-start(f32[4,8,128]{2,1,0:T(8,128)S(1)} %get-tuple-element.27), channel_id=1, source_target_pairs={{16,0},{32,16},{48,32},{64,48},{80,64},{96,80},{112,96},{128,112},... | collective-permute-start | bytes 49160 | tf_op jit(solution)/shard_map/ppermute | solution.py:300
  (14 other events, 33.4 us)
where the time goes:
time: 236 us; the launch traced here: 234 us
  waiting for transfers between devices  89.2 us (38%)
  starting transfers between devices  64.8 us (27%)
  Pallas kernels  38.1 us (16%)
  other arithmetic  29.4 us (12%)
  local copies, waits for them, and re-layouts  9.38 us (4%)
  between operations  2.85 us (1%)
    ppermute x9, waiting for transfers between devices, with_sides(): from_right = lax.ppermute(value, axis, grp_pairs(axis, -1))  71.5 us
    pallas_call x8, Pallas kernels, round_call(): pl.pallas_call(make_round_kernel(weight_now, weight_next, last, own_cols)...  38.1 us
    ppermute x9, starting transfers between devices, with_sides(): from_left = lax.ppermute(value, axis, grp_pairs(axis, 1))  25 us
    ppermute x9, starting transfers between devices, with_sides(): from_right = lax.ppermute(value, axis, grp_pairs(axis, -1))  21.1 us
    concatenate x9, other arithmetic, with_sides(): return jnp.concatenate([from_left, value, from_right], axis=dim)  11.4 us
    ppermute x1, waiting for transfers between devices, on_device(): from_above = lax.ppermute(correction[:span], 'sub', grp_pairs('sub', -1))  6.25 us
    another operation x1, other arithmetic, on_device(): stacked = jnp.stack([perm_local, pressure_start, source])  5.96 us
    ppermute x1, starting transfers between devices, on_device(): lax.ppermute(correction[margin_rows - span:], 'sub', grp_pairs('sub', 1))  5.08 us
  transfers between devices with their start and end apart: 24, of which 14 were waited for; matrix products, arithmetic and copies ran while one was open for 3% of the time, Pallas kernels for 0%

commit v1 on v0

--- a/solution.py
+++ b/solution.py
@@ -99,11 +99,27 @@
 
 def make_round_kernel(weight_now, weight_next, last, own_cols):
     def kernel(
-        e_ref, t_ref, d_ref, fb_ref, fa_ref, fl_ref, fr_ref, ff_ref, fk_ref, act_ref,
-        ym_ref, yi_ref, yu_ref, zm_ref, zi_ref, zu_ref, xm_ref, xi_ref, xu_ref,
-        o_ref, s_ref, f_ref,
+        depth_ref, left_ref, own_ref, right_ref, t_ref, d_ref, fb_ref, fa_ref, fl_ref, fr_ref,
+        ff_ref, fk_ref, ym_ref, yi_ref, zm_ref, zi_ref, xm_ref, xi_ref,
+        o_ref, s_ref, f_ref, zu_ref,
     ):
-        rows, cols, lanes = e_ref.shape
+        rows, cols, lanes = t_ref.shape
+        shape = (rows, cols, lanes)
+        offsets = lax.broadcasted_iota(jnp.int32, shape, 0) - OV
+        slab_rows = rows - 2 * OV
+        depth_low = depth_ref[0]
+        depth_high = depth_ref[1]
+        act = jnp.where(
+            (offsets >= -depth_low) & (offsets < slab_rows + depth_high), 1.0, 0.0
+        )
+        act_high = jnp.where(
+            (offsets + 1 >= -depth_low) & (offsets + 1 < slab_rows + depth_high) & (offsets + 1 < rows - OV),
+            1.0,
+            0.0,
+        )
+        lane_end = lax.broadcasted_iota(jnp.int32, shape, 2) % BL != BL - 1
+        row_end = (offsets + OV) % BL != BL - 1
+        zu_ref[...] = jnp.where(row_end, -fa_ref[...] * act * act_high, 0.0)
 
         def row_lower(x):
             return jnp.concatenate([jnp.zeros_like(x[:1]), x[:-1]], axis=0)
@@ -131,11 +147,11 @@
                 result = (forward - u * pltpu.roll(result, extent - 1, axis)) * inv
             return result
 
-        act = act_ref[...]
         target = t_ref[...]
-        e = e_ref[...]
+        e = jnp.concatenate([left_ref[...], own_ref[...], right_ref[...]], axis=1)
+        upper_y = jnp.where(lane_end, -fk_ref[...] * act * act, 0.0)
         update = act * (target - operate(e))
-        e = e + weight_now * roll_solve(update, ym_ref[...], yi_ref[...], yu_ref[...], 2, lanes)
+        e = e + weight_now * roll_solve(update, ym_ref[...], yi_ref[...], upper_y, 2, lanes)
         s_ref[...] = act * (target - operate(e))
         for block in range(rows // BL):
             base = block * BL
@@ -156,22 +172,29 @@
             o_ref[...] = e
         else:
             update = (act * (target - operate(e)))[:, own_cols]
+            own_act = act[:, own_cols]
+            col_end = lax.broadcasted_iota(jnp.int32, update.shape, 1) % BL != BL - 1
+            upper_x = jnp.where(col_end, -fr_ref[:, own_cols] * own_act * own_act, 0.0)
             o_ref[...] = e[:, own_cols] + weight_next * roll_solve(
-                update, xm_ref[...], xi_ref[...], xu_ref[...], 1, BL
+                update, xm_ref[...], xi_ref[...], upper_x, 1, BL
             )
 
     return kernel
 
 
-def round_call(weight_now, weight_next, last, tile_cols, estimate, target, coeffs, active, fy, fz, fx):
+def round_call(weight_now, weight_next, last, depths, pieces, target, coeffs, fy, fz, fx):
+    tile_cols = pieces[1].shape[1]
     own_cols = slice(tile_cols, 2 * tile_cols)
-    shape = estimate.shape
-    out_shape = shape if last else (shape[0], tile_cols, shape[2])
+    shape = target.shape
+    out_shape = shape if last else pieces[1].shape
+    vmem = pl.BlockSpec(memory_space=pltpu.VMEM)
     return pl.pallas_call(
         make_round_kernel(weight_now, weight_next, last, own_cols),
         out_shape=jax.ShapeDtypeStruct(out_shape, jnp.float32),
-        scratch_shapes=[pltpu.VMEM(shape, jnp.float32), pltpu.VMEM(shape, jnp.float32)],
-    )(estimate, target, *coeffs, active, *fy[:3], *fz[:3], *fx[:3])
+        in_specs=[pl.BlockSpec(memory_space=pltpu.SMEM)] + [vmem] * 17,
+        out_specs=vmem,
+        scratch_shapes=[pltpu.VMEM(shape, jnp.float32)] * 3,
+    )(depths, *pieces, target, *coeffs, *fy[:2], *fz[:2], *fx[:2])
 
 
 def grp_pairs(axis, by):
@@ -192,6 +215,47 @@
     )
     above = lax.ppermute(lax.slice_in_dim(value, 0, width, axis=dim), axis, grp_pairs(axis, -1))
     return jnp.concatenate([below, value, above], axis=dim)
+
+
+def with_halo(value, width):
+    subs, grps = lax.axis_size("sub"), lax.axis_size("grp")
+    top = value[:, -width:]
+    bottom = value[:, :width]
+
+    def diagonal(part, dsub, dgrp):
+        pairs = [
+            (s * grps + g, (s + dsub) * grps + g + dgrp)
+            for s in range(subs)
+            for g in range(grps)
+            if 0 <= s + dsub < subs and 0 <= g + dgrp < grps
+        ]
+        return lax.ppermute(part, ("sub", "grp"), pairs)
+
+    middle = jnp.concatenate(
+        [
+            lax.ppermute(top, "sub", grp_pairs("sub", 1)),
+            value,
+            lax.ppermute(bottom, "sub", grp_pairs("sub", -1)),
+        ],
+        axis=1,
+    )
+    left = jnp.concatenate(
+        [
+            diagonal(top, 1, 1),
+            lax.ppermute(value, "grp", grp_pairs("grp", 1)),
+            diagonal(bottom, -1, 1),
+        ],
+        axis=1,
+    )
+    right = jnp.concatenate(
+        [
+            diagonal(top, 1, -1),
+            lax.ppermute(value, "grp", grp_pairs("grp", -1)),
+            diagonal(bottom, -1, -1),
+        ],
+        axis=1,
+    )
+    return jnp.concatenate([left, middle, right], axis=2)
 
 
 def on_device(facies, facies_perm, perm_scale, source, pressure_start, intersection_depth):
@@ -203,8 +267,7 @@
     perm_local = perm_local * perm_scale
 
     stacked = jnp.stack([perm_local, pressure_start, source])
-    stacked = with_rows(stacked, "sub", 1, OV + 1)
-    stacked = with_sides(stacked, "grp", 2)
+    stacked = with_halo(stacked, OV + 1)
     perm_wide = stacked[0]
     pressure_wide = stacked[1]
     source_wide = stacked[2][1:-1]
@@ -232,6 +295,7 @@
     )
     depth_low = bounds[slab_index]
     depth_high = bounds[slab_index + 1]
+    depths = jnp.stack([depth_low, depth_high])
     offsets = jnp.arange(margin_rows, dtype=jnp.int32) - OV
     inside_slab = (offsets >= -depth_low) & (offsets < slab_rows + depth_high)
     band_rows = (offsets < depth_low) | (offsets >= slab_rows - depth_high)
@@ -260,17 +324,20 @@
         target = residual * active
         estimate_own = relax_weight(0) * solve_lines(factors_x, target[:, own])
         for round_index in range(ROUNDS):
-            estimate = with_sides(estimate_own, "grp", 1)
+            pieces = (
+                lax.ppermute(estimate_own, "grp", grp_pairs("grp", 1)),
+                estimate_own,
+                lax.ppermute(estimate_own, "grp", grp_pairs("grp", -1)),
+            )
             last = round_index + 1 == ROUNDS
             estimate = round_call(
                 relax_weight(round_index),
                 0.0 if last else relax_weight(round_index + 1),
                 last,
-                tile_cols,
-                estimate,
+                depths,
+                pieces,
                 target,
                 coeffs,
-                full_active,
                 factors_y,
                 factors_z,
                 factors_x,

time: 236 us -> 236 us (level)
  starting transfers between devices: 64.8 us -> 83.6 us
  waiting for transfers between devices: 89.2 us -> 77.7 us
  other arithmetic: 29.4 us -> 21.4 us
  local copies, waits for them, and re-layouts: 9.38 us -> 11.8 us
    ppermute x20 -> x24, starting transfers between devices: 52.6 us -> 72 us  [the longest x8 23.8 us: on_device(): lax.ppermute(estimate_own, 'grp', grp_pairs('grp', 1))]
    ppermute x20 -> x24, waiting for transfers between devices: 79.1 us -> 67.4 us  [the longest x8 61.8 us: on_device(): lax.ppermute(estimate_own, 'grp', grp_pairs('grp', -1))]
    concatenate x10 -> x1, other arithmetic: 11.4 us -> 0.07 us  [with_halo(): return jnp.concatenate([left, middle, right], axis=2)]
    unnamed x28 -> x58, local copies, waits for them, and re-layouts: 4 us -> 8.21 us
    another operation x1 -> x2, other arithmetic: 5.96 us -> 6.06 us  [on_device(): stacked = jnp.stack([perm_local, pressure_start, source])]
  transfers between devices with their start and end apart: 24 -> 28, of which waited for: 14 -> 12; matrix products, arithmetic and copies ran while one was open for 3% -> 4% of each run, Pallas kernels for 0% -> 0%
where the time goes in v1:
time: 236 us; the launch traced here: 234 us
  starting transfers between devices  83.6 us (35%)
  waiting for transfers between devices  77.7 us (33%)
  Pallas kernels  36.1 us (15%)
  other arithmetic  21.4 us (9%)
  local copies, waits for them, and re-layouts  11.8 us (5%)
  between operations  3.11 us (1%)
    ppermute x8, waiting for transfers between devices, on_device(): lax.ppermute(estimate_own, 'grp', grp_pairs('grp', -1))  61.8 us
    pallas_call x8, Pallas kernels, round_call(): pl.pallas_call(make_round_kernel(weight_now, weight_next, last, own_cols)...  36.1 us
    ppermute x8, starting transfers between devices, on_device(): lax.ppermute(estimate_own, 'grp', grp_pairs('grp', 1))  23.8 us
    ppermute x8, starting transfers between devices, on_device(): lax.ppermute(estimate_own, 'grp', grp_pairs('grp', -1))  17.9 us
    ppermute x4, starting transfers between devices, diagonal(): return lax.ppermute(part, ('sub', 'grp'), pairs)  17.3 us
    unnamed x58, local copies, waits for them, and re-layouts  8.21 us
    ppermute x1, waiting for transfers between devices, on_device(): from_above = lax.ppermute(correction[:span], 'sub', grp_pairs('sub', -1))  6.25 us
    another operation x2, other arithmetic, on_device(): stacked = jnp.stack([perm_local, pressure_start, source])  6.06 us
  transfers between devices with their start and end apart: 28, of which 12 were waited for; matrix products, arithmetic and copies ran while one was open for 4% of the time, Pallas kernels for 0%

profile of v1, /device:TPU:225, one launch (start us, length us, event | category | flops | bytes accessed | tf_op | source)
XLA Modules:
  0.0 233.8 jit_solution(567055507748668144)
XLA Ops:
  1.6 6.0 %multiply_bitcast_fusion = f32[1,16,8,128]{3,2,1,0:T(8,128)S(1)} fusion(f32[16,8,128]{2,1,0:T(8,128)} %param.8, s32[16,8,128]{2,1,0:T(8,128)} %param.6, f32[]{:T(128)} %bitcast.7, f32[]{:T(128)} %bitcast.6, f32[]{:T(128)} %bitcast.5, f32[]{:T(128)} %bitcast.4, f32[]{:T(128)} %bitcast.3, f32[]{:T(128)} %bitcast.2, f32[]{:T(128)} %bitcast.1, f32[]{:T(128)} %bitcast), kind=kLoop, calls=%fused_computation.199 | loop fusion | flops 393216 | bytes 196640 | tf_op jit(solution)/shard_map/stack | solution.py:269
  9.7 4.9 %collective-permute-start.3 = (f32[3,5,8,128]{3,2,1,0:T(8,128)S(1)}, f32[3,5,8,128]{3,2,1,0:T(8,128)S(1)}, u32[]{:S(2)}, u32[]{:S(2)}) collective-permute-start(f32[3,5,8,128]{3,2,1,0:T(8,128)S(1)} %get-tuple-element.40), channel_id=1, source_target_pairs={{0,16},{16,32},{32,48},{48,64},{64,80},{80,96},{96,112},{112,128},... | collective-permute-start | bytes 184328 | tf_op jit(solution)/shard_map/ppermute | solution.py:236
  19.6 7.5 %collective-permute-start.2 = (f32[3,5,8,128]{3,2,1,0:T(8,128)S(1)}, f32[3,5,8,128]{3,2,1,0:T(8,128)S(1)}, u32[]{:S(2)}, u32[]{:S(2)}) collective-permute-start(f32[3,5,8,128]{3,2,1,0:T(8,128)S(1)} %get-tuple-element.41), channel_id=1, source_target_pairs={{16,1},{17,2},{18,3},{19,4},{20,5},{21,6},{22,7},{23,8},{24,9},{25... | collective-permute-start | bytes 184328 | tf_op jit(solution)/shard_map/ppermute | solution.py:232
  35.2 5.0 %collective-permute-start.5 = (f32[3,5,8,128]{3,2,1,0:T(8,128)S(1)}, f32[3,5,8,128]{3,2,1,0:T(8,128)S(1)}, u32[]{:S(2)}, u32[]{:S(2)}) collective-permute-start(f32[3,5,8,128]{3,2,1,0:T(8,128)S(1)} %get-tuple-element.40), channel_id=1, source_target_pairs={{1,16},{2,17},{3,18},{4,19},{5,20},{6,21},{7,22},{8,23},{9,24},{10... | collective-permute-start | bytes 184328 | tf_op jit(solution)/shard_map/ppermute | solution.py:232
  53.7 5.1 %collective-permute-start.8 = (f32[24,8,128]{2,1,0:T(8,128)S(1)}, f32[24,8,128]{2,1,0:T(8,128)S(1)}, u32[]{:S(2)}, u32[]{:S(2)}) collective-permute-start(f32[24,8,128]{2,1,0:T(8,128)S(1)} %multiply_multiply_fusion.1.own_ref), channel_id=1, source_target_pairs={{0,1},{1,2},{2,3},{3,4},{4,5},{5,6},{6,7},{7,8},{8,9},{9,10},{10,1... | collective-permute-start | bytes 294920 | tf_op jit(solution)/shard_map/ppermute | solution.py:328
  70.2 4.6 %shard_map.64.own_ref = f32[24,8,128]{2,1,0:T(8,128)} custom-call(s32[2]{0:T(128)} %pad_add_fusion.1.depth_ref, f32[24,8,128]{2,1,0:T(8,128)} %copy-done.12, f32[24,8,128]{2,1,0:T(8,128)} %copy-done.8, f32[24,8,128]{2,1,0:T(8,128)} %copy-done.13, f32[24,24,128]{2,1,0:T(8,128)} %copy-done.6, f32[24,24,128]{2,1,0:T(8,128)} %copy-done.5, ...), custom_call_target="tpu_custom_call" | custom-call | tf_op jit(solution)/shard_map/pallas_call | solution.py:191
  74.7 5.6 %collective-permute-start.10 = (f32[24,8,128]{2,1,0:T(8,128)}, f32[24,8,128]{2,1,0:T(8,128)S(1)}, u32[]{:S(2)}, u32[]{:S(2)}) collective-permute-start(f32[24,8,128]{2,1,0:T(8,128)} %shard_map.64.own_ref), channel_id=1, source_target_pairs={{0,1},{1,2},{2,3},{3,4},{4,5},{5,6},{6,7},{7,8},{8,9},{9,10},{10,1... | collective-permute-start | bytes 294920 | tf_op jit(solution)/shard_map/ppermute | solution.py:328
  82.3 9.0 %collective-permute-done.11.right_ref = f32[24,8,128]{2,1,0:T(8,128)S(1)} collective-permute-done((f32[24,8,128]{2,1,0:T(8,128)}, f32[24,8,128]{2,1,0:T(8,128)S(1)}, u32[]{:S(2)}, u32[]{:S(2)}) %collective-permute-start.11) | collective-permute-done | bytes 98336 | tf_op jit(solution)/shard_map/ppermute | solution.py:330
  91.9 4.6 %shard_map.65.own_ref = f32[24,8,128]{2,1,0:T(8,128)} custom-call(s32[2]{0:T(128)} %pad_add_fusion.1.depth_ref, f32[24,8,128]{2,1,0:T(8,128)} %copy-done.19, f32[24,8,128]{2,1,0:T(8,128)} %shard_map.64.own_ref, f32[24,8,128]{2,1,0:T(8,128)} %copy-done.24, f32[24,24,128]{2,1,0:T(8,128)} %copy-done.6, f32[24,24,128]{2,1,0:T(8,128)} %copy-done.5, ...), custom_call_target="tpu_custom_call" | custom-call | tf_op jit(solution)/shard_map/pallas_call | solution.py:191
  101.7 7.7 %collective-permute-done.13.right_ref = f32[24,8,128]{2,1,0:T(8,128)S(1)} collective-permute-done((f32[24,8,128]{2,1,0:T(8,128)}, f32[24,8,128]{2,1,0:T(8,128)S(1)}, u32[]{:S(2)}, u32[]{:S(2)}) %collective-permute-start.13) | collective-permute-done | bytes 98336 | tf_op jit(solution)/shard_map/ppermute | solution.py:330
  110.0 4.6 %shard_map.66.own_ref = f32[24,8,128]{2,1,0:T(8,128)} custom-call(s32[2]{0:T(128)} %pad_add_fusion.1.depth_ref, f32[24,8,128]{2,1,0:T(8,128)} %copy-done.17, f32[24,8,128]{2,1,0:T(8,128)} %shard_map.65.own_ref, f32[24,8,128]{2,1,0:T(8,128)} %copy-done.20, f32[24,24,128]{2,1,0:T(8,128)} %copy-done.6, f32[24,24,128]{2,1,0:T(8,128)} %copy-done.5, ...), custom_call_target="tpu_custom_call" | custom-call | tf_op jit(solution)/shard_map/pallas_call | solution.py:191
  119.5 7.9 %collective-permute-done.15.right_ref = f32[24,8,128]{2,1,0:T(8,128)S(1)} collective-permute-done((f32[24,8,128]{2,1,0:T(8,128)}, f32[24,8,128]{2,1,0:T(8,128)S(1)}, u32[]{:S(2)}, u32[]{:S(2)}) %collective-permute-start.15) | collective-permute-done | bytes 98336 | tf_op jit(solution)/shard_map/ppermute | solution.py:330
  128.1 4.4 %shard_map.67 = f32[24,24,128]{2,1,0:T(8,128)} custom-call(s32[2]{0:T(128)} %pad_add_fusion.1.depth_ref, f32[24,8,128]{2,1,0:T(8,128)} %copy-done.16, f32[24,8,128]{2,1,0:T(8,128)} %shard_map.66.own_ref, f32[24,8,128]{2,1,0:T(8,128)} %copy-done.18, f32[24,24,128]{2,1,0:T(8,128)} %copy-done.6, f32[24,24,128]{2,1,0:T(8,128)} %copy-done.5, ...), custom_call_target="tpu_custom_call" | custom-call | tf_op jit(solution)/shard_map/pallas_call | solution.py:191
  133.5 4.4 %collective-permute-start.16 = (f32[9,24,128]{2,1,0:T(8,128)S(1)}, f32[9,24,128]{2,1,0:T(8,128)S(1)}, u32[]{:S(2)}, u32[]{:S(2)}) collective-permute-start(f32[9,24,128]{2,1,0:T(8,128)S(1)} %get-tuple-element.27), channel_id=1, source_target_pairs={{0,16},{16,32},{32,48},{48,64},{64,80},{80,96},{96,112},{112,128},... | collective-permute-start | bytes 331784 | tf_op jit(solution)/shard_map/ppermute | solution.py:349
  139.8 6.3 %collective-permute-done.17 = f32[9,24,128]{2,1,0:T(8,128)S(1)} collective-permute-done((f32[9,24,128]{2,1,0:T(8,128)S(1)}, f32[9,24,128]{2,1,0:T(8,128)S(1)}, u32[]{:S(2)}, u32[]{:S(2)}) %collective-permute-start.17) | collective-permute-done | bytes 110624 | tf_op jit(solution)/shard_map/ppermute | solution.py:352
  154.7 8.8 %collective-permute-done.19.right_ref = f32[24,8,128]{2,1,0:T(8,128)S(1)} collective-permute-done((f32[24,8,128]{2,1,0:T(8,128)S(1)}, f32[24,8,128]{2,1,0:T(8,128)S(1)}, u32[]{:S(2)}, u32[]{:S(2)}) %collective-permute-start.19) | collective-permute-done | bytes 98336 | tf_op jit(solution)/shard_map/ppermute | solution.py:330
  164.1 4.6 %shard_map.68.own_ref = f32[24,8,128]{2,1,0:T(8,128)} custom-call(s32[2]{0:T(128)} %pad_add_fusion.1.depth_ref, f32[24,8,128]{2,1,0:T(8,128)} %copy-done.21, f32[24,8,128]{2,1,0:T(8,128)} %copy-done.9, f32[24,8,128]{2,1,0:T(8,128)} %copy-done.25, f32[24,24,128]{2,1,0:T(8,128)} %copy-done.7, f32[24,24,128]{2,1,0:T(8,128)} %copy-done.5, ...), custom_call_target="tpu_custom_call" | custom-call | tf_op jit(solution)/shard_map/pallas_call | solution.py:191
  173.0 8.5 %collective-permute-done.21.right_ref = f32[24,8,128]{2,1,0:T(8,128)S(1)} collective-permute-done((f32[24,8,128]{2,1,0:T(8,128)}, f32[24,8,128]{2,1,0:T(8,128)S(1)}, u32[]{:S(2)}, u32[]{:S(2)}) %collective-permute-start.21) | collective-permute-done | bytes 98336 | tf_op jit(solution)/shard_map/ppermute | solution.py:330
  182.2 4.6 %shard_map.69.own_ref = f32[24,8,128]{2,1,0:T(8,128)} custom-call(s32[2]{0:T(128)} %pad_add_fusion.1.depth_ref, f32[24,8,128]{2,1,0:T(8,128)} %copy-done.22, f32[24,8,128]{2,1,0:T(8,128)} %shard_map.68.own_ref, f32[24,8,128]{2,1,0:T(8,128)} %copy-done.26, f32[24,24,128]{2,1,0:T(8,128)} %copy-done.7, f32[24,24,128]{2,1,0:T(8,128)} %copy-done.5, ...), custom_call_target="tpu_custom_call" | custom-call | tf_op jit(solution)/shard_map/pallas_call | solution.py:191
  191.1 8.5 %collective-permute-done.23.right_ref = f32[24,8,128]{2,1,0:T(8,128)S(1)} collective-permute-done((f32[24,8,128]{2,1,0:T(8,128)}, f32[24,8,128]{2,1,0:T(8,128)S(1)}, u32[]{:S(2)}, u32[]{:S(2)}) %collective-permute-start.23) | collective-permute-done | bytes 98336 | tf_op jit(solution)/shard_map/ppermute | solution.py:330
  200.3 4.6 %shard_map.70.own_ref = f32[24,8,128]{2,1,0:T(8,128)} custom-call(s32[2]{0:T(128)} %pad_add_fusion.1.depth_ref, f32[24,8,128]{2,1,0:T(8,128)} %copy-done.23, f32[24,8,128]{2,1,0:T(8,128)} %shard_map.69.own_ref, f32[24,8,128]{2,1,0:T(8,128)} %copy-done.27, f32[24,24,128]{2,1,0:T(8,128)} %copy-done.7, f32[24,24,128]{2,1,0:T(8,128)} %copy-done.5, ...), custom_call_target="tpu_custom_call" | custom-call | tf_op jit(solution)/shard_map/pallas_call | solution.py:191
  209.2 8.5 %collective-permute-done.25.right_ref = f32[24,8,128]{2,1,0:T(8,128)S(1)} collective-permute-done((f32[24,8,128]{2,1,0:T(8,128)}, f32[24,8,128]{2,1,0:T(8,128)S(1)}, u32[]{:S(2)}, u32[]{:S(2)}) %collective-permute-start.25) | collective-permute-done | bytes 98336 | tf_op jit(solution)/shard_map/ppermute | solution.py:330
  218.3 4.4 %shard_map.71 = f32[24,24,128]{2,1,0:T(8,128)} custom-call(s32[2]{0:T(128)} %pad_add_fusion.1.depth_ref, f32[24,8,128]{2,1,0:T(8,128)} %copy-done.14, f32[24,8,128]{2,1,0:T(8,128)} %shard_map.70.own_ref, f32[24,8,128]{2,1,0:T(8,128)} %copy-done.15, f32[24,24,128]{2,1,0:T(8,128)} %copy-done.7, f32[24,24,128]{2,1,0:T(8,128)} %copy-done.5, ...), custom_call_target="tpu_custom_call" | custom-call | tf_op jit(solution)/shard_map/pallas_call | solution.py:191
  229.1 4.1 %collective-permute-done.27 = f32[4,8,128]{2,1,0:T(8,128)S(1)} collective-permute-done((f32[4,8,128]{2,1,0:T(8,128)S(1)}, f32[4,8,128]{2,1,0:T(8,128)S(1)}, u32[]{:S(2)}, u32[]{:S(2)}) %collective-permute-start.27) | collective-permute-done | bytes 16416 | tf_op jit(solution)/shard_map/ppermute | solution.py:367
  (198 shorter events, 86.9 us)
Async XLA Ops:
  7.8 24.4 %collective-permute-start = (f32[3,5,8,128]{3,2,1,0:T(8,128)S(1)}, f32[3,5,8,128]{3,2,1,0:T(8,128)S(1)}, u32[]{:S(2)}, u32[]{:S(2)}) collective-permute-start(f32[3,5,8,128]{3,2,1,0:T(8,128)S(1)} %get-tuple-element.40), channel_id=1, source_target_pairs={{0,17},{1,18},{2,19},{3,20},{4,21},{5,22},{6,23},{7,24},{8,25},{9,... | collective-permute-start | bytes 184328 | tf_op jit(solution)/shard_map/ppermute | solution.py:232
  9.7 30.5 %collective-permute-start.3 = (f32[3,5,8,128]{3,2,1,0:T(8,128)S(1)}, f32[3,5,8,128]{3,2,1,0:T(8,128)S(1)}, u32[]{:S(2)}, u32[]{:S(2)}) collective-permute-start(f32[3,5,8,128]{3,2,1,0:T(8,128)S(1)} %get-tuple-element.40), channel_id=1, source_target_pairs={{0,16},{16,32},{32,48},{48,64},{64,80},{80,96},{96,112},{112,128},... | collective-permute-start | bytes 184328 | tf_op jit(solution)/shard_map/ppermute | solution.py:236
  14.6 34.1 %collective-permute-start.1 = (f32[3,16,8,128]{3,2,1,0:T(8,128)S(1)}, f32[3,16,8,128]{3,2,1,0:T(8,128)S(1)}, u32[]{:S(2)}, u32[]{:S(2)}) collective-permute-start(f32[3,16,8,128]{3,2,1,0:T(8,128)S(1)} %pad_maximum_fusion), channel_id=1, source_target_pairs={{0,1},{1,2},{2,3},{3,4},{4,5},{5,6},{6,7},{7,8},{8,9},{9,10},{10,1... | collective-permute-start | bytes 589832 | tf_op jit(solution)/shard_map/ppermute | solution.py:245
  17.7 31.1 %collective-permute-start.6 = (f32[3,16,8,128]{3,2,1,0:T(8,128)S(1)}, f32[3,16,8,128]{3,2,1,0:T(8,128)S(1)}, u32[]{:S(2)}, u32[]{:S(2)}) collective-permute-start(f32[3,16,8,128]{3,2,1,0:T(8,128)S(1)} %pad_maximum_fusion), channel_id=1, source_target_pairs={{1,0},{2,1},{3,2},{4,3},{5,4},{6,5},{7,6},{8,7},{9,8},{10,9},{11,1... | collective-permute-start | bytes 589832 | tf_op jit(solution)/shard_map/ppermute | solution.py:253
  19.6 15.5 %collective-permute-start.2 = (f32[3,5,8,128]{3,2,1,0:T(8,128)S(1)}, f32[3,5,8,128]{3,2,1,0:T(8,128)S(1)}, u32[]{:S(2)}, u32[]{:S(2)}) collective-permute-start(f32[3,5,8,128]{3,2,1,0:T(8,128)S(1)} %get-tuple-element.41), channel_id=1, source_target_pairs={{16,1},{17,2},{18,3},{19,4},{20,5},{21,6},{22,7},{23,8},{24,9},{25... | collective-permute-start | bytes 184328 | tf_op jit(solution)/shard_map/ppermute | solution.py:232
  32.1 11.1 %collective-permute-start.4 = (f32[3,5,8,128]{3,2,1,0:T(8,128)S(1)}, f32[3,5,8,128]{3,2,1,0:T(8,128)S(1)}, u32[]{:S(2)}, u32[]{:S(2)}) collective-permute-start(f32[3,5,8,128]{3,2,1,0:T(8,128)S(1)} %get-tuple-element.41), channel_id=1, source_target_pairs={{16,0},{32,16},{48,32},{64,48},{80,64},{96,80},{112,96},{128,112},... | collective-permute-start | bytes 184328 | tf_op jit(solution)/shard_map/ppermute | solution.py:238
  35.2 10.2 %collective-permute-start.5 = (f32[3,5,8,128]{3,2,1,0:T(8,128)S(1)}, f32[3,5,8,128]{3,2,1,0:T(8,128)S(1)}, u32[]{:S(2)}, u32[]{:S(2)}) collective-permute-start(f32[3,5,8,128]{3,2,1,0:T(8,128)S(1)} %get-tuple-element.40), channel_id=1, source_target_pairs={{1,16},{2,17},{3,18},{4,19},{5,20},{6,21},{7,22},{8,23},{9,24},{10... | collective-permute-start | bytes 184328 | tf_op jit(solution)/shard_map/ppermute | solution.py:232
  40.2 8.5 %collective-permute-start.7 = (f32[3,5,8,128]{3,2,1,0:T(8,128)S(1)}, f32[3,5,8,128]{3,2,1,0:T(8,128)S(1)}, u32[]{:S(2)}, u32[]{:S(2)}) collective-permute-start(f32[3,5,8,128]{3,2,1,0:T(8,128)S(1)} %get-tuple-element.41), channel_id=1, source_target_pairs={{17,0},{18,1},{19,2},{20,3},{21,4},{22,5},{23,6},{24,7},{25,8},{26... | collective-permute-start | bytes 184328 | tf_op jit(solution)/shard_map/ppermute | solution.py:232
  53.7 12.9 %collective-permute-start.8 = (f32[24,8,128]{2,1,0:T(8,128)S(1)}, f32[24,8,128]{2,1,0:T(8,128)S(1)}, u32[]{:S(2)}, u32[]{:S(2)}) collective-permute-start(f32[24,8,128]{2,1,0:T(8,128)S(1)} %multiply_multiply_fusion.1.own_ref), channel_id=1, source_target_pairs={{0,1},{1,2},{2,3},{3,4},{4,5},{5,6},{6,7},{7,8},{8,9},{9,10},{10,1... | collective-permute-start | bytes 294920 | tf_op jit(solution)/shard_map/ppermute | solution.py:328
  58.8 10.7 %collective-permute-start.9 = (f32[24,8,128]{2,1,0:T(8,128)S(1)}, f32[24,8,128]{2,1,0:T(8,128)S(1)}, u32[]{:S(2)}, u32[]{:S(2)}) collective-permute-start(f32[24,8,128]{2,1,0:T(8,128)S(1)} %multiply_multiply_fusion.1.own_ref), channel_id=1, source_target_pairs={{1,0},{2,1},{3,2},{4,3},{5,4},{6,5},{7,6},{8,7},{9,8},{10,9},{11,1... | collective-permute-start | bytes 294920 | tf_op jit(solution)/shard_map/ppermute | solution.py:330
  74.7 7.5 %collective-permute-start.10 = (f32[24,8,128]{2,1,0:T(8,128)}, f32[24,8,128]{2,1,0:T(8,128)S(1)}, u32[]{:S(2)}, u32[]{:S(2)}) collective-permute-start(f32[24,8,128]{2,1,0:T(8,128)} %shard_map.64.own_ref), channel_id=1, source_target_pairs={{0,1},{1,2},{2,3},{3,4},{4,5},{5,6},{6,7},{7,8},{8,9},{9,10},{10,1... | collective-permute-start | bytes 294920 | tf_op jit(solution)/shard_map/ppermute | solution.py:328
  80.3 11.0 %collective-permute-start.11 = (f32[24,8,128]{2,1,0:T(8,128)}, f32[24,8,128]{2,1,0:T(8,128)S(1)}, u32[]{:S(2)}, u32[]{:S(2)}) collective-permute-start(f32[24,8,128]{2,1,0:T(8,128)} %shard_map.64.own_ref), channel_id=1, source_target_pairs={{1,0},{2,1},{3,2},{4,3},{5,4},{6,5},{7,6},{8,7},{9,8},{10,9},{11,1... | collective-permute-start | bytes 294920 | tf_op jit(solution)/shard_map/ppermute | solution.py:330
  96.5 5.2 %collective-permute-start.12 = (f32[24,8,128]{2,1,0:T(8,128)}, f32[24,8,128]{2,1,0:T(8,128)S(1)}, u32[]{:S(2)}, u32[]{:S(2)}) collective-permute-start(f32[24,8,128]{2,1,0:T(8,128)} %shard_map.65.own_ref), channel_id=1, source_target_pairs={{0,1},{1,2},{2,3},{3,4},{4,5},{5,6},{6,7},{7,8},{8,9},{9,10},{10,1... | collective-permute-start | bytes 294920 | tf_op jit(solution)/shard_map/ppermute | solution.py:328
  98.4 11.0 %collective-permute-start.13 = (f32[24,8,128]{2,1,0:T(8,128)}, f32[24,8,128]{2,1,0:T(8,128)S(1)}, u32[]{:S(2)}, u32[]{:S(2)}) collective-permute-start(f32[24,8,128]{2,1,0:T(8,128)} %shard_map.65.own_ref), channel_id=1, source_target_pairs={{1,0},{2,1},{3,2},{4,3},{5,4},{6,5},{7,6},{8,7},{9,8},{10,9},{11,1... | collective-permute-start | bytes 294920 | tf_op jit(solution)/shard_map/ppermute | solution.py:330
  116.5 11.0 %collective-permute-start.15 = (f32[24,8,128]{2,1,0:T(8,128)}, f32[24,8,128]{2,1,0:T(8,128)S(1)}, u32[]{:S(2)}, u32[]{:S(2)}) collective-permute-start(f32[24,8,128]{2,1,0:T(8,128)} %shard_map.66.own_ref), channel_id=1, source_target_pairs={{1,0},{2,1},{3,2},{4,3},{5,4},{6,5},{7,6},{8,7},{9,8},{10,9},{11,1... | collective-permute-start | bytes 294920 | tf_op jit(solution)/shard_map/ppermute | solution.py:330
  133.5 6.3 %collective-permute-start.16 = (f32[9,24,128]{2,1,0:T(8,128)S(1)}, f32[9,24,128]{2,1,0:T(8,128)S(1)}, u32[]{:S(2)}, u32[]{:S(2)}) collective-permute-start(f32[9,24,128]{2,1,0:T(8,128)S(1)} %get-tuple-element.27), channel_id=1, source_target_pairs={{0,16},{16,32},{32,48},{48,64},{64,80},{80,96},{96,112},{112,128},... | collective-permute-start | bytes 331784 | tf_op jit(solution)/shard_map/ppermute | solution.py:349
  137.9 8.2 %collective-permute-start.17 = (f32[9,24,128]{2,1,0:T(8,128)S(1)}, f32[9,24,128]{2,1,0:T(8,128)S(1)}, u32[]{:S(2)}, u32[]{:S(2)}) collective-permute-start(f32[9,24,128]{2,1,0:T(8,128)S(1)} %get-tuple-element.28), channel_id=1, source_target_pairs={{16,0},{32,16},{48,32},{64,48},{80,64},{96,80},{112,96},{128,112},... | collective-permute-start | bytes 331784 | tf_op jit(solution)/shard_map/ppermute | solution.py:352
  149.2 5.5 %collective-permute-start.18 = (f32[24,8,128]{2,1,0:T(8,128)S(1)}, f32[24,8,128]{2,1,0:T(8,128)S(1)}, u32[]{:S(2)}, u32[]{:S(2)}) collective-permute-start(f32[24,8,128]{2,1,0:T(8,128)S(1)} %multiply_multiply_fusion.own_ref), channel_id=1, source_target_pairs={{0,1},{1,2},{2,3},{3,4},{4,5},{5,6},{6,7},{7,8},{8,9},{9,10},{10,1... | collective-permute-start | bytes 294920 | tf_op jit(solution)/shard_map/ppermute | solution.py:328
  152.7 10.7 %collective-permute-start.19 = (f32[24,8,128]{2,1,0:T(8,128)S(1)}, f32[24,8,128]{2,1,0:T(8,128)S(1)}, u32[]{:S(2)}, u32[]{:S(2)}) collective-permute-start(f32[24,8,128]{2,1,0:T(8,128)S(1)} %multiply_multiply_fusion.own_ref), channel_id=1, source_target_pairs={{1,0},{2,1},{3,2},{4,3},{5,4},{6,5},{7,6},{8,7},{9,8},{10,9},{11,1... | collective-permute-start | bytes 294920 | tf_op jit(solution)/shard_map/ppermute | solution.py:330
  170.6 11.0 %collective-permute-start.21 = (f32[24,8,128]{2,1,0:T(8,128)}, f32[24,8,128]{2,1,0:T(8,128)S(1)}, u32[]{:S(2)}, u32[]{:S(2)}) collective-permute-start(f32[24,8,128]{2,1,0:T(8,128)} %shard_map.68.own_ref), channel_id=1, source_target_pairs={{1,0},{2,1},{3,2},{4,3},{5,4},{6,5},{7,6},{8,7},{9,8},{10,9},{11,1... | collective-permute-start | bytes 294920 | tf_op jit(solution)/shard_map/ppermute | solution.py:330
  188.7 11.0 %collective-permute-start.23 = (f32[24,8,128]{2,1,0:T(8,128)}, f32[24,8,128]{2,1,0:T(8,128)S(1)}, u32[]{:S(2)}, u32[]{:S(2)}) collective-permute-start(f32[24,8,128]{2,1,0:T(8,128)} %shard_map.69.own_ref), channel_id=1, source_target_pairs={{1,0},{2,1},{3,2},{4,3},{5,4},{6,5},{7,6},{8,7},{9,8},{10,9},{11,1... | collective-permute-start | bytes 294920 | tf_op jit(solution)/shard_map/ppermute | solution.py:330
  206.7 11.0 %collective-permute-start.25 = (f32[24,8,128]{2,1,0:T(8,128)}, f32[24,8,128]{2,1,0:T(8,128)S(1)}, u32[]{:S(2)}, u32[]{:S(2)}) collective-permute-start(f32[24,8,128]{2,1,0:T(8,128)} %shard_map.70.own_ref), channel_id=1, source_target_pairs={{1,0},{2,1},{3,2},{4,3},{5,4},{6,5},{7,6},{8,7},{9,8},{10,9},{11,1... | collective-permute-start | bytes 294920 | tf_op jit(solution)/shard_map/ppermute | solution.py:330
  223.8 5.3 %collective-permute-start.26 = (f32[4,8,128]{2,1,0:T(8,128)S(1)}, f32[4,8,128]{2,1,0:T(8,128)S(1)}, u32[]{:S(2)}, u32[]{:S(2)}) collective-permute-start(f32[4,8,128]{2,1,0:T(8,128)S(1)} %get-tuple-element.25), channel_id=1, source_target_pairs={{0,16},{16,32},{32,48},{48,64},{64,80},{80,96},{96,112},{112,128},... | collective-permute-start | bytes 49160 | tf_op jit(solution)/shard_map/ppermute | solution.py:364
  226.0 7.2 %collective-permute-start.27 = (f32[4,8,128]{2,1,0:T(8,128)S(1)}, f32[4,8,128]{2,1,0:T(8,128)S(1)}, u32[]{:S(2)}, u32[]{:S(2)}) collective-permute-start(f32[4,8,128]{2,1,0:T(8,128)S(1)} %get-tuple-element.26), channel_id=1, source_target_pairs={{16,0},{32,16},{48,32},{64,48},{80,64},{96,80},{112,96},{128,112},... | collective-permute-start | bytes 49160 | tf_op jit(solution)/shard_map/ppermute | solution.py:367
  (33 other events, 138.5 us)

commit v2 on v1

--- a/solution.py
+++ b/solution.py
@@ -267,7 +267,8 @@
     perm_local = perm_local * perm_scale
 
     stacked = jnp.stack([perm_local, pressure_start, source])
-    stacked = with_halo(stacked, OV + 1)
+    stacked = with_rows(stacked, "sub", 1, OV + 1)
+    stacked = with_sides(stacked, "grp", 2)
     perm_wide = stacked[0]
     pressure_wide = stacked[1]
     source_wide = stacked[2][1:-1]

time: 236 us -> 228 us (0.966)
  starting transfers between devices: 83.6 us -> 64.9 us
  waiting for transfers between devices: 77.7 us -> 89.7 us
    ppermute x8 -> x4, starting transfers between devices: 30.3 us -> 12.4 us  [the longest x1 4.54 us: with_rows(): lax.ppermute(lax.slice_in_dim(value, length - width, length, axis=dim), a...]
    ppermute x8 -> x4, waiting for transfers between devices: 5.59 us -> 16.8 us  [the longest x1 11 us: with_sides(): from_right = lax.ppermute(value, axis, grp_pairs(axis, -1))]
    ppermute x8, starting transfers between devices: 23.8 us -> 20.6 us  [on_device(): lax.ppermute(estimate_own, 'grp', grp_pairs('grp', 1))]
    another operation x2 -> x1, other arithmetic: 6.06 us -> 5.9 us  [on_device(): stacked = jnp.stack([perm_local, pressure_start, source])]
  transfers between devices with their start and end apart: 28 -> 24, of which waited for: 12 -> 14; matrix products, arithmetic and copies ran while one was open for 4% -> 4% of each run, Pallas kernels for 0% -> 0%
where the time goes in v2:
time: 228 us; the launch traced here: 227 us
  waiting for transfers between devices  89.7 us (39%)
  starting transfers between devices  64.9 us (28%)
  Pallas kernels  36.1 us (16%)
  other arithmetic  21 us (9%)
  local copies, waits for them, and re-layouts  11.9 us (5%)
  between operations  2.89 us (1%)
    ppermute x8, waiting for transfers between devices, on_device(): lax.ppermute(estimate_own, 'grp', grp_pairs('grp', -1))  60.2 us
    pallas_call x8, Pallas kernels, round_call(): pl.pallas_call(make_round_kernel(weight_now, weight_next, last, own_cols)...  36.1 us
    ppermute x8, starting transfers between devices, on_device(): lax.ppermute(estimate_own, 'grp', grp_pairs('grp', 1))  20.6 us
    ppermute x8, starting transfers between devices, on_device(): lax.ppermute(estimate_own, 'grp', grp_pairs('grp', -1))  18.4 us
    ppermute x1, waiting for transfers between devices, with_sides(): from_right = lax.ppermute(value, axis, grp_pairs(axis, -1))  11 us
    unnamed x58, local copies, waits for them, and re-layouts  8.31 us
    ppermute x1, waiting for transfers between devices, on_device(): from_above = lax.ppermute(correction[:span], 'sub', grp_pairs('sub', -1))  6.25 us
    another operation x1, other arithmetic, on_device(): stacked = jnp.stack([perm_local, pressure_start, source])  5.9 us
  transfers between devices with their start and end apart: 24, of which 14 were waited for; matrix products, arithmetic and copies ran while one was open for 4% of the time, Pallas kernels for 0%

profile of v2, /device:TPU:225, one launch (start us, length us, event | category | flops | bytes accessed | tf_op | source)
XLA Modules:
  0.0 226.5 jit_solution(9071617199318770915)
XLA Ops:
  1.6 5.9 %multiply_bitcast_fusion = f32[1,16,8,128]{3,2,1,0:T(8,128)S(1)} fusion(f32[16,8,128]{2,1,0:T(8,128)} %param.8, s32[16,8,128]{2,1,0:T(8,128)} %param.6, f32[]{:T(128)} %bitcast.7, f32[]{:T(128)} %bitcast.6, f32[]{:T(128)} %bitcast.5, f32[]{:T(128)} %bitcast.4, f32[]{:T(128)} %bitcast.3, f32[]{:T(128)} %bitcast.2, f32[]{:T(128)} %bitcast.1, f32[]{:T(128)} %bitcast), kind=kLoop, calls=%fused_computation.199 | loop fusion | flops 393216 | bytes 196640 | tf_op jit(solution)/shard_map/stack | solution.py:269
  7.6 4.5 %collective-permute-start = (f32[3,5,8,128]{3,2,1,0:T(8,128)S(1)}, f32[3,5,8,128]{3,2,1,0:T(8,128)S(1)}, u32[]{:S(2)}, u32[]{:S(2)}) collective-permute-start(f32[3,5,8,128]{3,2,1,0:T(8,128)S(1)} %get-tuple-element.40), channel_id=1, source_target_pairs={{0,16},{16,32},{32,48},{48,64},{64,80},{80,96},{96,112},{112,128},... | collective-permute-start | bytes 184328 | tf_op jit(solution)/shard_map/ppermute | solution.py:213
  25.8 4.6 %collective-permute-done.2 = f32[3,26,8,128]{3,2,1,0:T(8,128)S(1)} collective-permute-done((f32[3,26,8,128]{3,2,1,0:T(8,128)S(1)}, f32[3,26,8,128]{3,2,1,0:T(8,128)S(1)}, u32[]{:S(2)}, u32[]{:S(2)}) %collective-permute-start.2) | collective-permute-done | bytes 319520 | tf_op jit(solution)/shard_map/ppermute | solution.py:206
  30.4 11.0 %collective-permute-done.3 = f32[3,26,8,128]{3,2,1,0:T(8,128)S(1)} collective-permute-done((f32[3,26,8,128]{3,2,1,0:T(8,128)S(1)}, f32[3,26,8,128]{3,2,1,0:T(8,128)S(1)}, u32[]{:S(2)}, u32[]{:S(2)}) %collective-permute-start.3) | collective-permute-done | bytes 319520 | tf_op jit(solution)/shard_map/ppermute | solution.py:207
  59.7 4.6 %shard_map.64.own_ref = f32[24,8,128]{2,1,0:T(8,128)} custom-call(s32[2]{0:T(128)} %pad_add_fusion.1.depth_ref, f32[24,8,128]{2,1,0:T(8,128)} %copy-done.12, f32[24,8,128]{2,1,0:T(8,128)} %copy-done.10, f32[24,8,128]{2,1,0:T(8,128)} %copy-done.13, f32[24,24,128]{2,1,0:T(8,128)} %copy-done.6, f32[24,24,128]{2,1,0:T(8,128)} %copy-done.5, ...), custom_call_target="tpu_custom_call" | custom-call | tf_op jit(solution)/shard_map/pallas_call | solution.py:191
  64.3 5.5 %collective-permute-start.6 = (f32[24,8,128]{2,1,0:T(8,128)}, f32[24,8,128]{2,1,0:T(8,128)S(1)}, u32[]{:S(2)}, u32[]{:S(2)}) collective-permute-start(f32[24,8,128]{2,1,0:T(8,128)} %shard_map.64.own_ref), channel_id=1, source_target_pairs={{0,1},{1,2},{2,3},{3,4},{4,5},{5,6},{6,7},{7,8},{8,9},{9,10},{10,1... | collective-permute-start | bytes 294920 | tf_op jit(solution)/shard_map/ppermute | solution.py:329
  73.0 7.8 %collective-permute-done.7.right_ref = f32[24,8,128]{2,1,0:T(8,128)S(1)} collective-permute-done((f32[24,8,128]{2,1,0:T(8,128)}, f32[24,8,128]{2,1,0:T(8,128)S(1)}, u32[]{:S(2)}, u32[]{:S(2)}) %collective-permute-start.7) | collective-permute-done | bytes 98336 | tf_op jit(solution)/shard_map/ppermute | solution.py:331
  81.4 4.6 %shard_map.65.own_ref = f32[24,8,128]{2,1,0:T(8,128)} custom-call(s32[2]{0:T(128)} %pad_add_fusion.1.depth_ref, f32[24,8,128]{2,1,0:T(8,128)} %copy-done.19, f32[24,8,128]{2,1,0:T(8,128)} %shard_map.64.own_ref, f32[24,8,128]{2,1,0:T(8,128)} %copy-done.24, f32[24,24,128]{2,1,0:T(8,128)} %copy-done.6, f32[24,24,128]{2,1,0:T(8,128)} %copy-done.5, ...), custom_call_target="tpu_custom_call" | custom-call | tf_op jit(solution)/shard_map/pallas_call | solution.py:191
  91.1 7.7 %collective-permute-done.9.right_ref = f32[24,8,128]{2,1,0:T(8,128)S(1)} collective-permute-done((f32[24,8,128]{2,1,0:T(8,128)}, f32[24,8,128]{2,1,0:T(8,128)S(1)}, u32[]{:S(2)}, u32[]{:S(2)}) %collective-permute-start.9) | collective-permute-done | bytes 98336 | tf_op jit(solution)/shard_map/ppermute | solution.py:331
  99.5 4.6 %shard_map.66.own_ref = f32[24,8,128]{2,1,0:T(8,128)} custom-call(s32[2]{0:T(128)} %pad_add_fusion.1.depth_ref, f32[24,8,128]{2,1,0:T(8,128)} %copy-done.17, f32[24,8,128]{2,1,0:T(8,128)} %shard_map.65.own_ref, f32[24,8,128]{2,1,0:T(8,128)} %copy-done.20, f32[24,24,128]{2,1,0:T(8,128)} %copy-done.6, f32[24,24,128]{2,1,0:T(8,128)} %copy-done.5, ...), custom_call_target="tpu_custom_call" | custom-call | tf_op jit(solution)/shard_map/pallas_call | solution.py:191
  109.1 7.9 %collective-permute-done.11.right_ref = f32[24,8,128]{2,1,0:T(8,128)S(1)} collective-permute-done((f32[24,8,128]{2,1,0:T(8,128)}, f32[24,8,128]{2,1,0:T(8,128)S(1)}, u32[]{:S(2)}, u32[]{:S(2)}) %collective-permute-start.11) | collective-permute-done | bytes 98336 | tf_op jit(solution)/shard_map/ppermute | solution.py:331
  117.6 4.4 %shard_map.67 = f32[24,24,128]{2,1,0:T(8,128)} custom-call(s32[2]{0:T(128)} %pad_add_fusion.1.depth_ref, f32[24,8,128]{2,1,0:T(8,128)} %copy-done.16, f32[24,8,128]{2,1,0:T(8,128)} %shard_map.66.own_ref, f32[24,8,128]{2,1,0:T(8,128)} %copy-done.18, f32[24,24,128]{2,1,0:T(8,128)} %copy-done.6, f32[24,24,128]{2,1,0:T(8,128)} %copy-done.5, ...), custom_call_target="tpu_custom_call" | custom-call | tf_op jit(solution)/shard_map/pallas_call | solution.py:191
  123.1 5.4 %collective-permute-start.12 = (f32[9,24,128]{2,1,0:T(8,128)S(1)}, f32[9,24,128]{2,1,0:T(8,128)S(1)}, u32[]{:S(2)}, u32[]{:S(2)}) collective-permute-start(f32[9,24,128]{2,1,0:T(8,128)S(1)} %get-tuple-element.27), channel_id=1, source_target_pairs={{0,16},{16,32},{32,48},{48,64},{64,80},{80,96},{96,112},{112,128},... | collective-permute-start | bytes 331784 | tf_op jit(solution)/shard_map/ppermute | solution.py:350
  130.5 6.3 %collective-permute-done.13 = f32[9,24,128]{2,1,0:T(8,128)S(1)} collective-permute-done((f32[9,24,128]{2,1,0:T(8,128)S(1)}, f32[9,24,128]{2,1,0:T(8,128)S(1)}, u32[]{:S(2)}, u32[]{:S(2)}) %collective-permute-start.13) | collective-permute-done | bytes 110624 | tf_op jit(solution)/shard_map/ppermute | solution.py:353
  145.3 8.8 %collective-permute-done.15.right_ref = f32[24,8,128]{2,1,0:T(8,128)S(1)} collective-permute-done((f32[24,8,128]{2,1,0:T(8,128)S(1)}, f32[24,8,128]{2,1,0:T(8,128)S(1)}, u32[]{:S(2)}, u32[]{:S(2)}) %collective-permute-start.15) | collective-permute-done | bytes 98336 | tf_op jit(solution)/shard_map/ppermute | solution.py:331
  154.8 4.6 %shard_map.68.own_ref = f32[24,8,128]{2,1,0:T(8,128)} custom-call(s32[2]{0:T(128)} %pad_add_fusion.1.depth_ref, f32[24,8,128]{2,1,0:T(8,128)} %copy-done.21, f32[24,8,128]{2,1,0:T(8,128)} %copy-done.11, f32[24,8,128]{2,1,0:T(8,128)} %copy-done.25, f32[24,24,128]{2,1,0:T(8,128)} %copy-done.7, f32[24,24,128]{2,1,0:T(8,128)} %copy-done.5, ...), custom_call_target="tpu_custom_call" | custom-call | tf_op jit(solution)/shard_map/pallas_call | solution.py:191
  163.7 8.5 %collective-permute-done.17.right_ref = f32[24,8,128]{2,1,0:T(8,128)S(1)} collective-permute-done((f32[24,8,128]{2,1,0:T(8,128)}, f32[24,8,128]{2,1,0:T(8,128)S(1)}, u32[]{:S(2)}, u32[]{:S(2)}) %collective-permute-start.17) | collective-permute-done | bytes 98336 | tf_op jit(solution)/shard_map/ppermute | solution.py:331
  172.9 4.6 %shard_map.69.own_ref = f32[24,8,128]{2,1,0:T(8,128)} custom-call(s32[2]{0:T(128)} %pad_add_fusion.1.depth_ref, f32[24,8,128]{2,1,0:T(8,128)} %copy-done.22, f32[24,8,128]{2,1,0:T(8,128)} %shard_map.68.own_ref, f32[24,8,128]{2,1,0:T(8,128)} %copy-done.26, f32[24,24,128]{2,1,0:T(8,128)} %copy-done.7, f32[24,24,128]{2,1,0:T(8,128)} %copy-done.5, ...), custom_call_target="tpu_custom_call" | custom-call | tf_op jit(solution)/shard_map/pallas_call | solution.py:191
  181.8 8.5 %collective-permute-done.19.right_ref = f32[24,8,128]{2,1,0:T(8,128)S(1)} collective-permute-done((f32[24,8,128]{2,1,0:T(8,128)}, f32[24,8,128]{2,1,0:T(8,128)S(1)}, u32[]{:S(2)}, u32[]{:S(2)}) %collective-permute-start.19) | collective-permute-done | bytes 98336 | tf_op jit(solution)/shard_map/ppermute | solution.py:331
  190.9 4.6 %shard_map.70.own_ref = f32[24,8,128]{2,1,0:T(8,128)} custom-call(s32[2]{0:T(128)} %pad_add_fusion.1.depth_ref, f32[24,8,128]{2,1,0:T(8,128)} %copy-done.23, f32[24,8,128]{2,1,0:T(8,128)} %shard_map.69.own_ref, f32[24,8,128]{2,1,0:T(8,128)} %copy-done.27, f32[24,24,128]{2,1,0:T(8,128)} %copy-done.7, f32[24,24,128]{2,1,0:T(8,128)} %copy-done.5, ...), custom_call_target="tpu_custom_call" | custom-call | tf_op jit(solution)/shard_map/pallas_call | solution.py:191
  199.9 8.5 %collective-permute-done.21.right_ref = f32[24,8,128]{2,1,0:T(8,128)S(1)} collective-permute-done((f32[24,8,128]{2,1,0:T(8,128)}, f32[24,8,128]{2,1,0:T(8,128)S(1)}, u32[]{:S(2)}, u32[]{:S(2)}) %collective-permute-start.21) | collective-permute-done | bytes 98336 | tf_op jit(solution)/shard_map/ppermute | solution.py:331
  209.0 4.4 %shard_map.71 = f32[24,24,128]{2,1,0:T(8,128)} custom-call(s32[2]{0:T(128)} %pad_add_fusion.1.depth_ref, f32[24,8,128]{2,1,0:T(8,128)} %copy-done.14, f32[24,8,128]{2,1,0:T(8,128)} %shard_map.70.own_ref, f32[24,8,128]{2,1,0:T(8,128)} %copy-done.15, f32[24,24,128]{2,1,0:T(8,128)} %copy-done.7, f32[24,24,128]{2,1,0:T(8,128)} %copy-done.5, ...), custom_call_target="tpu_custom_call" | custom-call | tf_op jit(solution)/shard_map/pallas_call | solution.py:191
  214.5 4.2 %collective-permute-start.22 = (f32[4,8,128]{2,1,0:T(8,128)S(1)}, f32[4,8,128]{2,1,0:T(8,128)S(1)}, u32[]{:S(2)}, u32[]{:S(2)}) collective-permute-start(f32[4,8,128]{2,1,0:T(8,128)S(1)} %get-tuple-element.25), channel_id=1, source_target_pairs={{0,16},{16,32},{32,48},{48,64},{64,80},{80,96},{96,112},{112,128},... | collective-permute-start | bytes 49160 | tf_op jit(solution)/shard_map/ppermute | solution.py:365
  220.6 5.2 %collective-permute-done.23 = f32[4,8,128]{2,1,0:T(8,128)S(1)} collective-permute-done((f32[4,8,128]{2,1,0:T(8,128)S(1)}, f32[4,8,128]{2,1,0:T(8,128)S(1)}, u32[]{:S(2)}, u32[]{:S(2)}) %collective-permute-start.23) | collective-permute-done | bytes 16416 | tf_op jit(solution)/shard_map/ppermute | solution.py:368
  (190 shorter events, 77.0 us)
Async XLA Ops:
  7.6 11.1 %collective-permute-start = (f32[3,5,8,128]{3,2,1,0:T(8,128)S(1)}, f32[3,5,8,128]{3,2,1,0:T(8,128)S(1)}, u32[]{:S(2)}, u32[]{:S(2)}) collective-permute-start(f32[3,5,8,128]{3,2,1,0:T(8,128)S(1)} %get-tuple-element.40), channel_id=1, source_target_pairs={{0,16},{16,32},{32,48},{48,64},{64,80},{80,96},{96,112},{112,128},... | collective-permute-start | bytes 184328 | tf_op jit(solution)/shard_map/ppermute | solution.py:213
  12.1 7.7 %collective-permute-start.1 = (f32[3,5,8,128]{3,2,1,0:T(8,128)S(1)}, f32[3,5,8,128]{3,2,1,0:T(8,128)S(1)}, u32[]{:S(2)}, u32[]{:S(2)}) collective-permute-start(f32[3,5,8,128]{3,2,1,0:T(8,128)S(1)} %get-tuple-element.41), channel_id=1, source_target_pairs={{16,0},{32,16},{48,32},{64,48},{80,64},{96,80},{112,96},{128,112},... | collective-permute-start | bytes 184328 | tf_op jit(solution)/shard_map/ppermute | solution.py:216
  19.8 10.6 %collective-permute-start.2 = (f32[3,26,8,128]{3,2,1,0:T(8,128)S(1)}, f32[3,26,8,128]{3,2,1,0:T(8,128)S(1)}, u32[]{:S(2)}, u32[]{:S(2)}) collective-permute-start(f32[3,26,8,128]{3,2,1,0:T(8,128)S(1)} %pad_maximum_fusion.1), channel_id=1, source_target_pairs={{0,1},{1,2},{2,3},{3,4},{4,5},{5,6},{6,7},{7,8},{8,9},{9,10},{10,1... | collective-permute-start | bytes 958472 | tf_op jit(solution)/shard_map/ppermute | solution.py:206
  23.1 18.4 %collective-permute-start.3 = (f32[3,26,8,128]{3,2,1,0:T(8,128)S(1)}, f32[3,26,8,128]{3,2,1,0:T(8,128)S(1)}, u32[]{:S(2)}, u32[]{:S(2)}) collective-permute-start(f32[3,26,8,128]{3,2,1,0:T(8,128)S(1)} %pad_maximum_fusion.1), channel_id=1, source_target_pairs={{1,0},{2,1},{3,2},{4,3},{5,4},{6,5},{7,6},{8,7},{9,8},{10,9},{11,1... | collective-permute-start | bytes 958472 | tf_op jit(solution)/shard_map/ppermute | solution.py:207
  46.4 10.2 %collective-permute-start.4 = (f32[24,8,128]{2,1,0:T(8,128)S(1)}, f32[24,8,128]{2,1,0:T(8,128)S(1)}, u32[]{:S(2)}, u32[]{:S(2)}) collective-permute-start(f32[24,8,128]{2,1,0:T(8,128)S(1)} %multiply_multiply_fusion.1.own_ref), channel_id=1, source_target_pairs={{0,1},{1,2},{2,3},{3,4},{4,5},{5,6},{6,7},{7,8},{8,9},{9,10},{10,1... | collective-permute-start | bytes 294920 | tf_op jit(solution)/shard_map/ppermute | solution.py:329
  48.3 10.7 %collective-permute-start.5 = (f32[24,8,128]{2,1,0:T(8,128)S(1)}, f32[24,8,128]{2,1,0:T(8,128)S(1)}, u32[]{:S(2)}, u32[]{:S(2)}) collective-permute-start(f32[24,8,128]{2,1,0:T(8,128)S(1)} %multiply_multiply_fusion.1.own_ref), channel_id=1, source_target_pairs={{1,0},{2,1},{3,2},{4,3},{5,4},{6,5},{7,6},{8,7},{9,8},{10,9},{11,1... | collective-permute-start | bytes 294920 | tf_op jit(solution)/shard_map/ppermute | solution.py:331
  64.3 8.7 %collective-permute-start.6 = (f32[24,8,128]{2,1,0:T(8,128)}, f32[24,8,128]{2,1,0:T(8,128)S(1)}, u32[]{:S(2)}, u32[]{:S(2)}) collective-permute-start(f32[24,8,128]{2,1,0:T(8,128)} %shard_map.64.own_ref), channel_id=1, source_target_pairs={{0,1},{1,2},{2,3},{3,4},{4,5},{5,6},{6,7},{7,8},{8,9},{9,10},{10,1... | collective-permute-start | bytes 294920 | tf_op jit(solution)/shard_map/ppermute | solution.py:329
  69.8 11.0 %collective-permute-start.7 = (f32[24,8,128]{2,1,0:T(8,128)}, f32[24,8,128]{2,1,0:T(8,128)S(1)}, u32[]{:S(2)}, u32[]{:S(2)}) collective-permute-start(f32[24,8,128]{2,1,0:T(8,128)} %shard_map.64.own_ref), channel_id=1, source_target_pairs={{1,0},{2,1},{3,2},{4,3},{5,4},{6,5},{7,6},{8,7},{9,8},{10,9},{11,1... | collective-permute-start | bytes 294920 | tf_op jit(solution)/shard_map/ppermute | solution.py:331
  86.0 5.1 %collective-permute-start.8 = (f32[24,8,128]{2,1,0:T(8,128)}, f32[24,8,128]{2,1,0:T(8,128)S(1)}, u32[]{:S(2)}, u32[]{:S(2)}) collective-permute-start(f32[24,8,128]{2,1,0:T(8,128)} %shard_map.65.own_ref), channel_id=1, source_target_pairs={{0,1},{1,2},{2,3},{3,4},{4,5},{5,6},{6,7},{7,8},{8,9},{9,10},{10,1... | collective-permute-start | bytes 294920 | tf_op jit(solution)/shard_map/ppermute | solution.py:329
  87.9 11.0 %collective-permute-start.9 = (f32[24,8,128]{2,1,0:T(8,128)}, f32[24,8,128]{2,1,0:T(8,128)S(1)}, u32[]{:S(2)}, u32[]{:S(2)}) collective-permute-start(f32[24,8,128]{2,1,0:T(8,128)} %shard_map.65.own_ref), channel_id=1, source_target_pairs={{1,0},{2,1},{3,2},{4,3},{5,4},{6,5},{7,6},{8,7},{9,8},{10,9},{11,1... | collective-permute-start | bytes 294920 | tf_op jit(solution)/shard_map/ppermute | solution.py:331
  104.1 5.0 %collective-permute-start.10 = (f32[24,8,128]{2,1,0:T(8,128)}, f32[24,8,128]{2,1,0:T(8,128)S(1)}, u32[]{:S(2)}, u32[]{:S(2)}) collective-permute-start(f32[24,8,128]{2,1,0:T(8,128)} %shard_map.66.own_ref), channel_id=1, source_target_pairs={{0,1},{1,2},{2,3},{3,4},{4,5},{5,6},{6,7},{7,8},{8,9},{9,10},{10,1... | collective-permute-start | bytes 294920 | tf_op jit(solution)/shard_map/ppermute | solution.py:329
  106.0 11.0 %collective-permute-start.11 = (f32[24,8,128]{2,1,0:T(8,128)}, f32[24,8,128]{2,1,0:T(8,128)S(1)}, u32[]{:S(2)}, u32[]{:S(2)}) collective-permute-start(f32[24,8,128]{2,1,0:T(8,128)} %shard_map.66.own_ref), channel_id=1, source_target_pairs={{1,0},{2,1},{3,2},{4,3},{5,4},{6,5},{7,6},{8,7},{9,8},{10,9},{11,1... | collective-permute-start | bytes 294920 | tf_op jit(solution)/shard_map/ppermute | solution.py:331
  123.1 7.4 %collective-permute-start.12 = (f32[9,24,128]{2,1,0:T(8,128)S(1)}, f32[9,24,128]{2,1,0:T(8,128)S(1)}, u32[]{:S(2)}, u32[]{:S(2)}) collective-permute-start(f32[9,24,128]{2,1,0:T(8,128)S(1)} %get-tuple-element.27), channel_id=1, source_target_pairs={{0,16},{16,32},{32,48},{48,64},{64,80},{80,96},{96,112},{112,128},... | collective-permute-start | bytes 331784 | tf_op jit(solution)/shard_map/ppermute | solution.py:350
  128.5 8.2 %collective-permute-start.13 = (f32[9,24,128]{2,1,0:T(8,128)S(1)}, f32[9,24,128]{2,1,0:T(8,128)S(1)}, u32[]{:S(2)}, u32[]{:S(2)}) collective-permute-start(f32[9,24,128]{2,1,0:T(8,128)S(1)} %get-tuple-element.28), channel_id=1, source_target_pairs={{16,0},{32,16},{48,32},{64,48},{80,64},{96,80},{112,96},{128,112},... | collective-permute-start | bytes 331784 | tf_op jit(solution)/shard_map/ppermute | solution.py:353
  139.8 5.5 %collective-permute-start.14 = (f32[24,8,128]{2,1,0:T(8,128)S(1)}, f32[24,8,128]{2,1,0:T(8,128)S(1)}, u32[]{:S(2)}, u32[]{:S(2)}) collective-permute-start(f32[24,8,128]{2,1,0:T(8,128)S(1)} %multiply_multiply_fusion.own_ref), channel_id=1, source_target_pairs={{0,1},{1,2},{2,3},{3,4},{4,5},{5,6},{6,7},{7,8},{8,9},{9,10},{10,1... | collective-permute-start | bytes 294920 | tf_op jit(solution)/shard_map/ppermute | solution.py:329
  143.4 10.7 %collective-permute-start.15 = (f32[24,8,128]{2,1,0:T(8,128)S(1)}, f32[24,8,128]{2,1,0:T(8,128)S(1)}, u32[]{:S(2)}, u32[]{:S(2)}) collective-permute-start(f32[24,8,128]{2,1,0:T(8,128)S(1)} %multiply_multiply_fusion.own_ref), channel_id=1, source_target_pairs={{1,0},{2,1},{3,2},{4,3},{5,4},{6,5},{7,6},{8,7},{9,8},{10,9},{11,1... | collective-permute-start | bytes 294920 | tf_op jit(solution)/shard_map/ppermute | solution.py:331
  159.3 4.3 %collective-permute-start.16 = (f32[24,8,128]{2,1,0:T(8,128)}, f32[24,8,128]{2,1,0:T(8,128)S(1)}, u32[]{:S(2)}, u32[]{:S(2)}) collective-permute-start(f32[24,8,128]{2,1,0:T(8,128)} %shard_map.68.own_ref), channel_id=1, source_target_pairs={{0,1},{1,2},{2,3},{3,4},{4,5},{5,6},{6,7},{7,8},{8,9},{9,10},{10,1... | collective-permute-start | bytes 294920 | tf_op jit(solution)/shard_map/ppermute | solution.py:329
  161.3 11.0 %collective-permute-start.17 = (f32[24,8,128]{2,1,0:T(8,128)}, f32[24,8,128]{2,1,0:T(8,128)S(1)}, u32[]{:S(2)}, u32[]{:S(2)}) collective-permute-start(f32[24,8,128]{2,1,0:T(8,128)} %shard_map.68.own_ref), channel_id=1, source_target_pairs={{1,0},{2,1},{3,2},{4,3},{5,4},{6,5},{7,6},{8,7},{9,8},{10,9},{11,1... | collective-permute-start | bytes 294920 | tf_op jit(solution)/shard_map/ppermute | solution.py:331
  177.4 4.3 %collective-permute-start.18 = (f32[24,8,128]{2,1,0:T(8,128)}, f32[24,8,128]{2,1,0:T(8,128)S(1)}, u32[]{:S(2)}, u32[]{:S(2)}) collective-permute-start(f32[24,8,128]{2,1,0:T(8,128)} %shard_map.69.own_ref), channel_id=1, source_target_pairs={{0,1},{1,2},{2,3},{3,4},{4,5},{5,6},{6,7},{7,8},{8,9},{9,10},{10,1... | collective-permute-start | bytes 294920 | tf_op jit(solution)/shard_map/ppermute | solution.py:329
  179.3 11.0 %collective-permute-start.19 = (f32[24,8,128]{2,1,0:T(8,128)}, f32[24,8,128]{2,1,0:T(8,128)S(1)}, u32[]{:S(2)}, u32[]{:S(2)}) collective-permute-start(f32[24,8,128]{2,1,0:T(8,128)} %shard_map.69.own_ref), channel_id=1, source_target_pairs={{1,0},{2,1},{3,2},{4,3},{5,4},{6,5},{7,6},{8,7},{9,8},{10,9},{11,1... | collective-permute-start | bytes 294920 | tf_op jit(solution)/shard_map/ppermute | solution.py:331
  195.5 4.3 %collective-permute-start.20 = (f32[24,8,128]{2,1,0:T(8,128)}, f32[24,8,128]{2,1,0:T(8,128)S(1)}, u32[]{:S(2)}, u32[]{:S(2)}) collective-permute-start(f32[24,8,128]{2,1,0:T(8,128)} %shard_map.70.own_ref), channel_id=1, source_target_pairs={{0,1},{1,2},{2,3},{3,4},{4,5},{5,6},{6,7},{7,8},{8,9},{9,10},{10,1... | collective-permute-start | bytes 294920 | tf_op jit(solution)/shard_map/ppermute | solution.py:329
  197.4 11.0 %collective-permute-start.21 = (f32[24,8,128]{2,1,0:T(8,128)}, f32[24,8,128]{2,1,0:T(8,128)S(1)}, u32[]{:S(2)}, u32[]{:S(2)}) collective-permute-start(f32[24,8,128]{2,1,0:T(8,128)} %shard_map.70.own_ref), channel_id=1, source_target_pairs={{1,0},{2,1},{3,2},{4,3},{5,4},{6,5},{7,6},{8,7},{9,8},{10,9},{11,1... | collective-permute-start | bytes 294920 | tf_op jit(solution)/shard_map/ppermute | solution.py:331
  214.5 6.2 %collective-permute-start.22 = (f32[4,8,128]{2,1,0:T(8,128)S(1)}, f32[4,8,128]{2,1,0:T(8,128)S(1)}, u32[]{:S(2)}, u32[]{:S(2)}) collective-permute-start(f32[4,8,128]{2,1,0:T(8,128)S(1)} %get-tuple-element.25), channel_id=1, source_target_pairs={{0,16},{16,32},{32,48},{48,64},{64,80},{80,96},{96,112},{112,128},... | collective-permute-start | bytes 49160 | tf_op jit(solution)/shard_map/ppermute | solution.py:365
  218.7 7.2 %collective-permute-start.23 = (f32[4,8,128]{2,1,0:T(8,128)S(1)}, f32[4,8,128]{2,1,0:T(8,128)S(1)}, u32[]{:S(2)}, u32[]{:S(2)}) collective-permute-start(f32[4,8,128]{2,1,0:T(8,128)S(1)} %get-tuple-element.26), channel_id=1, source_target_pairs={{16,0},{32,16},{48,32},{64,48},{80,64},{96,80},{112,96},{128,112},... | collective-permute-start | bytes 49160 | tf_op jit(solution)/shard_map/ppermute | solution.py:368
  (29 other events, 113.4 us)

commit v3 on v2

--- a/solution.py
+++ b/solution.py
@@ -268,21 +268,25 @@
 
     stacked = jnp.stack([perm_local, pressure_start, source])
     stacked = with_rows(stacked, "sub", 1, OV + 1)
+    far_left = lax.ppermute(stacked[:, :, tile_cols - 1 :], "grp", grp_pairs("grp", 2))
+    far_right = lax.ppermute(stacked[:, :, :1], "grp", grp_pairs("grp", -2))
     stacked = with_sides(stacked, "grp", 2)
+    pressure_edge = jnp.concatenate([far_left[1], stacked[1], far_right[1]], axis=1)
+    perm_edge = jnp.concatenate([far_left[0], stacked[0], far_right[0]], axis=1)
     perm_wide = stacked[0]
     pressure_wide = stacked[1]
     source_wide = stacked[2][1:-1]
 
     faces_vertical = harmonic(perm_wide[:-1], perm_wide[1:])
     middle_block = perm_wide[1:-1]
-    faces_across = harmonic(middle_block[:, :-1], middle_block[:, 1:])
+    middle_edge = perm_edge[1:-1]
+    faces_across = harmonic(middle_edge[:, :-1], middle_edge[:, 1:])
     faces_along = harmonic(middle_block[:, :, :-1], middle_block[:, :, 1:])
-    zero_col = jnp.zeros_like(middle_block[:, :1])
     zero_lane = jnp.zeros_like(middle_block[:, :, :1])
     face_below = faces_vertical[:-1]
     face_above = faces_vertical[1:]
-    face_left = jnp.concatenate([zero_col, faces_across], axis=1)
-    face_right = jnp.concatenate([faces_across, zero_col], axis=1)
+    face_left = faces_across[:, :-1]
+    face_right = faces_across[:, 1:]
     face_front = jnp.concatenate([zero_lane, faces_along], axis=2)
     face_back = jnp.concatenate([faces_along, zero_lane], axis=2)
     diagonal = STORE + face_below + face_above + face_left + face_right + face_front + face_back
@@ -307,29 +311,39 @@
     full_active = jnp.broadcast_to(active, diagonal.shape)
     own_active = jnp.broadcast_to(active, own_coeffs[0].shape)
     factors_x = line_factors(own_coeffs, own_active, 1)
+    factors_wide_x = line_factors(coeffs, full_active, 1)
     factors_y = line_factors(coeffs, full_active, 2)
     factors_z = line_factors(coeffs, full_active, 0)
 
     rows_pad = jnp.zeros_like(pressure_wide[:1])
     for outer_turn in range(OUTER):
+        if outer_turn > 0:
+            pressure_edge = jnp.pad(pressure_wide, ((0, 0), (1, 1), (0, 0)))
         center = pressure_wide[1:-1]
         coupled = (
             face_below * pressure_wide[:-2]
             + face_above * pressure_wide[2:]
-            + face_left * lower_nb(center, 1)
-            + face_right * upper_nb(center, 1)
+            + face_left * pressure_edge[1:-1, :-2]
+            + face_right * pressure_edge[1:-1, 2:]
             + face_front * lower_nb(center, 2)
             + face_back * upper_nb(center, 2)
         )
         residual = source_wide - (diagonal * center - coupled)
         target = residual * active
-        estimate_own = relax_weight(0) * solve_lines(factors_x, target[:, own])
+        if outer_turn == 0:
+            first = relax_weight(0) * solve_lines(factors_wide_x, target)
+            first_pieces = (first[:, :tile_cols], first[:, own], first[:, 2 * tile_cols :])
+        else:
+            estimate_own = relax_weight(0) * solve_lines(factors_x, target[:, own])
         for round_index in range(ROUNDS):
-            pieces = (
-                lax.ppermute(estimate_own, "grp", grp_pairs("grp", 1)),
-                estimate_own,
-                lax.ppermute(estimate_own, "grp", grp_pairs("grp", -1)),
-            )
+            if round_index == 0 and outer_turn == 0:
+                pieces = first_pieces
+            else:
+                pieces = (
+                    lax.ppermute(estimate_own, "grp", grp_pairs("grp", 1)),
+                    estimate_own,
+                    lax.ppermute(estimate_own, "grp", grp_pairs("grp", -1)),
+                )
             last = round_index + 1 == ROUNDS
             estimate = round_call(
                 relax_weight(round_index),

time: 228 us -> 231 us (1.013)
  starting transfers between devices: 64.9 us -> 70.5 us
  waiting for transfers between devices: 89.7 us -> 84.9 us
  other arithmetic: 21 us -> 24.6 us
    ppermute x0 -> x2, waiting for transfers between devices: none -> 9.53 us  [the longest x1 9.53 us: on_device(): far_right = lax.ppermute(stacked[:, :, :1], 'grp', grp_pairs('grp', -2))]
    ppermute x1, waiting for transfers between devices: 11 us -> 3.49 us  [with_sides(): from_right = lax.ppermute(value, axis, grp_pairs(axis, -1))]
    ppermute x1, starting transfers between devices: 3.29 us -> 10.5 us  [with_sides(): from_left = lax.ppermute(value, axis, grp_pairs(axis, 1))]
    ppermute x1, waiting for transfers between devices: 4.64 us -> 0.01 us  [with_sides(): from_left = lax.ppermute(value, axis, grp_pairs(axis, 1))]
    ppermute x0 -> x2, starting transfers between devices: none -> 3.84 us  [the longest x1 1.92 us: on_device(): lax.ppermute(stacked[:, :, tile_cols - 1:], 'grp', grp_pairs('grp', 2))]
    ppermute x8 -> x7, starting transfers between devices: 18.4 us -> 16 us  [on_device(): lax.ppermute(estimate_own, 'grp', grp_pairs('grp', -1))]
    ppermute x8 -> x7, starting transfers between devices: 20.6 us -> 18.9 us  [on_device(): lax.ppermute(estimate_own, 'grp', grp_pairs('grp', 1))]
    unnamed x58 -> x48, local copies, waits for them, and re-layouts: 8.31 us -> 7.12 us
  transfers between devices with their start and end apart: 24 -> 24, of which waited for: 14 -> 12; matrix products, arithmetic and copies ran while one was open for 4% -> 1% of each run, Pallas kernels for 0% -> 0%
where the time goes in v3:
time: 231 us; the launch traced here: 230 us
  waiting for transfers between devices  84.9 us (37%)
  starting transfers between devices  70.5 us (31%)
  Pallas kernels  36.1 us (16%)
  other arithmetic  24.6 us (11%)
  local copies, waits for them, and re-layouts  10.7 us (5%)
  between operations  2.85 us (1%)
    ppermute x7, waiting for transfers between devices, on_device(): lax.ppermute(estimate_own, 'grp', grp_pairs('grp', -1))  59.2 us
    pallas_call x8, Pallas kernels, round_call(): pl.pallas_call(make_round_kernel(weight_now, weight_next, last, own_cols)...  36.1 us
    ppermute x7, starting transfers between devices, on_device(): lax.ppermute(estimate_own, 'grp', grp_pairs('grp', 1))  18.9 us
    ppermute x7, starting transfers between devices, on_device(): lax.ppermute(estimate_own, 'grp', grp_pairs('grp', -1))  16 us
    ppermute x1, starting transfers between devices, with_sides(): from_left = lax.ppermute(value, axis, grp_pairs(axis, 1))  10.5 us
    ppermute x1, waiting for transfers between devices, on_device(): far_right = lax.ppermute(stacked[:, :, :1], 'grp', grp_pairs('grp', -2))  9.53 us
    unnamed x48, local copies, waits for them, and re-layouts  7.12 us
    ppermute x1, waiting for transfers between devices, on_device(): from_above = lax.ppermute(correction[:span], 'sub', grp_pairs('sub', -1))  6.25 us
  transfers between devices with their start and end apart: 24, of which 12 were waited for; matrix products, arithmetic and copies ran while one was open for 1% of the time, Pallas kernels for 0%

profile of v3, /device:TPU:225, one launch (start us, length us, event | category | flops | bytes accessed | tf_op | source)
XLA Modules:
  0.0 229.8 jit_solution(5222661744998851321)
XLA Ops:
  1.6 6.0 %multiply_bitcast_fusion = f32[1,16,8,128]{3,2,1,0:T(8,128)S(1)} fusion(f32[16,8,128]{2,1,0:T(8,128)} %param.8, s32[16,8,128]{2,1,0:T(8,128)} %param.6, f32[]{:T(128)} %bitcast.7, f32[]{:T(128)} %bitcast.6, f32[]{:T(128)} %bitcast.5, f32[]{:T(128)} %bitcast.4, f32[]{:T(128)} %bitcast.3, f32[]{:T(128)} %bitcast.2, f32[]{:T(128)} %bitcast.1, f32[]{:T(128)} %bitcast), kind=kLoop, calls=%fused_computation.237 | loop fusion | flops 393216 | bytes 196640 | tf_op jit(solution)/shard_map/stack | solution.py:269
  7.6 4.5 %collective-permute-start = (f32[3,5,8,128]{3,2,1,0:T(8,128)S(1)}, f32[3,5,8,128]{3,2,1,0:T(8,128)S(1)}, u32[]{:S(2)}, u32[]{:S(2)}) collective-permute-start(f32[3,5,8,128]{3,2,1,0:T(8,128)S(1)} %get-tuple-element.52), channel_id=1, source_target_pairs={{0,16},{16,32},{32,48},{48,64},{64,80},{80,96},{96,112},{112,128},... | collective-permute-start | bytes 184328 | tf_op jit(solution)/shard_map/ppermute | solution.py:213
  22.0 10.5 %collective-permute-start.2 = (f32[3,26,8,128]{3,2,1,0:T(8,128)S(1)}, f32[3,26,8,128]{3,2,1,0:T(8,128)S(1)}, u32[]{:S(2)}, u32[]{:S(2)}) collective-permute-start(f32[3,26,8,128]{3,2,1,0:T(8,128)S(1)} %pad_maximum_fusion.3), channel_id=1, source_target_pairs={{0,1},{1,2},{2,3},{3,4},{4,5},{5,6},{6,7},{7,8},{8,9},{9,10},{10,1... | collective-permute-start | bytes 958472 | tf_op jit(solution)/shard_map/ppermute | solution.py:206
  36.3 9.5 %collective-permute-done.5 = f32[3,26,1,128]{3,2,1,0:T(1,128)S(1)} collective-permute-done((f32[3,26,1,128]{3,2,1,0:T(1,128)S(1)}, f32[3,26,1,128]{3,2,1,0:T(1,128)S(1)}, u32[]{:S(2)}, u32[]{:S(2)}) %collective-permute-start.5) | collective-permute-done | bytes 39968 | tf_op jit(solution)/shard_map/ppermute | solution.py:272
  63.1 4.6 %shard_map.64.own_ref = f32[24,8,128]{2,1,0:T(8,128)} custom-call(s32[2]{0:T(128)} %pad_add_fusion.1.depth_ref, f32[24,8,128]{2,1,0:T(8,128)} %get-tuple-element.49.left_ref, f32[24,8,128]{2,1,0:T(8,128)} %get-tuple-element.48.own_ref, f32[24,8,128]{2,1,0:T(8,128)} %get-tuple-element.47.right_ref, f32[24,24,128]{2,1,0:T(8,128)} %copy-done, ...), custom_call_target="tpu_custom_call" | custom-call | tf_op jit(solution)/shard_map/pallas_call | solution.py:191
  67.7 5.2 %collective-permute-start.6 = (f32[24,8,128]{2,1,0:T(8,128)}, f32[24,8,128]{2,1,0:T(8,128)S(1)}, u32[]{:S(2)}, u32[]{:S(2)}) collective-permute-start(f32[24,8,128]{2,1,0:T(8,128)} %shard_map.64.own_ref), channel_id=1, source_target_pairs={{0,1},{1,2},{2,3},{3,4},{4,5},{5,6},{6,7},{7,8},{8,9},{9,10},{10,1... | collective-permute-start | bytes 294920 | tf_op jit(solution)/shard_map/ppermute | solution.py:343
  74.8 9.3 %collective-permute-done.7.right_ref = f32[24,8,128]{2,1,0:T(8,128)S(1)} collective-permute-done((f32[24,8,128]{2,1,0:T(8,128)}, f32[24,8,128]{2,1,0:T(8,128)S(1)}, u32[]{:S(2)}, u32[]{:S(2)}) %collective-permute-start.7) | collective-permute-done | bytes 98336 | tf_op jit(solution)/shard_map/ppermute | solution.py:345
  84.7 4.6 %shard_map.65.own_ref = f32[24,8,128]{2,1,0:T(8,128)} custom-call(s32[2]{0:T(128)} %pad_add_fusion.1.depth_ref, f32[24,8,128]{2,1,0:T(8,128)} %copy-done.14, f32[24,8,128]{2,1,0:T(8,128)} %shard_map.64.own_ref, f32[24,8,128]{2,1,0:T(8,128)} %copy-done.19, f32[24,24,128]{2,1,0:T(8,128)} %copy-done, f32[24,24,128]{2,1,0:T(8,128)} %copy-done.2, ...), custom_call_target="tpu_custom_call" | custom-call | tf_op jit(solution)/shard_map/pallas_call | solution.py:191
  94.4 7.7 %collective-permute-done.9.right_ref = f32[24,8,128]{2,1,0:T(8,128)S(1)} collective-permute-done((f32[24,8,128]{2,1,0:T(8,128)}, f32[24,8,128]{2,1,0:T(8,128)S(1)}, u32[]{:S(2)}, u32[]{:S(2)}) %collective-permute-start.9) | collective-permute-done | bytes 98336 | tf_op jit(solution)/shard_map/ppermute | solution.py:345
  102.8 4.6 %shard_map.66.own_ref = f32[24,8,128]{2,1,0:T(8,128)} custom-call(s32[2]{0:T(128)} %pad_add_fusion.1.depth_ref, f32[24,8,128]{2,1,0:T(8,128)} %copy-done.12, f32[24,8,128]{2,1,0:T(8,128)} %shard_map.65.own_ref, f32[24,8,128]{2,1,0:T(8,128)} %copy-done.15, f32[24,24,128]{2,1,0:T(8,128)} %copy-done, f32[24,24,128]{2,1,0:T(8,128)} %copy-done.2, ...), custom_call_target="tpu_custom_call" | custom-call | tf_op jit(solution)/shard_map/pallas_call | solution.py:191
  112.3 7.9 %collective-permute-done.11.right_ref = f32[24,8,128]{2,1,0:T(8,128)S(1)} collective-permute-done((f32[24,8,128]{2,1,0:T(8,128)}, f32[24,8,128]{2,1,0:T(8,128)S(1)}, u32[]{:S(2)}, u32[]{:S(2)}) %collective-permute-start.11) | collective-permute-done | bytes 98336 | tf_op jit(solution)/shard_map/ppermute | solution.py:345
  120.9 4.4 %shard_map.67 = f32[24,24,128]{2,1,0:T(8,128)} custom-call(s32[2]{0:T(128)} %pad_add_fusion.1.depth_ref, f32[24,8,128]{2,1,0:T(8,128)} %copy-done.11, f32[24,8,128]{2,1,0:T(8,128)} %shard_map.66.own_ref, f32[24,8,128]{2,1,0:T(8,128)} %copy-done.13, f32[24,24,128]{2,1,0:T(8,128)} %copy-done, f32[24,24,128]{2,1,0:T(8,128)} %copy-done.2, ...), custom_call_target="tpu_custom_call" | custom-call | tf_op jit(solution)/shard_map/pallas_call | solution.py:191
  126.3 5.1 %collective-permute-start.12 = (f32[9,24,128]{2,1,0:T(8,128)S(1)}, f32[9,24,128]{2,1,0:T(8,128)S(1)}, u32[]{:S(2)}, u32[]{:S(2)}) collective-permute-start(f32[9,24,128]{2,1,0:T(8,128)S(1)} %get-tuple-element.38), channel_id=1, source_target_pairs={{0,16},{16,32},{32,48},{48,64},{64,80},{80,96},{96,112},{112,128},... | collective-permute-start | bytes 331784 | tf_op jit(solution)/shard_map/ppermute | solution.py:364
  133.4 6.3 %collective-permute-done.13 = f32[9,24,128]{2,1,0:T(8,128)S(1)} collective-permute-done((f32[9,24,128]{2,1,0:T(8,128)S(1)}, f32[9,24,128]{2,1,0:T(8,128)S(1)}, u32[]{:S(2)}, u32[]{:S(2)}) %collective-permute-start.13) | collective-permute-done | bytes 110624 | tf_op jit(solution)/shard_map/ppermute | solution.py:367
  142.7 4.2 %collective-permute-start.14 = (f32[24,8,128]{2,1,0:T(8,128)S(1)}, f32[24,8,128]{2,1,0:T(8,128)S(1)}, u32[]{:S(2)}, u32[]{:S(2)}) collective-permute-start(f32[24,8,128]{2,1,0:T(8,128)S(1)} %multiply_multiply_fusion.1.own_ref), channel_id=1, source_target_pairs={{0,1},{1,2},{2,3},{3,4},{4,5},{5,6},{6,7},{7,8},{8,9},{9,10},{10,1... | collective-permute-start | bytes 294920 | tf_op jit(solution)/shard_map/ppermute | solution.py:343
  148.9 8.8 %collective-permute-done.15.right_ref = f32[24,8,128]{2,1,0:T(8,128)S(1)} collective-permute-done((f32[24,8,128]{2,1,0:T(8,128)S(1)}, f32[24,8,128]{2,1,0:T(8,128)S(1)}, u32[]{:S(2)}, u32[]{:S(2)}) %collective-permute-start.15) | collective-permute-done | bytes 98336 | tf_op jit(solution)/shard_map/ppermute | solution.py:345
  158.3 4.6 %shard_map.68.own_ref = f32[24,8,128]{2,1,0:T(8,128)} custom-call(s32[2]{0:T(128)} %pad_add_fusion.1.depth_ref, f32[24,8,128]{2,1,0:T(8,128)} %copy-done.16, f32[24,8,128]{2,1,0:T(8,128)} %copy-done.8, f32[24,8,128]{2,1,0:T(8,128)} %copy-done.20, f32[24,24,128]{2,1,0:T(8,128)} %copy-done.5, f32[24,24,128]{2,1,0:T(8,128)} %copy-done.2, ...), custom_call_target="tpu_custom_call" | custom-call | tf_op jit(solution)/shard_map/pallas_call | solution.py:191
  167.2 8.5 %collective-permute-done.17.right_ref = f32[24,8,128]{2,1,0:T(8,128)S(1)} collective-permute-done((f32[24,8,128]{2,1,0:T(8,128)}, f32[24,8,128]{2,1,0:T(8,128)S(1)}, u32[]{:S(2)}, u32[]{:S(2)}) %collective-permute-start.17) | collective-permute-done | bytes 98336 | tf_op jit(solution)/shard_map/ppermute | solution.py:345
  176.4 4.6 %shard_map.69.own_ref = f32[24,8,128]{2,1,0:T(8,128)} custom-call(s32[2]{0:T(128)} %pad_add_fusion.1.depth_ref, f32[24,8,128]{2,1,0:T(8,128)} %copy-done.17, f32[24,8,128]{2,1,0:T(8,128)} %shard_map.68.own_ref, f32[24,8,128]{2,1,0:T(8,128)} %copy-done.21, f32[24,24,128]{2,1,0:T(8,128)} %copy-done.5, f32[24,24,128]{2,1,0:T(8,128)} %copy-done.2, ...), custom_call_target="tpu_custom_call" | custom-call | tf_op jit(solution)/shard_map/pallas_call | solution.py:191
  185.3 8.5 %collective-permute-done.19.right_ref = f32[24,8,128]{2,1,0:T(8,128)S(1)} collective-permute-done((f32[24,8,128]{2,1,0:T(8,128)}, f32[24,8,128]{2,1,0:T(8,128)S(1)}, u32[]{:S(2)}, u32[]{:S(2)}) %collective-permute-start.19) | collective-permute-done | bytes 98336 | tf_op jit(solution)/shard_map/ppermute | solution.py:345
  194.5 4.6 %shard_map.70.own_ref = f32[24,8,128]{2,1,0:T(8,128)} custom-call(s32[2]{0:T(128)} %pad_add_fusion.1.depth_ref, f32[24,8,128]{2,1,0:T(8,128)} %copy-done.18, f32[24,8,128]{2,1,0:T(8,128)} %shard_map.69.own_ref, f32[24,8,128]{2,1,0:T(8,128)} %copy-done.22, f32[24,24,128]{2,1,0:T(8,128)} %copy-done.5, f32[24,24,128]{2,1,0:T(8,128)} %copy-done.2, ...), custom_call_target="tpu_custom_call" | custom-call | tf_op jit(solution)/shard_map/pallas_call | solution.py:191
  203.4 8.5 %collective-permute-done.21.right_ref = f32[24,8,128]{2,1,0:T(8,128)S(1)} collective-permute-done((f32[24,8,128]{2,1,0:T(8,128)}, f32[24,8,128]{2,1,0:T(8,128)S(1)}, u32[]{:S(2)}, u32[]{:S(2)}) %collective-permute-start.21) | collective-permute-done | bytes 98336 | tf_op jit(solution)/shard_map/ppermute | solution.py:345
  212.6 4.4 %shard_map.71 = f32[24,24,128]{2,1,0:T(8,128)} custom-call(s32[2]{0:T(128)} %pad_add_fusion.1.depth_ref, f32[24,8,128]{2,1,0:T(8,128)} %copy-done.9, f32[24,8,128]{2,1,0:T(8,128)} %shard_map.70.own_ref, f32[24,8,128]{2,1,0:T(8,128)} %copy-done.10, f32[24,24,128]{2,1,0:T(8,128)} %copy-done.5, f32[24,24,128]{2,1,0:T(8,128)} %copy-done.2, ...), custom_call_target="tpu_custom_call" | custom-call | tf_op jit(solution)/shard_map/pallas_call | solution.py:191
  223.9 5.2 %collective-permute-done.23 = f32[4,8,128]{2,1,0:T(8,128)S(1)} collective-permute-done((f32[4,8,128]{2,1,0:T(8,128)S(1)}, f32[4,8,128]{2,1,0:T(8,128)S(1)}, u32[]{:S(2)}, u32[]{:S(2)}) %collective-permute-start.23) | collective-permute-done | bytes 16416 | tf_op jit(solution)/shard_map/ppermute | solution.py:382
  (189 shorter events, 75.1 us)
Async XLA Ops:
  7.6 11.1 %collective-permute-start = (f32[3,5,8,128]{3,2,1,0:T(8,128)S(1)}, f32[3,5,8,128]{3,2,1,0:T(8,128)S(1)}, u32[]{:S(2)}, u32[]{:S(2)}) collective-permute-start(f32[3,5,8,128]{3,2,1,0:T(8,128)S(1)} %get-tuple-element.52), channel_id=1, source_target_pairs={{0,16},{16,32},{32,48},{48,64},{64,80},{80,96},{96,112},{112,128},... | collective-permute-start | bytes 184328 | tf_op jit(solution)/shard_map/ppermute | solution.py:213
  12.2 7.7 %collective-permute-start.1 = (f32[3,5,8,128]{3,2,1,0:T(8,128)S(1)}, f32[3,5,8,128]{3,2,1,0:T(8,128)S(1)}, u32[]{:S(2)}, u32[]{:S(2)}) collective-permute-start(f32[3,5,8,128]{3,2,1,0:T(8,128)S(1)} %get-tuple-element.53), channel_id=1, source_target_pairs={{16,0},{32,16},{48,32},{64,48},{80,64},{96,80},{112,96},{128,112},... | collective-permute-start | bytes 184328 | tf_op jit(solution)/shard_map/ppermute | solution.py:216
  19.9 16.3 %collective-permute-start.4 = (f32[3,26,1,128]{3,2,1,0:T(1,128)S(1)}, f32[3,26,1,128]{3,2,1,0:T(1,128)S(1)}, u32[]{:S(2)}, u32[]{:S(2)}) collective-permute-start(f32[3,26,1,128]{3,2,1,0:T(1,128)S(1)} %get-tuple-element.32), channel_id=1, source_target_pairs={{0,2},{1,3},{2,4},{3,5},{4,6},{5,7},{6,8},{7,9},{8,10},{9,11},{10,... | collective-permute-start | bytes 119816 | tf_op jit(solution)/shard_map/ppermute | solution.py:271
  22.0 23.9 %collective-permute-start.2 = (f32[3,26,8,128]{3,2,1,0:T(8,128)S(1)}, f32[3,26,8,128]{3,2,1,0:T(8,128)S(1)}, u32[]{:S(2)}, u32[]{:S(2)}) collective-permute-start(f32[3,26,8,128]{3,2,1,0:T(8,128)S(1)} %pad_maximum_fusion.3), channel_id=1, source_target_pairs={{0,1},{1,2},{2,3},{3,4},{4,5},{5,6},{6,7},{7,8},{8,9},{9,10},{10,1... | collective-permute-start | bytes 958472 | tf_op jit(solution)/shard_map/ppermute | solution.py:206
  32.4 16.9 %collective-permute-start.3 = (f32[3,26,8,128]{3,2,1,0:T(8,128)S(1)}, f32[3,26,8,128]{3,2,1,0:T(8,128)S(1)}, u32[]{:S(2)}, u32[]{:S(2)}) collective-permute-start(f32[3,26,8,128]{3,2,1,0:T(8,128)S(1)} %pad_maximum_fusion.3), channel_id=1, source_target_pairs={{1,0},{2,1},{3,2},{4,3},{5,4},{6,5},{7,6},{8,7},{9,8},{10,9},{11,1... | collective-permute-start | bytes 958472 | tf_op jit(solution)/shard_map/ppermute | solution.py:207
  34.3 11.5 %collective-permute-start.5 = (f32[3,26,1,128]{3,2,1,0:T(1,128)S(1)}, f32[3,26,1,128]{3,2,1,0:T(1,128)S(1)}, u32[]{:S(2)}, u32[]{:S(2)}) collective-permute-start(f32[3,26,1,128]{3,2,1,0:T(1,128)S(1)} %get-tuple-element.31), channel_id=1, source_target_pairs={{2,0},{3,1},{4,2},{5,3},{6,4},{7,5},{8,6},{9,7},{10,8},{11,9},{12,... | collective-permute-start | bytes 119816 | tf_op jit(solution)/shard_map/ppermute | solution.py:272
  67.7 7.1 %collective-permute-start.6 = (f32[24,8,128]{2,1,0:T(8,128)}, f32[24,8,128]{2,1,0:T(8,128)S(1)}, u32[]{:S(2)}, u32[]{:S(2)}) collective-permute-start(f32[24,8,128]{2,1,0:T(8,128)} %shard_map.64.own_ref), channel_id=1, source_target_pairs={{0,1},{1,2},{2,3},{3,4},{4,5},{5,6},{6,7},{7,8},{8,9},{9,10},{10,1... | collective-permute-start | bytes 294920 | tf_op jit(solution)/shard_map/ppermute | solution.py:343
  72.8 11.2 %collective-permute-start.7 = (f32[24,8,128]{2,1,0:T(8,128)}, f32[24,8,128]{2,1,0:T(8,128)S(1)}, u32[]{:S(2)}, u32[]{:S(2)}) collective-permute-start(f32[24,8,128]{2,1,0:T(8,128)} %shard_map.64.own_ref), channel_id=1, source_target_pairs={{1,0},{2,1},{3,2},{4,3},{5,4},{6,5},{7,6},{8,7},{9,8},{10,9},{11,1... | collective-permute-start | bytes 294920 | tf_op jit(solution)/shard_map/ppermute | solution.py:345
  89.3 5.1 %collective-permute-start.8 = (f32[24,8,128]{2,1,0:T(8,128)}, f32[24,8,128]{2,1,0:T(8,128)S(1)}, u32[]{:S(2)}, u32[]{:S(2)}) collective-permute-start(f32[24,8,128]{2,1,0:T(8,128)} %shard_map.65.own_ref), channel_id=1, source_target_pairs={{0,1},{1,2},{2,3},{3,4},{4,5},{5,6},{6,7},{7,8},{8,9},{9,10},{10,1... | collective-permute-start | bytes 294920 | tf_op jit(solution)/shard_map/ppermute | solution.py:343
  91.2 11.0 %collective-permute-start.9 = (f32[24,8,128]{2,1,0:T(8,128)}, f32[24,8,128]{2,1,0:T(8,128)S(1)}, u32[]{:S(2)}, u32[]{:S(2)}) collective-permute-start(f32[24,8,128]{2,1,0:T(8,128)} %shard_map.65.own_ref), channel_id=1, source_target_pairs={{1,0},{2,1},{3,2},{4,3},{5,4},{6,5},{7,6},{8,7},{9,8},{10,9},{11,1... | collective-permute-start | bytes 294920 | tf_op jit(solution)/shard_map/ppermute | solution.py:345
  107.3 5.0 %collective-permute-start.10 = (f32[24,8,128]{2,1,0:T(8,128)}, f32[24,8,128]{2,1,0:T(8,128)S(1)}, u32[]{:S(2)}, u32[]{:S(2)}) collective-permute-start(f32[24,8,128]{2,1,0:T(8,128)} %shard_map.66.own_ref), channel_id=1, source_target_pairs={{0,1},{1,2},{2,3},{3,4},{4,5},{5,6},{6,7},{7,8},{8,9},{9,10},{10,1... | collective-permute-start | bytes 294920 | tf_op jit(solution)/shard_map/ppermute | solution.py:343
  109.2 11.0 %collective-permute-start.11 = (f32[24,8,128]{2,1,0:T(8,128)}, f32[24,8,128]{2,1,0:T(8,128)S(1)}, u32[]{:S(2)}, u32[]{:S(2)}) collective-permute-start(f32[24,8,128]{2,1,0:T(8,128)} %shard_map.66.own_ref), channel_id=1, source_target_pairs={{1,0},{2,1},{3,2},{4,3},{5,4},{6,5},{7,6},{8,7},{9,8},{10,9},{11,1... | collective-permute-start | bytes 294920 | tf_op jit(solution)/shard_map/ppermute | solution.py:345
  126.3 7.1 %collective-permute-start.12 = (f32[9,24,128]{2,1,0:T(8,128)S(1)}, f32[9,24,128]{2,1,0:T(8,128)S(1)}, u32[]{:S(2)}, u32[]{:S(2)}) collective-permute-start(f32[9,24,128]{2,1,0:T(8,128)S(1)} %get-tuple-element.38), channel_id=1, source_target_pairs={{0,16},{16,32},{32,48},{48,64},{64,80},{80,96},{96,112},{112,128},... | collective-permute-start | bytes 331784 | tf_op jit(solution)/shard_map/ppermute | solution.py:364
  131.5 8.2 %collective-permute-start.13 = (f32[9,24,128]{2,1,0:T(8,128)S(1)}, f32[9,24,128]{2,1,0:T(8,128)S(1)}, u32[]{:S(2)}, u32[]{:S(2)}) collective-permute-start(f32[9,24,128]{2,1,0:T(8,128)S(1)} %get-tuple-element.39), channel_id=1, source_target_pairs={{16,0},{32,16},{48,32},{64,48},{80,64},{96,80},{112,96},{128,112},... | collective-permute-start | bytes 331784 | tf_op jit(solution)/shard_map/ppermute | solution.py:367
  142.7 6.1 %collective-permute-start.14 = (f32[24,8,128]{2,1,0:T(8,128)S(1)}, f32[24,8,128]{2,1,0:T(8,128)S(1)}, u32[]{:S(2)}, u32[]{:S(2)}) collective-permute-start(f32[24,8,128]{2,1,0:T(8,128)S(1)} %multiply_multiply_fusion.1.own_ref), channel_id=1, source_target_pairs={{0,1},{1,2},{2,3},{3,4},{4,5},{5,6},{6,7},{7,8},{8,9},{9,10},{10,1... | collective-permute-start | bytes 294920 | tf_op jit(solution)/shard_map/ppermute | solution.py:343
  146.9 10.7 %collective-permute-start.15 = (f32[24,8,128]{2,1,0:T(8,128)S(1)}, f32[24,8,128]{2,1,0:T(8,128)S(1)}, u32[]{:S(2)}, u32[]{:S(2)}) collective-permute-start(f32[24,8,128]{2,1,0:T(8,128)S(1)} %multiply_multiply_fusion.1.own_ref), channel_id=1, source_target_pairs={{1,0},{2,1},{3,2},{4,3},{5,4},{6,5},{7,6},{8,7},{9,8},{10,9},{11,1... | collective-permute-start | bytes 294920 | tf_op jit(solution)/shard_map/ppermute | solution.py:345
  162.9 4.3 %collective-permute-start.16 = (f32[24,8,128]{2,1,0:T(8,128)}, f32[24,8,128]{2,1,0:T(8,128)S(1)}, u32[]{:S(2)}, u32[]{:S(2)}) collective-permute-start(f32[24,8,128]{2,1,0:T(8,128)} %shard_map.68.own_ref), channel_id=1, source_target_pairs={{0,1},{1,2},{2,3},{3,4},{4,5},{5,6},{6,7},{7,8},{8,9},{9,10},{10,1... | collective-permute-start | bytes 294920 | tf_op jit(solution)/shard_map/ppermute | solution.py:343
  164.8 11.0 %collective-permute-start.17 = (f32[24,8,128]{2,1,0:T(8,128)}, f32[24,8,128]{2,1,0:T(8,128)S(1)}, u32[]{:S(2)}, u32[]{:S(2)}) collective-permute-start(f32[24,8,128]{2,1,0:T(8,128)} %shard_map.68.own_ref), channel_id=1, source_target_pairs={{1,0},{2,1},{3,2},{4,3},{5,4},{6,5},{7,6},{8,7},{9,8},{10,9},{11,1... | collective-permute-start | bytes 294920 | tf_op jit(solution)/shard_map/ppermute | solution.py:345
  180.9 4.3 %collective-permute-start.18 = (f32[24,8,128]{2,1,0:T(8,128)}, f32[24,8,128]{2,1,0:T(8,128)S(1)}, u32[]{:S(2)}, u32[]{:S(2)}) collective-permute-start(f32[24,8,128]{2,1,0:T(8,128)} %shard_map.69.own_ref), channel_id=1, source_target_pairs={{0,1},{1,2},{2,3},{3,4},{4,5},{5,6},{6,7},{7,8},{8,9},{9,10},{10,1... | collective-permute-start | bytes 294920 | tf_op jit(solution)/shard_map/ppermute | solution.py:343
  182.9 11.0 %collective-permute-start.19 = (f32[24,8,128]{2,1,0:T(8,128)}, f32[24,8,128]{2,1,0:T(8,128)S(1)}, u32[]{:S(2)}, u32[]{:S(2)}) collective-permute-start(f32[24,8,128]{2,1,0:T(8,128)} %shard_map.69.own_ref), channel_id=1, source_target_pairs={{1,0},{2,1},{3,2},{4,3},{5,4},{6,5},{7,6},{8,7},{9,8},{10,9},{11,1... | collective-permute-start | bytes 294920 | tf_op jit(solution)/shard_map/ppermute | solution.py:345
  199.0 4.3 %collective-permute-start.20 = (f32[24,8,128]{2,1,0:T(8,128)}, f32[24,8,128]{2,1,0:T(8,128)S(1)}, u32[]{:S(2)}, u32[]{:S(2)}) collective-permute-start(f32[24,8,128]{2,1,0:T(8,128)} %shard_map.70.own_ref), channel_id=1, source_target_pairs={{0,1},{1,2},{2,3},{3,4},{4,5},{5,6},{6,7},{7,8},{8,9},{9,10},{10,1... | collective-permute-start | bytes 294920 | tf_op jit(solution)/shard_map/ppermute | solution.py:343
  200.9 11.0 %collective-permute-start.21 = (f32[24,8,128]{2,1,0:T(8,128)}, f32[24,8,128]{2,1,0:T(8,128)S(1)}, u32[]{:S(2)}, u32[]{:S(2)}) collective-permute-start(f32[24,8,128]{2,1,0:T(8,128)} %shard_map.70.own_ref), channel_id=1, source_target_pairs={{1,0},{2,1},{3,2},{4,3},{5,4},{6,5},{7,6},{8,7},{9,8},{10,9},{11,1... | collective-permute-start | bytes 294920 | tf_op jit(solution)/shard_map/ppermute | solution.py:345
  218.0 5.9 %collective-permute-start.22 = (f32[4,8,128]{2,1,0:T(8,128)S(1)}, f32[4,8,128]{2,1,0:T(8,128)S(1)}, u32[]{:S(2)}, u32[]{:S(2)}) collective-permute-start(f32[4,8,128]{2,1,0:T(8,128)S(1)} %get-tuple-element.36), channel_id=1, source_target_pairs={{0,16},{16,32},{32,48},{48,64},{64,80},{80,96},{96,112},{112,128},... | collective-permute-start | bytes 49160 | tf_op jit(solution)/shard_map/ppermute | solution.py:379
  221.9 7.2 %collective-permute-start.23 = (f32[4,8,128]{2,1,0:T(8,128)S(1)}, f32[4,8,128]{2,1,0:T(8,128)S(1)}, u32[]{:S(2)}, u32[]{:S(2)}) collective-permute-start(f32[4,8,128]{2,1,0:T(8,128)S(1)} %get-tuple-element.37), channel_id=1, source_target_pairs={{16,0},{32,16},{48,32},{64,48},{80,64},{96,80},{112,96},{128,112},... | collective-permute-start | bytes 49160 | tf_op jit(solution)/shard_map/ppermute | solution.py:382
  (24 other events, 111.9 us)

commit v4 on v2

--- a/solution.py
+++ b/solution.py
@@ -184,7 +184,8 @@
 
 def round_call(weight_now, weight_next, last, depths, pieces, target, coeffs, fy, fz, fx):
     tile_cols = pieces[1].shape[1]
-    own_cols = slice(tile_cols, 2 * tile_cols)
+    ghost = pieces[0].shape[1]
+    own_cols = slice(ghost, ghost + tile_cols)
     shape = target.shape
     out_shape = shape if last else pieces[1].shape
     vmem = pl.BlockSpec(memory_space=pltpu.VMEM)
@@ -325,22 +326,24 @@
         target = residual * active
         estimate_own = relax_weight(0) * solve_lines(factors_x, target[:, own])
         for round_index in range(ROUNDS):
+            last = round_index + 1 == ROUNDS
+            ghost = tile_cols if (last and outer_turn + 1 < OUTER) else tile_cols // 2
+            window = slice(tile_cols - ghost, 2 * tile_cols + ghost)
             pieces = (
-                lax.ppermute(estimate_own, "grp", grp_pairs("grp", 1)),
+                lax.ppermute(estimate_own[:, tile_cols - ghost :], "grp", grp_pairs("grp", 1)),
                 estimate_own,
-                lax.ppermute(estimate_own, "grp", grp_pairs("grp", -1)),
-            )
-            last = round_index + 1 == ROUNDS
+                lax.ppermute(estimate_own[:, :ghost], "grp", grp_pairs("grp", -1)),
+            )
             estimate = round_call(
                 relax_weight(round_index),
                 0.0 if last else relax_weight(round_index + 1),
                 last,
                 depths,
                 pieces,
-                target,
-                coeffs,
-                factors_y,
-                factors_z,
+                target[:, window],
+                tuple(member[:, window] for member in coeffs),
+                tuple(member[:, window] for member in factors_y[:2]),
+                tuple(member[:, window] for member in factors_z[:2]),
                 factors_x,
             )
             estimate_own = estimate
@@ -361,7 +364,7 @@
                 + jnp.concatenate([filler, from_above], axis=0)
             )
         else:
-            own_corr = correction[:, own]
+            own_corr = correction[:, ghost : ghost + tile_cols]
             from_below = lax.ppermute(
                 own_corr[margin_rows - OV :], "sub", grp_pairs("sub", 1)
             )

time: 228 us -> 231 us (1.013)
  local copies, waits for them, and re-layouts: 11.9 us -> 25.7 us
  waiting for transfers between devices: 89.7 us -> 82.8 us
  other arithmetic: 21 us -> 18.6 us
    slice x0 -> x17, local copies, waits for them, and re-layouts: none -> 12.3 us  [the longest x8 5.88 us: on_device(): member[:, window]]
    ppermute x16, waiting for transfers between devices: 61.5 us -> 56.1 us  [the longest x8 56 us: on_device(): lax.ppermute(estimate_own[:, :ghost], 'grp', grp_pairs('grp', -1))]
    unnamed x58 -> x66, local copies, waits for them, and re-layouts: 8.31 us -> 9.86 us
  transfers between devices with their start and end apart: 24 -> 24, of which waited for: 14 -> 13; matrix products, arithmetic and copies ran while one was open for 4% -> 4% of each run, Pallas kernels for 0% -> 0%
where the time goes in v4:
time: 231 us; the launch traced here: 229 us
  waiting for transfers between devices  82.8 us (36%)
  starting transfers between devices  64.3 us (28%)
  Pallas kernels  35.2 us (15%)
  local copies, waits for them, and re-layouts  25.7 us (11%)
  other arithmetic  18.6 us (8%)
  between operations  2.8 us (1%)
    ppermute x8, waiting for transfers between devices, on_device(): lax.ppermute(estimate_own[:, :ghost], 'grp', grp_pairs('grp', -1))  56 us
    pallas_call x8, Pallas kernels, round_call(): pl.pallas_call(make_round_kernel(weight_now, weight_next, last, own_cols)...  35.2 us
    ppermute x8, starting transfers between devices, on_device(): lax.ppermute(estimate_own[:, tile_cols - ghost:], 'grp', grp_pairs('grp',...  21.2 us
    ppermute x8, starting transfers between devices, on_device(): lax.ppermute(estimate_own[:, :ghost], 'grp', grp_pairs('grp', -1))  18.5 us
    ppermute x1, waiting for transfers between devices, with_sides(): from_right = lax.ppermute(value, axis, grp_pairs(axis, -1))  10.8 us
    unnamed x66, local copies, waits for them, and re-layouts  9.86 us
    ppermute x1, waiting for transfers between devices, on_device(): from_above = lax.ppermute(correction[:span], 'sub', grp_pairs('sub', -1))  6.25 us
    another operation x1, other arithmetic, on_device(): stacked = jnp.stack([perm_local, pressure_start, source])  5.96 us
  transfers between devices with their start and end apart: 24, of which 13 were waited for; matrix products, arithmetic and copies ran while one was open for 4% of the time, Pallas kernels for 0%

profile of v4, /device:TPU:225, one launch (start us, length us, event | category | flops | bytes accessed | tf_op | source)
XLA Modules:
  0.0 229.4 jit_solution(1129889455113019855)
XLA Ops:
  1.6 6.0 %multiply_bitcast_fusion = f32[1,16,8,128]{3,2,1,0:T(8,128)S(1)} fusion(f32[16,8,128]{2,1,0:T(8,128)} %param.8, s32[16,8,128]{2,1,0:T(8,128)} %param.6, f32[]{:T(128)} %bitcast.7, f32[]{:T(128)} %bitcast.6, f32[]{:T(128)} %bitcast.5, f32[]{:T(128)} %bitcast.4, f32[]{:T(128)} %bitcast.3, f32[]{:T(128)} %bitcast.2, f32[]{:T(128)} %bitcast.1, f32[]{:T(128)} %bitcast), kind=kLoop, calls=%fused_computation.198 | loop fusion | flops 393216 | bytes 196640 | tf_op jit(solution)/shard_map/stack | solution.py:270
  7.6 4.5 %collective-permute-start = (f32[3,5,8,128]{3,2,1,0:T(8,128)S(1)}, f32[3,5,8,128]{3,2,1,0:T(8,128)S(1)}, u32[]{:S(2)}, u32[]{:S(2)}) collective-permute-start(f32[3,5,8,128]{3,2,1,0:T(8,128)S(1)} %get-tuple-element.47), channel_id=1, source_target_pairs={{0,16},{16,32},{32,48},{48,64},{64,80},{80,96},{96,112},{112,128},... | collective-permute-start | bytes 184328 | tf_op jit(solution)/shard_map/ppermute | solution.py:214
  30.5 10.8 %collective-permute-done.3 = f32[3,26,8,128]{3,2,1,0:T(8,128)S(1)} collective-permute-done((f32[3,26,8,128]{3,2,1,0:T(8,128)S(1)}, f32[3,26,8,128]{3,2,1,0:T(8,128)S(1)}, u32[]{:S(2)}, u32[]{:S(2)}) %collective-permute-start.3) | collective-permute-done | bytes 319520 | tf_op jit(solution)/shard_map/ppermute | solution.py:208
  63.8 4.5 %shard_map.64.own_ref = f32[24,8,128]{2,1,0:T(8,128)} custom-call(s32[2]{0:T(128)} %pad_add_fusion.1.depth_ref, f32[24,4,128]{2,1,0:T(4,128)} %copy-done.19, f32[24,8,128]{2,1,0:T(8,128)} %copy-done.12, f32[24,4,128]{2,1,0:T(4,128)} %copy-done.21, f32[24,16,128]{2,1,0:T(8,128)} %slice.722.t_ref, f32[24,16,128]{2,1,0:T(8,128)} %slice.723.d_ref, ...), custom_call_target="tpu_custom_call" | custom-call | tf_op jit(solution)/shard_map/pallas_call | solution.py:192
  69.2 5.2 %collective-permute-start.6 = (f32[24,4,128]{2,1,0:T(4,128)S(1)}, f32[24,4,128]{2,1,0:T(4,128)S(1)}, u32[]{:S(2)}, u32[]{:S(2)}) collective-permute-start(f32[24,4,128]{2,1,0:T(4,128)S(1)} %get-tuple-element.60), channel_id=1, source_target_pairs={{0,1},{1,2},{2,3},{3,4},{4,5},{5,6},{6,7},{7,8},{8,9},{9,10},{10,1... | collective-permute-start | bytes 147464 | tf_op jit(solution)/shard_map/ppermute | solution.py:333
  77.0 7.6 %collective-permute-done.7.right_ref = f32[24,4,128]{2,1,0:T(4,128)S(1)} collective-permute-done((f32[24,4,128]{2,1,0:T(4,128)S(1)}, f32[24,4,128]{2,1,0:T(4,128)S(1)}, u32[]{:S(2)}, u32[]{:S(2)}) %collective-permute-start.7) | collective-permute-done | bytes 49184 | tf_op jit(solution)/shard_map/ppermute | solution.py:335
  85.3 4.5 %shard_map.65.own_ref = f32[24,8,128]{2,1,0:T(8,128)} custom-call(s32[2]{0:T(128)} %pad_add_fusion.1.depth_ref, f32[24,4,128]{2,1,0:T(4,128)} %copy-done.23, f32[24,8,128]{2,1,0:T(8,128)} %shard_map.64.own_ref, f32[24,4,128]{2,1,0:T(4,128)} %copy-done.28, f32[24,16,128]{2,1,0:T(8,128)} %slice.722.t_ref, f32[24,16,128]{2,1,0:T(8,128)} %slice.723.d_ref, ...), custom_call_target="tpu_custom_call" | custom-call | tf_op jit(solution)/shard_map/pallas_call | solution.py:192
  95.9 7.0 %collective-permute-done.9.right_ref = f32[24,4,128]{2,1,0:T(4,128)S(1)} collective-permute-done((f32[24,4,128]{2,1,0:T(4,128)S(1)}, f32[24,4,128]{2,1,0:T(4,128)S(1)}, u32[]{:S(2)}, u32[]{:S(2)}) %collective-permute-start.9) | collective-permute-done | bytes 49184 | tf_op jit(solution)/shard_map/ppermute | solution.py:335
  103.5 4.5 %shard_map.66.own_ref = f32[24,8,128]{2,1,0:T(8,128)} custom-call(s32[2]{0:T(128)} %pad_add_fusion.1.depth_ref, f32[24,4,128]{2,1,0:T(4,128)} %copy-done.22, f32[24,8,128]{2,1,0:T(8,128)} %shard_map.65.own_ref, f32[24,4,128]{2,1,0:T(4,128)} %copy-done.24, f32[24,16,128]{2,1,0:T(8,128)} %slice.722.t_ref, f32[24,16,128]{2,1,0:T(8,128)} %slice.723.d_ref, ...), custom_call_target="tpu_custom_call" | custom-call | tf_op jit(solution)/shard_map/pallas_call | solution.py:192
  113.2 7.7 %collective-permute-done.11.right_ref = f32[24,8,128]{2,1,0:T(8,128)S(1)} collective-permute-done((f32[24,8,128]{2,1,0:T(8,128)}, f32[24,8,128]{2,1,0:T(8,128)S(1)}, u32[]{:S(2)}, u32[]{:S(2)}) %collective-permute-start.11) | collective-permute-done | bytes 98336 | tf_op jit(solution)/shard_map/ppermute | solution.py:335
  121.5 4.4 %shard_map.67 = f32[24,24,128]{2,1,0:T(8,128)} custom-call(s32[2]{0:T(128)} %pad_add_fusion.1.depth_ref, f32[24,8,128]{2,1,0:T(8,128)} %copy-done.16, f32[24,8,128]{2,1,0:T(8,128)} %shard_map.66.own_ref, f32[24,8,128]{2,1,0:T(8,128)} %copy-done.17, f32[24,24,128]{2,1,0:T(8,128)} %copy-done.6, f32[24,24,128]{2,1,0:T(8,128)} %copy-done.4, ...), custom_call_target="tpu_custom_call" | custom-call | tf_op jit(solution)/shard_map/pallas_call | solution.py:192
  127.0 5.1 %collective-permute-start.12 = (f32[9,24,128]{2,1,0:T(8,128)S(1)}, f32[9,24,128]{2,1,0:T(8,128)S(1)}, u32[]{:S(2)}, u32[]{:S(2)}) collective-permute-start(f32[9,24,128]{2,1,0:T(8,128)S(1)} %get-tuple-element.29), channel_id=1, source_target_pairs={{0,16},{16,32},{32,48},{48,64},{64,80},{80,96},{96,112},{112,128},... | collective-permute-start | bytes 331784 | tf_op jit(solution)/shard_map/ppermute | solution.py:353
  134.0 6.3 %collective-permute-done.13 = f32[9,24,128]{2,1,0:T(8,128)S(1)} collective-permute-done((f32[9,24,128]{2,1,0:T(8,128)S(1)}, f32[9,24,128]{2,1,0:T(8,128)S(1)}, u32[]{:S(2)}, u32[]{:S(2)}) %collective-permute-start.13) | collective-permute-done | bytes 110624 | tf_op jit(solution)/shard_map/ppermute | solution.py:356
  144.7 4.5 %collective-permute-start.14 = (f32[24,4,128]{2,1,0:T(4,128)S(1)}, f32[24,4,128]{2,1,0:T(4,128)S(1)}, u32[]{:S(2)}, u32[]{:S(2)}) collective-permute-start(f32[24,4,128]{2,1,0:T(4,128)S(1)} %get-tuple-element.56), channel_id=1, source_target_pairs={{0,1},{1,2},{2,3},{3,4},{4,5},{5,6},{6,7},{7,8},{8,9},{9,10},{10,1... | collective-permute-start | bytes 147464 | tf_op jit(solution)/shard_map/ppermute | solution.py:333
  151.9 7.6 %collective-permute-done.15.right_ref = f32[24,4,128]{2,1,0:T(4,128)S(1)} collective-permute-done((f32[24,4,128]{2,1,0:T(4,128)S(1)}, f32[24,4,128]{2,1,0:T(4,128)S(1)}, u32[]{:S(2)}, u32[]{:S(2)}) %collective-permute-start.15) | collective-permute-done | bytes 49184 | tf_op jit(solution)/shard_map/ppermute | solution.py:335
  160.0 4.5 %shard_map.68.own_ref = f32[24,8,128]{2,1,0:T(8,128)} custom-call(s32[2]{0:T(128)} %pad_add_fusion.1.depth_ref, f32[24,4,128]{2,1,0:T(4,128)} %copy-done.25, f32[24,8,128]{2,1,0:T(8,128)} %copy-done.13, f32[24,4,128]{2,1,0:T(4,128)} %copy-done.29, f32[24,16,128]{2,1,0:T(8,128)} %slice.815.t_ref, f32[24,16,128]{2,1,0:T(8,128)} %slice.723.d_ref, ...), custom_call_target="tpu_custom_call" | custom-call | tf_op jit(solution)/shard_map/pallas_call | solution.py:192
  169.9 7.8 %collective-permute-done.17.right_ref = f32[24,4,128]{2,1,0:T(4,128)S(1)} collective-permute-done((f32[24,4,128]{2,1,0:T(4,128)S(1)}, f32[24,4,128]{2,1,0:T(4,128)S(1)}, u32[]{:S(2)}, u32[]{:S(2)}) %collective-permute-start.17) | collective-permute-done | bytes 49184 | tf_op jit(solution)/shard_map/ppermute | solution.py:335
  178.3 4.5 %shard_map.69.own_ref = f32[24,8,128]{2,1,0:T(8,128)} custom-call(s32[2]{0:T(128)} %pad_add_fusion.1.depth_ref, f32[24,4,128]{2,1,0:T(4,128)} %copy-done.26, f32[24,8,128]{2,1,0:T(8,128)} %shard_map.68.own_ref, f32[24,4,128]{2,1,0:T(4,128)} %copy-done.30, f32[24,16,128]{2,1,0:T(8,128)} %slice.815.t_ref, f32[24,16,128]{2,1,0:T(8,128)} %slice.723.d_ref, ...), custom_call_target="tpu_custom_call" | custom-call | tf_op jit(solution)/shard_map/pallas_call | solution.py:192
  188.1 7.8 %collective-permute-done.19.right_ref = f32[24,4,128]{2,1,0:T(4,128)S(1)} collective-permute-done((f32[24,4,128]{2,1,0:T(4,128)S(1)}, f32[24,4,128]{2,1,0:T(4,128)S(1)}, u32[]{:S(2)}, u32[]{:S(2)}) %collective-permute-start.19) | collective-permute-done | bytes 49184 | tf_op jit(solution)/shard_map/ppermute | solution.py:335
  196.5 4.5 %shard_map.70.own_ref = f32[24,8,128]{2,1,0:T(8,128)} custom-call(s32[2]{0:T(128)} %pad_add_fusion.1.depth_ref, f32[24,4,128]{2,1,0:T(4,128)} %copy-done.27, f32[24,8,128]{2,1,0:T(8,128)} %shard_map.69.own_ref, f32[24,4,128]{2,1,0:T(4,128)} %copy-done.31, f32[24,16,128]{2,1,0:T(8,128)} %slice.815.t_ref, f32[24,16,128]{2,1,0:T(8,128)} %slice.723.d_ref, ...), custom_call_target="tpu_custom_call" | custom-call | tf_op jit(solution)/shard_map/pallas_call | solution.py:192
  206.3 7.8 %collective-permute-done.21.right_ref = f32[24,4,128]{2,1,0:T(4,128)S(1)} collective-permute-done((f32[24,4,128]{2,1,0:T(4,128)S(1)}, f32[24,4,128]{2,1,0:T(4,128)S(1)}, u32[]{:S(2)}, u32[]{:S(2)}) %collective-permute-start.21) | collective-permute-done | bytes 49184 | tf_op jit(solution)/shard_map/ppermute | solution.py:335
  214.7 3.9 %shard_map.71 = f32[24,16,128]{2,1,0:T(8,128)} custom-call(s32[2]{0:T(128)} %pad_add_fusion.1.depth_ref, f32[24,4,128]{2,1,0:T(4,128)} %copy-done.18, f32[24,8,128]{2,1,0:T(8,128)} %shard_map.70.own_ref, f32[24,4,128]{2,1,0:T(4,128)} %copy-done.20, f32[24,16,128]{2,1,0:T(8,128)} %slice.815.t_ref, f32[24,16,128]{2,1,0:T(8,128)} %slice.723.d_ref, ...), custom_call_target="tpu_custom_call" | custom-call | tf_op jit(solution)/shard_map/pallas_call | solution.py:192
  221.6 3.4 %collective-permute-start.23 = (f32[4,8,128]{2,1,0:T(8,128)S(1)}, f32[4,8,128]{2,1,0:T(8,128)S(1)}, u32[]{:S(2)}, u32[]{:S(2)}) collective-permute-start(f32[4,8,128]{2,1,0:T(8,128)S(1)} %get-tuple-element.46), channel_id=1, source_target_pairs={{16,0},{32,16},{48,32},{64,48},{80,64},{96,80},{112,96},{128,112},... | collective-permute-start | bytes 49160 | tf_op jit(solution)/shard_map/ppermute | solution.py:371
  224.9 3.8 %collective-permute-done.23 = f32[4,8,128]{2,1,0:T(8,128)S(1)} collective-permute-done((f32[4,8,128]{2,1,0:T(8,128)S(1)}, f32[4,8,128]{2,1,0:T(8,128)S(1)}, u32[]{:S(2)}, u32[]{:S(2)}) %collective-permute-start.23) | collective-permute-done | bytes 16416 | tf_op jit(solution)/shard_map/ppermute | solution.py:371
  (216 shorter events, 88.6 us)
Async XLA Ops:
  7.6 9.3 %collective-permute-start = (f32[3,5,8,128]{3,2,1,0:T(8,128)S(1)}, f32[3,5,8,128]{3,2,1,0:T(8,128)S(1)}, u32[]{:S(2)}, u32[]{:S(2)}) collective-permute-start(f32[3,5,8,128]{3,2,1,0:T(8,128)S(1)} %get-tuple-element.47), channel_id=1, source_target_pairs={{0,16},{16,32},{32,48},{48,64},{64,80},{80,96},{96,112},{112,128},... | collective-permute-start | bytes 184328 | tf_op jit(solution)/shard_map/ppermute | solution.py:214
  12.2 7.7 %collective-permute-start.1 = (f32[3,5,8,128]{3,2,1,0:T(8,128)S(1)}, f32[3,5,8,128]{3,2,1,0:T(8,128)S(1)}, u32[]{:S(2)}, u32[]{:S(2)}) collective-permute-start(f32[3,5,8,128]{3,2,1,0:T(8,128)S(1)} %get-tuple-element.48), channel_id=1, source_target_pairs={{16,0},{32,16},{48,32},{64,48},{80,64},{96,80},{112,96},{128,112},... | collective-permute-start | bytes 184328 | tf_op jit(solution)/shard_map/ppermute | solution.py:217
  19.9 10.6 %collective-permute-start.2 = (f32[3,26,8,128]{3,2,1,0:T(8,128)S(1)}, f32[3,26,8,128]{3,2,1,0:T(8,128)S(1)}, u32[]{:S(2)}, u32[]{:S(2)}) collective-permute-start(f32[3,26,8,128]{3,2,1,0:T(8,128)S(1)} %pad_maximum_fusion.1), channel_id=1, source_target_pairs={{0,1},{1,2},{2,3},{3,4},{4,5},{5,6},{6,7},{7,8},{8,9},{9,10},{10,1... | collective-permute-start | bytes 958472 | tf_op jit(solution)/shard_map/ppermute | solution.py:207
  23.2 18.2 %collective-permute-start.3 = (f32[3,26,8,128]{3,2,1,0:T(8,128)S(1)}, f32[3,26,8,128]{3,2,1,0:T(8,128)S(1)}, u32[]{:S(2)}, u32[]{:S(2)}) collective-permute-start(f32[3,26,8,128]{3,2,1,0:T(8,128)S(1)} %pad_maximum_fusion.1), channel_id=1, source_target_pairs={{1,0},{2,1},{3,2},{4,3},{5,4},{6,5},{7,6},{8,7},{9,8},{10,9},{11,1... | collective-permute-start | bytes 958472 | tf_op jit(solution)/shard_map/ppermute | solution.py:208
  51.0 9.4 %collective-permute-start.4 = (f32[24,4,128]{2,1,0:T(4,128)S(1)}, f32[24,4,128]{2,1,0:T(4,128)S(1)}, u32[]{:S(2)}, u32[]{:S(2)}) collective-permute-start(f32[24,4,128]{2,1,0:T(4,128)S(1)} %get-tuple-element.62), channel_id=1, source_target_pairs={{0,1},{1,2},{2,3},{3,4},{4,5},{5,6},{6,7},{7,8},{8,9},{9,10},{10,1... | collective-permute-start | bytes 147464 | tf_op jit(solution)/shard_map/ppermute | solution.py:333
  52.9 10.2 %collective-permute-start.5 = (f32[24,4,128]{2,1,0:T(4,128)S(1)}, f32[24,4,128]{2,1,0:T(4,128)S(1)}, u32[]{:S(2)}, u32[]{:S(2)}) collective-permute-start(f32[24,4,128]{2,1,0:T(4,128)S(1)} %get-tuple-element.61), channel_id=1, source_target_pairs={{1,0},{2,1},{3,2},{4,3},{5,4},{6,5},{7,6},{8,7},{9,8},{10,9},{11,1... | collective-permute-start | bytes 147464 | tf_op jit(solution)/shard_map/ppermute | solution.py:335
  69.2 7.8 %collective-permute-start.6 = (f32[24,4,128]{2,1,0:T(4,128)S(1)}, f32[24,4,128]{2,1,0:T(4,128)S(1)}, u32[]{:S(2)}, u32[]{:S(2)}) collective-permute-start(f32[24,4,128]{2,1,0:T(4,128)S(1)} %get-tuple-element.60), channel_id=1, source_target_pairs={{0,1},{1,2},{2,3},{3,4},{4,5},{5,6},{6,7},{7,8},{8,9},{9,10},{10,1... | collective-permute-start | bytes 147464 | tf_op jit(solution)/shard_map/ppermute | solution.py:333
  74.5 10.2 %collective-permute-start.7 = (f32[24,4,128]{2,1,0:T(4,128)S(1)}, f32[24,4,128]{2,1,0:T(4,128)S(1)}, u32[]{:S(2)}, u32[]{:S(2)}) collective-permute-start(f32[24,4,128]{2,1,0:T(4,128)S(1)} %get-tuple-element.59), channel_id=1, source_target_pairs={{1,0},{2,1},{3,2},{4,3},{5,4},{6,5},{7,6},{8,7},{9,8},{10,9},{11,1... | collective-permute-start | bytes 147464 | tf_op jit(solution)/shard_map/ppermute | solution.py:335
  90.8 5.1 %collective-permute-start.8 = (f32[24,4,128]{2,1,0:T(4,128)S(1)}, f32[24,4,128]{2,1,0:T(4,128)S(1)}, u32[]{:S(2)}, u32[]{:S(2)}) collective-permute-start(f32[24,4,128]{2,1,0:T(4,128)S(1)} %get-tuple-element.58), channel_id=1, source_target_pairs={{0,1},{1,2},{2,3},{3,4},{4,5},{5,6},{6,7},{7,8},{8,9},{9,10},{10,1... | collective-permute-start | bytes 147464 | tf_op jit(solution)/shard_map/ppermute | solution.py:333
  92.7 10.2 %collective-permute-start.9 = (f32[24,4,128]{2,1,0:T(4,128)S(1)}, f32[24,4,128]{2,1,0:T(4,128)S(1)}, u32[]{:S(2)}, u32[]{:S(2)}) collective-permute-start(f32[24,4,128]{2,1,0:T(4,128)S(1)} %get-tuple-element.57), channel_id=1, source_target_pairs={{1,0},{2,1},{3,2},{4,3},{5,4},{6,5},{7,6},{8,7},{9,8},{10,9},{11,1... | collective-permute-start | bytes 147464 | tf_op jit(solution)/shard_map/ppermute | solution.py:335
  108.0 5.2 %collective-permute-start.10 = (f32[24,8,128]{2,1,0:T(8,128)}, f32[24,8,128]{2,1,0:T(8,128)S(1)}, u32[]{:S(2)}, u32[]{:S(2)}) collective-permute-start(f32[24,8,128]{2,1,0:T(8,128)} %shard_map.66.own_ref), channel_id=1, source_target_pairs={{0,1},{1,2},{2,3},{3,4},{4,5},{5,6},{6,7},{7,8},{8,9},{9,10},{10,1... | collective-permute-start | bytes 294920 | tf_op jit(solution)/shard_map/ppermute | solution.py:333
  109.9 11.0 %collective-permute-start.11 = (f32[24,8,128]{2,1,0:T(8,128)}, f32[24,8,128]{2,1,0:T(8,128)S(1)}, u32[]{:S(2)}, u32[]{:S(2)}) collective-permute-start(f32[24,8,128]{2,1,0:T(8,128)} %shard_map.66.own_ref), channel_id=1, source_target_pairs={{1,0},{2,1},{3,2},{4,3},{5,4},{6,5},{7,6},{8,7},{9,8},{10,9},{11,1... | collective-permute-start | bytes 294920 | tf_op jit(solution)/shard_map/ppermute | solution.py:335
  127.0 7.0 %collective-permute-start.12 = (f32[9,24,128]{2,1,0:T(8,128)S(1)}, f32[9,24,128]{2,1,0:T(8,128)S(1)}, u32[]{:S(2)}, u32[]{:S(2)}) collective-permute-start(f32[9,24,128]{2,1,0:T(8,128)S(1)} %get-tuple-element.29), channel_id=1, source_target_pairs={{0,16},{16,32},{32,48},{48,64},{64,80},{80,96},{96,112},{112,128},... | collective-permute-start | bytes 331784 | tf_op jit(solution)/shard_map/ppermute | solution.py:353
  132.1 8.2 %collective-permute-start.13 = (f32[9,24,128]{2,1,0:T(8,128)S(1)}, f32[9,24,128]{2,1,0:T(8,128)S(1)}, u32[]{:S(2)}, u32[]{:S(2)}) collective-permute-start(f32[9,24,128]{2,1,0:T(8,128)S(1)} %get-tuple-element.30), channel_id=1, source_target_pairs={{16,0},{32,16},{48,32},{64,48},{80,64},{96,80},{112,96},{128,112},... | collective-permute-start | bytes 331784 | tf_op jit(solution)/shard_map/ppermute | solution.py:356
  144.7 7.2 %collective-permute-start.14 = (f32[24,4,128]{2,1,0:T(4,128)S(1)}, f32[24,4,128]{2,1,0:T(4,128)S(1)}, u32[]{:S(2)}, u32[]{:S(2)}) collective-permute-start(f32[24,4,128]{2,1,0:T(4,128)S(1)} %get-tuple-element.56), channel_id=1, source_target_pairs={{0,1},{1,2},{2,3},{3,4},{4,5},{5,6},{6,7},{7,8},{8,9},{9,10},{10,1... | collective-permute-start | bytes 147464 | tf_op jit(solution)/shard_map/ppermute | solution.py:333
  149.2 10.2 %collective-permute-start.15 = (f32[24,4,128]{2,1,0:T(4,128)S(1)}, f32[24,4,128]{2,1,0:T(4,128)S(1)}, u32[]{:S(2)}, u32[]{:S(2)}) collective-permute-start(f32[24,4,128]{2,1,0:T(4,128)S(1)} %get-tuple-element.55), channel_id=1, source_target_pairs={{1,0},{2,1},{3,2},{4,3},{5,4},{6,5},{7,6},{8,7},{9,8},{10,9},{11,1... | collective-permute-start | bytes 147464 | tf_op jit(solution)/shard_map/ppermute | solution.py:335
  165.5 4.3 %collective-permute-start.16 = (f32[24,4,128]{2,1,0:T(4,128)S(1)}, f32[24,4,128]{2,1,0:T(4,128)S(1)}, u32[]{:S(2)}, u32[]{:S(2)}) collective-permute-start(f32[24,4,128]{2,1,0:T(4,128)S(1)} %get-tuple-element.54), channel_id=1, source_target_pairs={{0,1},{1,2},{2,3},{3,4},{4,5},{5,6},{6,7},{7,8},{8,9},{9,10},{10,1... | collective-permute-start | bytes 147464 | tf_op jit(solution)/shard_map/ppermute | solution.py:333
  167.4 10.2 %collective-permute-start.17 = (f32[24,4,128]{2,1,0:T(4,128)S(1)}, f32[24,4,128]{2,1,0:T(4,128)S(1)}, u32[]{:S(2)}, u32[]{:S(2)}) collective-permute-start(f32[24,4,128]{2,1,0:T(4,128)S(1)} %get-tuple-element.53), channel_id=1, source_target_pairs={{1,0},{2,1},{3,2},{4,3},{5,4},{6,5},{7,6},{8,7},{9,8},{10,9},{11,1... | collective-permute-start | bytes 147464 | tf_op jit(solution)/shard_map/ppermute | solution.py:335
  183.7 4.3 %collective-permute-start.18 = (f32[24,4,128]{2,1,0:T(4,128)S(1)}, f32[24,4,128]{2,1,0:T(4,128)S(1)}, u32[]{:S(2)}, u32[]{:S(2)}) collective-permute-start(f32[24,4,128]{2,1,0:T(4,128)S(1)} %get-tuple-element.52), channel_id=1, source_target_pairs={{0,1},{1,2},{2,3},{3,4},{4,5},{5,6},{6,7},{7,8},{8,9},{9,10},{10,1... | collective-permute-start | bytes 147464 | tf_op jit(solution)/shard_map/ppermute | solution.py:333
  185.7 10.2 %collective-permute-start.19 = (f32[24,4,128]{2,1,0:T(4,128)S(1)}, f32[24,4,128]{2,1,0:T(4,128)S(1)}, u32[]{:S(2)}, u32[]{:S(2)}) collective-permute-start(f32[24,4,128]{2,1,0:T(4,128)S(1)} %get-tuple-element.51), channel_id=1, source_target_pairs={{1,0},{2,1},{3,2},{4,3},{5,4},{6,5},{7,6},{8,7},{9,8},{10,9},{11,1... | collective-permute-start | bytes 147464 | tf_op jit(solution)/shard_map/ppermute | solution.py:335
  202.0 4.3 %collective-permute-start.20 = (f32[24,4,128]{2,1,0:T(4,128)S(1)}, f32[24,4,128]{2,1,0:T(4,128)S(1)}, u32[]{:S(2)}, u32[]{:S(2)}) collective-permute-start(f32[24,4,128]{2,1,0:T(4,128)S(1)} %get-tuple-element.50), channel_id=1, source_target_pairs={{0,1},{1,2},{2,3},{3,4},{4,5},{5,6},{6,7},{7,8},{8,9},{9,10},{10,1... | collective-permute-start | bytes 147464 | tf_op jit(solution)/shard_map/ppermute | solution.py:333
  203.9 10.2 %collective-permute-start.21 = (f32[24,4,128]{2,1,0:T(4,128)S(1)}, f32[24,4,128]{2,1,0:T(4,128)S(1)}, u32[]{:S(2)}, u32[]{:S(2)}) collective-permute-start(f32[24,4,128]{2,1,0:T(4,128)S(1)} %get-tuple-element.49), channel_id=1, source_target_pairs={{1,0},{2,1},{3,2},{4,3},{5,4},{6,5},{7,6},{8,7},{9,8},{10,9},{11,1... | collective-permute-start | bytes 147464 | tf_op jit(solution)/shard_map/ppermute | solution.py:335
  219.6 5.3 %collective-permute-start.22 = (f32[4,8,128]{2,1,0:T(8,128)S(1)}, f32[4,8,128]{2,1,0:T(8,128)S(1)}, u32[]{:S(2)}, u32[]{:S(2)}) collective-permute-start(f32[4,8,128]{2,1,0:T(8,128)S(1)} %get-tuple-element.45), channel_id=1, source_target_pairs={{0,16},{16,32},{32,48},{48,64},{64,80},{80,96},{96,112},{112,128},... | collective-permute-start | bytes 49160 | tf_op jit(solution)/shard_map/ppermute | solution.py:368
  221.6 7.2 %collective-permute-start.23 = (f32[4,8,128]{2,1,0:T(8,128)S(1)}, f32[4,8,128]{2,1,0:T(8,128)S(1)}, u32[]{:S(2)}, u32[]{:S(2)}) collective-permute-start(f32[4,8,128]{2,1,0:T(8,128)S(1)} %get-tuple-element.46), channel_id=1, source_target_pairs={{16,0},{32,16},{48,32},{64,48},{80,64},{96,80},{112,96},{128,112},... | collective-permute-start | bytes 49160 | tf_op jit(solution)/shard_map/ppermute | solution.py:371
  (33 other events, 150.9 us)

commit v5 on v2

--- a/solution.py
+++ b/solution.py
@@ -261,10 +261,9 @@
 def on_device(facies, facies_perm, perm_scale, source, pressure_start, intersection_depth):
     slab_rows, tile_cols, line_cells = source.shape
     margin_rows = slab_rows + 2 * OV
-    perm_local = jnp.zeros(source.shape, jnp.float32)
-    for facies_kind in range(FACIES):
-        perm_local = perm_local + jnp.where(facies == facies_kind, facies_perm[facies_kind], 0.0)
-    perm_local = perm_local * perm_scale
+    kinds = jnp.arange(FACIES, dtype=jnp.int32).reshape(FACIES, 1, 1, 1)
+    table = facies_perm.reshape(FACIES, 1, 1, 1)
+    perm_local = jnp.sum(jnp.where(facies[None] == kinds, table, 0.0), axis=0) * perm_scale
 
     stacked = jnp.stack([perm_local, pressure_start, source])
     stacked = with_rows(stacked, "sub", 1, OV + 1)

time: 228 us -> 222 us (0.974)
  other arithmetic: 21 us -> 16.2 us
    another operation x1, other arithmetic: 5.9 us -> 0.01 us  [on_device(): stacked = jnp.stack([perm_local, pressure_start, source])]
    unnamed x58 -> x60, local copies, waits for them, and re-layouts: 8.31 us -> 9.05 us
where the time goes in v5:
time: 222 us; the launch traced here: 221 us
  waiting for transfers between devices  90.1 us (41%)
  starting transfers between devices  64.7 us (29%)
  Pallas kernels  36.1 us (16%)
  other arithmetic  16.2 us (7%)
  local copies, waits for them, and re-layouts  11 us (5%)
  between operations  2.79 us (1%)
    ppermute x8, waiting for transfers between devices, on_device(): lax.ppermute(estimate_own, 'grp', grp_pairs('grp', -1))  60.6 us
    pallas_call x8, Pallas kernels, round_call(): pl.pallas_call(make_round_kernel(weight_now, weight_next, last, own_cols)...  36.1 us
    ppermute x8, starting transfers between devices, on_device(): lax.ppermute(estimate_own, 'grp', grp_pairs('grp', 1))  20.8 us
    ppermute x8, starting transfers between devices, on_device(): lax.ppermute(estimate_own, 'grp', grp_pairs('grp', -1))  18 us
    ppermute x1, waiting for transfers between devices, with_sides(): from_right = lax.ppermute(value, axis, grp_pairs(axis, -1))  11 us
    unnamed x60, local copies, waits for them, and re-layouts  9.05 us
    ppermute x1, waiting for transfers between devices, on_device(): from_above = lax.ppermute(correction[:span], 'sub', grp_pairs('sub', -1))  6.25 us
    ppermute x1, starting transfers between devices, on_device(): lax.ppermute(correction[margin_rows - span:], 'sub', grp_pairs('sub', 1))  5.43 us
  transfers between devices with their start and end apart: 24, of which 14 were waited for; matrix products, arithmetic and copies ran while one was open for 4% of the time, Pallas kernels for 0%

profile of v5, /device:TPU:225, one launch (start us, length us, event | category | flops | bytes accessed | tf_op | source)
XLA Modules:
  0.0 220.9 jit_solution(3933117713553445566)
XLA Ops:
  1.9 4.5 %collective-permute-start = (f32[3,5,8,128]{3,2,1,0:T(8,128)S(1)}, f32[3,5,8,128]{3,2,1,0:T(8,128)S(1)}, u32[]{:S(2)}, u32[]{:S(2)}) collective-permute-start(f32[3,5,8,128]{3,2,1,0:T(8,128)S(1)} %get-tuple-element.40), channel_id=1, source_target_pairs={{0,16},{16,32},{32,48},{48,64},{64,80},{80,96},{96,112},{112,128},... | collective-permute-start | bytes 184328 | tf_op jit(solution)/shard_map/ppermute | solution.py:213
  20.1 4.6 %collective-permute-done.2 = f32[3,26,8,128]{3,2,1,0:T(8,128)S(1)} collective-permute-done((f32[3,26,8,128]{3,2,1,0:T(8,128)S(1)}, f32[3,26,8,128]{3,2,1,0:T(8,128)S(1)}, u32[]{:S(2)}, u32[]{:S(2)}) %collective-permute-start.2) | collective-permute-done | bytes 319520 | tf_op jit(solution)/shard_map/ppermute | solution.py:206
  24.8 11.0 %collective-permute-done.3 = f32[3,26,8,128]{3,2,1,0:T(8,128)S(1)} collective-permute-done((f32[3,26,8,128]{3,2,1,0:T(8,128)S(1)}, f32[3,26,8,128]{3,2,1,0:T(8,128)S(1)}, u32[]{:S(2)}, u32[]{:S(2)}) %collective-permute-start.3) | collective-permute-done | bytes 319520 | tf_op jit(solution)/shard_map/ppermute | solution.py:207
  54.0 4.6 %shard_map.64.own_ref = f32[24,8,128]{2,1,0:T(8,128)} custom-call(s32[2]{0:T(128)} %pad_add_fusion.1.depth_ref, f32[24,8,128]{2,1,0:T(8,128)} %copy-done.12, f32[24,8,128]{2,1,0:T(8,128)} %copy-done.10, f32[24,8,128]{2,1,0:T(8,128)} %copy-done.13, f32[24,24,128]{2,1,0:T(8,128)} %copy-done.6, f32[24,24,128]{2,1,0:T(8,128)} %copy-done.5, ...), custom_call_target="tpu_custom_call" | custom-call | tf_op jit(solution)/shard_map/pallas_call | solution.py:191
  58.5 5.5 %collective-permute-start.6 = (f32[24,8,128]{2,1,0:T(8,128)}, f32[24,8,128]{2,1,0:T(8,128)S(1)}, u32[]{:S(2)}, u32[]{:S(2)}) collective-permute-start(f32[24,8,128]{2,1,0:T(8,128)} %shard_map.64.own_ref), channel_id=1, source_target_pairs={{0,1},{1,2},{2,3},{3,4},{4,5},{5,6},{6,7},{7,8},{8,9},{9,10},{10,1... | collective-permute-start | bytes 294920 | tf_op jit(solution)/shard_map/ppermute | solution.py:328
  67.3 7.8 %collective-permute-done.7.right_ref = f32[24,8,128]{2,1,0:T(8,128)S(1)} collective-permute-done((f32[24,8,128]{2,1,0:T(8,128)}, f32[24,8,128]{2,1,0:T(8,128)S(1)}, u32[]{:S(2)}, u32[]{:S(2)}) %collective-permute-start.7) | collective-permute-done | bytes 98336 | tf_op jit(solution)/shard_map/ppermute | solution.py:330
  75.7 4.6 %shard_map.65.own_ref = f32[24,8,128]{2,1,0:T(8,128)} custom-call(s32[2]{0:T(128)} %pad_add_fusion.1.depth_ref, f32[24,8,128]{2,1,0:T(8,128)} %copy-done.19, f32[24,8,128]{2,1,0:T(8,128)} %shard_map.64.own_ref, f32[24,8,128]{2,1,0:T(8,128)} %copy-done.24, f32[24,24,128]{2,1,0:T(8,128)} %copy-done.6, f32[24,24,128]{2,1,0:T(8,128)} %copy-done.5, ...), custom_call_target="tpu_custom_call" | custom-call | tf_op jit(solution)/shard_map/pallas_call | solution.py:191
  85.2 8.0 %collective-permute-done.9.right_ref = f32[24,8,128]{2,1,0:T(8,128)S(1)} collective-permute-done((f32[24,8,128]{2,1,0:T(8,128)}, f32[24,8,128]{2,1,0:T(8,128)S(1)}, u32[]{:S(2)}, u32[]{:S(2)}) %collective-permute-start.9) | collective-permute-done | bytes 98336 | tf_op jit(solution)/shard_map/ppermute | solution.py:330
  93.8 4.6 %shard_map.66.own_ref = f32[24,8,128]{2,1,0:T(8,128)} custom-call(s32[2]{0:T(128)} %pad_add_fusion.1.depth_ref, f32[24,8,128]{2,1,0:T(8,128)} %copy-done.17, f32[24,8,128]{2,1,0:T(8,128)} %shard_map.65.own_ref, f32[24,8,128]{2,1,0:T(8,128)} %copy-done.20, f32[24,24,128]{2,1,0:T(8,128)} %copy-done.6, f32[24,24,128]{2,1,0:T(8,128)} %copy-done.5, ...), custom_call_target="tpu_custom_call" | custom-call | tf_op jit(solution)/shard_map/pallas_call | solution.py:191
  103.4 8.0 %collective-permute-done.11.right_ref = f32[24,8,128]{2,1,0:T(8,128)S(1)} collective-permute-done((f32[24,8,128]{2,1,0:T(8,128)}, f32[24,8,128]{2,1,0:T(8,128)S(1)}, u32[]{:S(2)}, u32[]{:S(2)}) %collective-permute-start.11) | collective-permute-done | bytes 98336 | tf_op jit(solution)/shard_map/ppermute | solution.py:330
  112.0 4.4 %shard_map.67 = f32[24,24,128]{2,1,0:T(8,128)} custom-call(s32[2]{0:T(128)} %pad_add_fusion.1.depth_ref, f32[24,8,128]{2,1,0:T(8,128)} %copy-done.16, f32[24,8,128]{2,1,0:T(8,128)} %shard_map.66.own_ref, f32[24,8,128]{2,1,0:T(8,128)} %copy-done.18, f32[24,24,128]{2,1,0:T(8,128)} %copy-done.6, f32[24,24,128]{2,1,0:T(8,128)} %copy-done.5, ...), custom_call_target="tpu_custom_call" | custom-call | tf_op jit(solution)/shard_map/pallas_call | solution.py:191
  117.5 5.4 %collective-permute-start.12 = (f32[9,24,128]{2,1,0:T(8,128)S(1)}, f32[9,24,128]{2,1,0:T(8,128)S(1)}, u32[]{:S(2)}, u32[]{:S(2)}) collective-permute-start(f32[9,24,128]{2,1,0:T(8,128)S(1)} %get-tuple-element.27), channel_id=1, source_target_pairs={{0,16},{16,32},{32,48},{48,64},{64,80},{80,96},{96,112},{112,128},... | collective-permute-start | bytes 331784 | tf_op jit(solution)/shard_map/ppermute | solution.py:349
  124.9 6.3 %collective-permute-done.13 = f32[9,24,128]{2,1,0:T(8,128)S(1)} collective-permute-done((f32[9,24,128]{2,1,0:T(8,128)S(1)}, f32[9,24,128]{2,1,0:T(8,128)S(1)}, u32[]{:S(2)}, u32[]{:S(2)}) %collective-permute-start.13) | collective-permute-done | bytes 110624 | tf_op jit(solution)/shard_map/ppermute | solution.py:352
  134.2 3.5 %collective-permute-start.14 = (f32[24,8,128]{2,1,0:T(8,128)S(1)}, f32[24,8,128]{2,1,0:T(8,128)S(1)}, u32[]{:S(2)}, u32[]{:S(2)}) collective-permute-start(f32[24,8,128]{2,1,0:T(8,128)S(1)} %multiply_multiply_fusion.own_ref), channel_id=1, source_target_pairs={{0,1},{1,2},{2,3},{3,4},{4,5},{5,6},{6,7},{7,8},{8,9},{9,10},{10,1... | collective-permute-start | bytes 294920 | tf_op jit(solution)/shard_map/ppermute | solution.py:328
  139.7 8.8 %collective-permute-done.15.right_ref = f32[24,8,128]{2,1,0:T(8,128)S(1)} collective-permute-done((f32[24,8,128]{2,1,0:T(8,128)S(1)}, f32[24,8,128]{2,1,0:T(8,128)S(1)}, u32[]{:S(2)}, u32[]{:S(2)}) %collective-permute-start.15) | collective-permute-done | bytes 98336 | tf_op jit(solution)/shard_map/ppermute | solution.py:330
  149.2 4.6 %shard_map.68.own_ref = f32[24,8,128]{2,1,0:T(8,128)} custom-call(s32[2]{0:T(128)} %pad_add_fusion.1.depth_ref, f32[24,8,128]{2,1,0:T(8,128)} %copy-done.21, f32[24,8,128]{2,1,0:T(8,128)} %copy-done.11, f32[24,8,128]{2,1,0:T(8,128)} %copy-done.25, f32[24,24,128]{2,1,0:T(8,128)} %copy-done.7, f32[24,24,128]{2,1,0:T(8,128)} %copy-done.5, ...), custom_call_target="tpu_custom_call" | custom-call | tf_op jit(solution)/shard_map/pallas_call | solution.py:191
  158.1 8.5 %collective-permute-done.17.right_ref = f32[24,8,128]{2,1,0:T(8,128)S(1)} collective-permute-done((f32[24,8,128]{2,1,0:T(8,128)}, f32[24,8,128]{2,1,0:T(8,128)S(1)}, u32[]{:S(2)}, u32[]{:S(2)}) %collective-permute-start.17) | collective-permute-done | bytes 98336 | tf_op jit(solution)/shard_map/ppermute | solution.py:330
  167.2 4.6 %shard_map.69.own_ref = f32[24,8,128]{2,1,0:T(8,128)} custom-call(s32[2]{0:T(128)} %pad_add_fusion.1.depth_ref, f32[24,8,128]{2,1,0:T(8,128)} %copy-done.22, f32[24,8,128]{2,1,0:T(8,128)} %shard_map.68.own_ref, f32[24,8,128]{2,1,0:T(8,128)} %copy-done.26, f32[24,24,128]{2,1,0:T(8,128)} %copy-done.7, f32[24,24,128]{2,1,0:T(8,128)} %copy-done.5, ...), custom_call_target="tpu_custom_call" | custom-call | tf_op jit(solution)/shard_map/pallas_call | solution.py:191
  176.1 8.5 %collective-permute-done.19.right_ref = f32[24,8,128]{2,1,0:T(8,128)S(1)} collective-permute-done((f32[24,8,128]{2,1,0:T(8,128)}, f32[24,8,128]{2,1,0:T(8,128)S(1)}, u32[]{:S(2)}, u32[]{:S(2)}) %collective-permute-start.19) | collective-permute-done | bytes 98336 | tf_op jit(solution)/shard_map/ppermute | solution.py:330
  185.3 4.6 %shard_map.70.own_ref = f32[24,8,128]{2,1,0:T(8,128)} custom-call(s32[2]{0:T(128)} %pad_add_fusion.1.depth_ref, f32[24,8,128]{2,1,0:T(8,128)} %copy-done.23, f32[24,8,128]{2,1,0:T(8,128)} %shard_map.69.own_ref, f32[24,8,128]{2,1,0:T(8,128)} %copy-done.27, f32[24,24,128]{2,1,0:T(8,128)} %copy-done.7, f32[24,24,128]{2,1,0:T(8,128)} %copy-done.5, ...), custom_call_target="tpu_custom_call" | custom-call | tf_op jit(solution)/shard_map/pallas_call | solution.py:191
  194.2 8.5 %collective-permute-done.21.right_ref = f32[24,8,128]{2,1,0:T(8,128)S(1)} collective-permute-done((f32[24,8,128]{2,1,0:T(8,128)}, f32[24,8,128]{2,1,0:T(8,128)S(1)}, u32[]{:S(2)}, u32[]{:S(2)}) %collective-permute-start.21) | collective-permute-done | bytes 98336 | tf_op jit(solution)/shard_map/ppermute | solution.py:330
  203.4 4.4 %shard_map.71 = f32[24,24,128]{2,1,0:T(8,128)} custom-call(s32[2]{0:T(128)} %pad_add_fusion.1.depth_ref, f32[24,8,128]{2,1,0:T(8,128)} %copy-done.14, f32[24,8,128]{2,1,0:T(8,128)} %shard_map.70.own_ref, f32[24,8,128]{2,1,0:T(8,128)} %copy-done.15, f32[24,24,128]{2,1,0:T(8,128)} %copy-done.7, f32[24,24,128]{2,1,0:T(8,128)} %copy-done.5, ...), custom_call_target="tpu_custom_call" | custom-call | tf_op jit(solution)/shard_map/pallas_call | solution.py:191
  208.8 4.2 %collective-permute-start.22 = (f32[4,8,128]{2,1,0:T(8,128)S(1)}, f32[4,8,128]{2,1,0:T(8,128)S(1)}, u32[]{:S(2)}, u32[]{:S(2)}) collective-permute-start(f32[4,8,128]{2,1,0:T(8,128)S(1)} %get-tuple-element.25), channel_id=1, source_target_pairs={{0,16},{16,32},{32,48},{48,64},{64,80},{80,96},{96,112},{112,128},... | collective-permute-start | bytes 49160 | tf_op jit(solution)/shard_map/ppermute | solution.py:364
  215.0 5.2 %collective-permute-done.23 = f32[4,8,128]{2,1,0:T(8,128)S(1)} collective-permute-done((f32[4,8,128]{2,1,0:T(8,128)S(1)}, f32[4,8,128]{2,1,0:T(8,128)S(1)}, u32[]{:S(2)}, u32[]{:S(2)}) %collective-permute-start.23) | collective-permute-done | bytes 16416 | tf_op jit(solution)/shard_map/ppermute | solution.py:367
  (192 shorter events, 73.4 us)
Async XLA Ops:
  1.9 11.1 %collective-permute-start = (f32[3,5,8,128]{3,2,1,0:T(8,128)S(1)}, f32[3,5,8,128]{3,2,1,0:T(8,128)S(1)}, u32[]{:S(2)}, u32[]{:S(2)}) collective-permute-start(f32[3,5,8,128]{3,2,1,0:T(8,128)S(1)} %get-tuple-element.40), channel_id=1, source_target_pairs={{0,16},{16,32},{32,48},{48,64},{64,80},{80,96},{96,112},{112,128},... | collective-permute-start | bytes 184328 | tf_op jit(solution)/shard_map/ppermute | solution.py:213
  6.5 7.7 %collective-permute-start.1 = (f32[3,5,8,128]{3,2,1,0:T(8,128)S(1)}, f32[3,5,8,128]{3,2,1,0:T(8,128)S(1)}, u32[]{:S(2)}, u32[]{:S(2)}) collective-permute-start(f32[3,5,8,128]{3,2,1,0:T(8,128)S(1)} %get-tuple-element.41), channel_id=1, source_target_pairs={{16,0},{32,16},{48,32},{64,48},{80,64},{96,80},{112,96},{128,112},... | collective-permute-start | bytes 184328 | tf_op jit(solution)/shard_map/ppermute | solution.py:216
  14.1 10.6 %collective-permute-start.2 = (f32[3,26,8,128]{3,2,1,0:T(8,128)S(1)}, f32[3,26,8,128]{3,2,1,0:T(8,128)S(1)}, u32[]{:S(2)}, u32[]{:S(2)}) collective-permute-start(f32[3,26,8,128]{3,2,1,0:T(8,128)S(1)} %pad_maximum_fusion.1), channel_id=1, source_target_pairs={{0,1},{1,2},{2,3},{3,4},{4,5},{5,6},{6,7},{7,8},{8,9},{9,10},{10,1... | collective-permute-start | bytes 958472 | tf_op jit(solution)/shard_map/ppermute | solution.py:206
  17.4 18.3 %collective-permute-start.3 = (f32[3,26,8,128]{3,2,1,0:T(8,128)S(1)}, f32[3,26,8,128]{3,2,1,0:T(8,128)S(1)}, u32[]{:S(2)}, u32[]{:S(2)}) collective-permute-start(f32[3,26,8,128]{3,2,1,0:T(8,128)S(1)} %pad_maximum_fusion.1), channel_id=1, source_target_pairs={{1,0},{2,1},{3,2},{4,3},{5,4},{6,5},{7,6},{8,7},{9,8},{10,9},{11,1... | collective-permute-start | bytes 958472 | tf_op jit(solution)/shard_map/ppermute | solution.py:207
  40.7 10.2 %collective-permute-start.4 = (f32[24,8,128]{2,1,0:T(8,128)S(1)}, f32[24,8,128]{2,1,0:T(8,128)S(1)}, u32[]{:S(2)}, u32[]{:S(2)}) collective-permute-start(f32[24,8,128]{2,1,0:T(8,128)S(1)} %multiply_multiply_fusion.1.own_ref), channel_id=1, source_target_pairs={{0,1},{1,2},{2,3},{3,4},{4,5},{5,6},{6,7},{7,8},{8,9},{9,10},{10,1... | collective-permute-start | bytes 294920 | tf_op jit(solution)/shard_map/ppermute | solution.py:328
  42.6 10.7 %collective-permute-start.5 = (f32[24,8,128]{2,1,0:T(8,128)S(1)}, f32[24,8,128]{2,1,0:T(8,128)S(1)}, u32[]{:S(2)}, u32[]{:S(2)}) collective-permute-start(f32[24,8,128]{2,1,0:T(8,128)S(1)} %multiply_multiply_fusion.1.own_ref), channel_id=1, source_target_pairs={{1,0},{2,1},{3,2},{4,3},{5,4},{6,5},{7,6},{8,7},{9,8},{10,9},{11,1... | collective-permute-start | bytes 294920 | tf_op jit(solution)/shard_map/ppermute | solution.py:330
  58.5 8.7 %collective-permute-start.6 = (f32[24,8,128]{2,1,0:T(8,128)}, f32[24,8,128]{2,1,0:T(8,128)S(1)}, u32[]{:S(2)}, u32[]{:S(2)}) collective-permute-start(f32[24,8,128]{2,1,0:T(8,128)} %shard_map.64.own_ref), channel_id=1, source_target_pairs={{0,1},{1,2},{2,3},{3,4},{4,5},{5,6},{6,7},{7,8},{8,9},{9,10},{10,1... | collective-permute-start | bytes 294920 | tf_op jit(solution)/shard_map/ppermute | solution.py:328
  64.1 11.0 %collective-permute-start.7 = (f32[24,8,128]{2,1,0:T(8,128)}, f32[24,8,128]{2,1,0:T(8,128)S(1)}, u32[]{:S(2)}, u32[]{:S(2)}) collective-permute-start(f32[24,8,128]{2,1,0:T(8,128)} %shard_map.64.own_ref), channel_id=1, source_target_pairs={{1,0},{2,1},{3,2},{4,3},{5,4},{6,5},{7,6},{8,7},{9,8},{10,9},{11,1... | collective-permute-start | bytes 294920 | tf_op jit(solution)/shard_map/ppermute | solution.py:330
  80.2 4.9 %collective-permute-start.8 = (f32[24,8,128]{2,1,0:T(8,128)}, f32[24,8,128]{2,1,0:T(8,128)S(1)}, u32[]{:S(2)}, u32[]{:S(2)}) collective-permute-start(f32[24,8,128]{2,1,0:T(8,128)} %shard_map.65.own_ref), channel_id=1, source_target_pairs={{0,1},{1,2},{2,3},{3,4},{4,5},{5,6},{6,7},{7,8},{8,9},{9,10},{10,1... | collective-permute-start | bytes 294920 | tf_op jit(solution)/shard_map/ppermute | solution.py:328
  82.2 11.0 %collective-permute-start.9 = (f32[24,8,128]{2,1,0:T(8,128)}, f32[24,8,128]{2,1,0:T(8,128)S(1)}, u32[]{:S(2)}, u32[]{:S(2)}) collective-permute-start(f32[24,8,128]{2,1,0:T(8,128)} %shard_map.65.own_ref), channel_id=1, source_target_pairs={{1,0},{2,1},{3,2},{4,3},{5,4},{6,5},{7,6},{8,7},{9,8},{10,9},{11,1... | collective-permute-start | bytes 294920 | tf_op jit(solution)/shard_map/ppermute | solution.py:330
  98.3 5.0 %collective-permute-start.10 = (f32[24,8,128]{2,1,0:T(8,128)}, f32[24,8,128]{2,1,0:T(8,128)S(1)}, u32[]{:S(2)}, u32[]{:S(2)}) collective-permute-start(f32[24,8,128]{2,1,0:T(8,128)} %shard_map.66.own_ref), channel_id=1, source_target_pairs={{0,1},{1,2},{2,3},{3,4},{4,5},{5,6},{6,7},{7,8},{8,9},{9,10},{10,1... | collective-permute-start | bytes 294920 | tf_op jit(solution)/shard_map/ppermute | solution.py:328
  100.4 11.0 %collective-permute-start.11 = (f32[24,8,128]{2,1,0:T(8,128)}, f32[24,8,128]{2,1,0:T(8,128)S(1)}, u32[]{:S(2)}, u32[]{:S(2)}) collective-permute-start(f32[24,8,128]{2,1,0:T(8,128)} %shard_map.66.own_ref), channel_id=1, source_target_pairs={{1,0},{2,1},{3,2},{4,3},{5,4},{6,5},{7,6},{8,7},{9,8},{10,9},{11,1... | collective-permute-start | bytes 294920 | tf_op jit(solution)/shard_map/ppermute | solution.py:330
  117.5 7.4 %collective-permute-start.12 = (f32[9,24,128]{2,1,0:T(8,128)S(1)}, f32[9,24,128]{2,1,0:T(8,128)S(1)}, u32[]{:S(2)}, u32[]{:S(2)}) collective-permute-start(f32[9,24,128]{2,1,0:T(8,128)S(1)} %get-tuple-element.27), channel_id=1, source_target_pairs={{0,16},{16,32},{32,48},{48,64},{64,80},{80,96},{96,112},{112,128},... | collective-permute-start | bytes 331784 | tf_op jit(solution)/shard_map/ppermute | solution.py:349
  122.9 8.2 %collective-permute-start.13 = (f32[9,24,128]{2,1,0:T(8,128)S(1)}, f32[9,24,128]{2,1,0:T(8,128)S(1)}, u32[]{:S(2)}, u32[]{:S(2)}) collective-permute-start(f32[9,24,128]{2,1,0:T(8,128)S(1)} %get-tuple-element.28), channel_id=1, source_target_pairs={{16,0},{32,16},{48,32},{64,48},{80,64},{96,80},{112,96},{128,112},... | collective-permute-start | bytes 331784 | tf_op jit(solution)/shard_map/ppermute | solution.py:352
  134.2 5.5 %collective-permute-start.14 = (f32[24,8,128]{2,1,0:T(8,128)S(1)}, f32[24,8,128]{2,1,0:T(8,128)S(1)}, u32[]{:S(2)}, u32[]{:S(2)}) collective-permute-start(f32[24,8,128]{2,1,0:T(8,128)S(1)} %multiply_multiply_fusion.own_ref), channel_id=1, source_target_pairs={{0,1},{1,2},{2,3},{3,4},{4,5},{5,6},{6,7},{7,8},{8,9},{9,10},{10,1... | collective-permute-start | bytes 294920 | tf_op jit(solution)/shard_map/ppermute | solution.py:328
  137.8 10.7 %collective-permute-start.15 = (f32[24,8,128]{2,1,0:T(8,128)S(1)}, f32[24,8,128]{2,1,0:T(8,128)S(1)}, u32[]{:S(2)}, u32[]{:S(2)}) collective-permute-start(f32[24,8,128]{2,1,0:T(8,128)S(1)} %multiply_multiply_fusion.own_ref), channel_id=1, source_target_pairs={{1,0},{2,1},{3,2},{4,3},{5,4},{6,5},{7,6},{8,7},{9,8},{10,9},{11,1... | collective-permute-start | bytes 294920 | tf_op jit(solution)/shard_map/ppermute | solution.py:330
  153.7 4.3 %collective-permute-start.16 = (f32[24,8,128]{2,1,0:T(8,128)}, f32[24,8,128]{2,1,0:T(8,128)S(1)}, u32[]{:S(2)}, u32[]{:S(2)}) collective-permute-start(f32[24,8,128]{2,1,0:T(8,128)} %shard_map.68.own_ref), channel_id=1, source_target_pairs={{0,1},{1,2},{2,3},{3,4},{4,5},{5,6},{6,7},{7,8},{8,9},{9,10},{10,1... | collective-permute-start | bytes 294920 | tf_op jit(solution)/shard_map/ppermute | solution.py:328
  155.6 11.0 %collective-permute-start.17 = (f32[24,8,128]{2,1,0:T(8,128)}, f32[24,8,128]{2,1,0:T(8,128)S(1)}, u32[]{:S(2)}, u32[]{:S(2)}) collective-permute-start(f32[24,8,128]{2,1,0:T(8,128)} %shard_map.68.own_ref), channel_id=1, source_target_pairs={{1,0},{2,1},{3,2},{4,3},{5,4},{6,5},{7,6},{8,7},{9,8},{10,9},{11,1... | collective-permute-start | bytes 294920 | tf_op jit(solution)/shard_map/ppermute | solution.py:330
  171.8 4.3 %collective-permute-start.18 = (f32[24,8,128]{2,1,0:T(8,128)}, f32[24,8,128]{2,1,0:T(8,128)S(1)}, u32[]{:S(2)}, u32[]{:S(2)}) collective-permute-start(f32[24,8,128]{2,1,0:T(8,128)} %shard_map.69.own_ref), channel_id=1, source_target_pairs={{0,1},{1,2},{2,3},{3,4},{4,5},{5,6},{6,7},{7,8},{8,9},{9,10},{10,1... | collective-permute-start | bytes 294920 | tf_op jit(solution)/shard_map/ppermute | solution.py:328
  173.7 11.0 %collective-permute-start.19 = (f32[24,8,128]{2,1,0:T(8,128)}, f32[24,8,128]{2,1,0:T(8,128)S(1)}, u32[]{:S(2)}, u32[]{:S(2)}) collective-permute-start(f32[24,8,128]{2,1,0:T(8,128)} %shard_map.69.own_ref), channel_id=1, source_target_pairs={{1,0},{2,1},{3,2},{4,3},{5,4},{6,5},{7,6},{8,7},{9,8},{10,9},{11,1... | collective-permute-start | bytes 294920 | tf_op jit(solution)/shard_map/ppermute | solution.py:330
  189.9 4.3 %collective-permute-start.20 = (f32[24,8,128]{2,1,0:T(8,128)}, f32[24,8,128]{2,1,0:T(8,128)S(1)}, u32[]{:S(2)}, u32[]{:S(2)}) collective-permute-start(f32[24,8,128]{2,1,0:T(8,128)} %shard_map.70.own_ref), channel_id=1, source_target_pairs={{0,1},{1,2},{2,3},{3,4},{4,5},{5,6},{6,7},{7,8},{8,9},{9,10},{10,1... | collective-permute-start | bytes 294920 | tf_op jit(solution)/shard_map/ppermute | solution.py:328
  191.8 11.0 %collective-permute-start.21 = (f32[24,8,128]{2,1,0:T(8,128)}, f32[24,8,128]{2,1,0:T(8,128)S(1)}, u32[]{:S(2)}, u32[]{:S(2)}) collective-permute-start(f32[24,8,128]{2,1,0:T(8,128)} %shard_map.70.own_ref), channel_id=1, source_target_pairs={{1,0},{2,1},{3,2},{4,3},{5,4},{6,5},{7,6},{8,7},{9,8},{10,9},{11,1... | collective-permute-start | bytes 294920 | tf_op jit(solution)/shard_map/ppermute | solution.py:330
  208.8 6.2 %collective-permute-start.22 = (f32[4,8,128]{2,1,0:T(8,128)S(1)}, f32[4,8,128]{2,1,0:T(8,128)S(1)}, u32[]{:S(2)}, u32[]{:S(2)}) collective-permute-start(f32[4,8,128]{2,1,0:T(8,128)S(1)} %get-tuple-element.25), channel_id=1, source_target_pairs={{0,16},{16,32},{32,48},{48,64},{64,80},{80,96},{96,112},{112,128},... | collective-permute-start | bytes 49160 | tf_op jit(solution)/shard_map/ppermute | solution.py:364
  213.1 7.2 %collective-permute-start.23 = (f32[4,8,128]{2,1,0:T(8,128)S(1)}, f32[4,8,128]{2,1,0:T(8,128)S(1)}, u32[]{:S(2)}, u32[]{:S(2)}) collective-permute-start(f32[4,8,128]{2,1,0:T(8,128)S(1)} %get-tuple-element.26), channel_id=1, source_target_pairs={{16,0},{32,16},{48,32},{64,48},{80,64},{96,80},{112,96},{128,112},... | collective-permute-start | bytes 49160 | tf_op jit(solution)/shard_map/ppermute | solution.py:367
  (30 other events, 104.5 us)

commit v6 on v5

--- a/solution.py
+++ b/solution.py
@@ -169,7 +169,9 @@
                 s_ref[r] = result
         e = e + weight_now * s_ref[...]
         if last:
-            o_ref[...] = e
+            inside = (offsets >= -depth_low) & (offsets < slab_rows + depth_high)
+            band = (offsets < depth_low) | (offsets >= slab_rows - depth_high)
+            o_ref[...] = jnp.where(inside & band, 0.5, jnp.where(inside, 1.0, 0.0)) * e
         else:
             update = (act * (target - operate(e)))[:, own_cols]
             own_act = act[:, own_cols]
@@ -343,7 +345,7 @@
                 factors_x,
             )
             estimate_own = estimate
-        correction = weight * estimate
+        correction = estimate
         if outer_turn + 1 < OUTER:
             span = 2 * OV + 1
             from_below = lax.ppermute(

time: 222 us -> 223 us (level)
    unnamed x60 -> x62, local copies, waits for them, and re-layouts: 9.05 us -> 9.13 us
  transfers between devices with their start and end apart: 24 -> 24, of which waited for: 14 -> 15; matrix products, arithmetic and copies ran while one was open for 4% -> 4% of each run, Pallas kernels for 0% -> 0%
where the time goes in v6:
time: 223 us; the launch traced here: 222 us
  waiting for transfers between devices  91.2 us (41%)
  starting transfers between devices  64.9 us (29%)
  Pallas kernels  36.2 us (16%)
  other arithmetic  14.4 us (6%)
  local copies, waits for them, and re-layouts  12.8 us (6%)
    ppermute x8, waiting for transfers between devices, on_device(): lax.ppermute(estimate_own, 'grp', grp_pairs('grp', -1))  61.4 us
    pallas_call x8, Pallas kernels, round_call(): pl.pallas_call(make_round_kernel(weight_now, weight_next, last, own_cols)...  36.2 us
    ppermute x8, starting transfers between devices, on_device(): lax.ppermute(estimate_own, 'grp', grp_pairs('grp', 1))  20.8 us
    ppermute x8, starting transfers between devices, on_device(): lax.ppermute(estimate_own, 'grp', grp_pairs('grp', -1))  18.2 us
    ppermute x1, waiting for transfers between devices, with_sides(): from_right = lax.ppermute(value, axis, grp_pairs(axis, -1))  11.1 us
    unnamed x62, local copies, waits for them, and re-layouts  9.13 us
    ppermute x1, waiting for transfers between devices, on_device(): from_above = lax.ppermute(correction[:span], 'sub', grp_pairs('sub', -1))  6.25 us
    ppermute x1, starting transfers between devices, on_device(): lax.ppermute(correction[margin_rows - span:], 'sub', grp_pairs('sub', 1))  5.44 us
  transfers between devices with their start and end apart: 24, of which 15 were waited for; matrix products, arithmetic and copies ran while one was open for 4% of the time, Pallas kernels for 0%

profile of v6, /device:TPU:225, one launch (start us, length us, event | category | flops | bytes accessed | tf_op | source)
XLA Modules:
  0.0 221.7 jit_solution(15235756099630065051)
XLA Ops:
  1.9 4.5 %collective-permute-start = (f32[3,5,8,128]{3,2,1,0:T(8,128)S(1)}, f32[3,5,8,128]{3,2,1,0:T(8,128)S(1)}, u32[]{:S(2)}, u32[]{:S(2)}) collective-permute-start(f32[3,5,8,128]{3,2,1,0:T(8,128)S(1)} %get-tuple-element.42), channel_id=1, source_target_pairs={{0,16},{16,32},{32,48},{48,64},{64,80},{80,96},{96,112},{112,128},... | collective-permute-start | bytes 184328 | tf_op jit(solution)/shard_map/ppermute | solution.py:215
  20.1 4.6 %collective-permute-done.2 = f32[3,26,8,128]{3,2,1,0:T(8,128)S(1)} collective-permute-done((f32[3,26,8,128]{3,2,1,0:T(8,128)S(1)}, f32[3,26,8,128]{3,2,1,0:T(8,128)S(1)}, u32[]{:S(2)}, u32[]{:S(2)}) %collective-permute-start.2) | collective-permute-done | bytes 319520 | tf_op jit(solution)/shard_map/ppermute | solution.py:208
  24.8 11.1 %collective-permute-done.3 = f32[3,26,8,128]{3,2,1,0:T(8,128)S(1)} collective-permute-done((f32[3,26,8,128]{3,2,1,0:T(8,128)S(1)}, f32[3,26,8,128]{3,2,1,0:T(8,128)S(1)}, u32[]{:S(2)}, u32[]{:S(2)}) %collective-permute-start.3) | collective-permute-done | bytes 319520 | tf_op jit(solution)/shard_map/ppermute | solution.py:209
  54.2 4.6 %shard_map.64.own_ref = f32[24,8,128]{2,1,0:T(8,128)} custom-call(s32[2]{0:T(128)} %pad_add_fusion.1.depth_ref, f32[24,8,128]{2,1,0:T(8,128)} %copy-done.13, f32[24,8,128]{2,1,0:T(8,128)} %copy-done.11, f32[24,8,128]{2,1,0:T(8,128)} %copy-done.14, f32[24,24,128]{2,1,0:T(8,128)} %copy-done.6, f32[24,24,128]{2,1,0:T(8,128)} %copy-done.5, ...), custom_call_target="tpu_custom_call" | custom-call | tf_op jit(solution)/shard_map/pallas_call | solution.py:193
  58.8 5.6 %collective-permute-start.6 = (f32[24,8,128]{2,1,0:T(8,128)}, f32[24,8,128]{2,1,0:T(8,128)S(1)}, u32[]{:S(2)}, u32[]{:S(2)}) collective-permute-start(f32[24,8,128]{2,1,0:T(8,128)} %shard_map.64.own_ref), channel_id=1, source_target_pairs={{0,1},{1,2},{2,3},{3,4},{4,5},{5,6},{6,7},{7,8},{8,9},{9,10},{10,1... | collective-permute-start | bytes 294920 | tf_op jit(solution)/shard_map/ppermute | solution.py:330
  67.5 7.8 %collective-permute-done.7.right_ref = f32[24,8,128]{2,1,0:T(8,128)S(1)} collective-permute-done((f32[24,8,128]{2,1,0:T(8,128)}, f32[24,8,128]{2,1,0:T(8,128)S(1)}, u32[]{:S(2)}, u32[]{:S(2)}) %collective-permute-start.7) | collective-permute-done | bytes 98336 | tf_op jit(solution)/shard_map/ppermute | solution.py:332
  75.9 4.6 %shard_map.65.own_ref = f32[24,8,128]{2,1,0:T(8,128)} custom-call(s32[2]{0:T(128)} %pad_add_fusion.1.depth_ref, f32[24,8,128]{2,1,0:T(8,128)} %copy-done.18, f32[24,8,128]{2,1,0:T(8,128)} %shard_map.64.own_ref, f32[24,8,128]{2,1,0:T(8,128)} %copy-done.24, f32[24,24,128]{2,1,0:T(8,128)} %copy-done.6, f32[24,24,128]{2,1,0:T(8,128)} %copy-done.5, ...), custom_call_target="tpu_custom_call" | custom-call | tf_op jit(solution)/shard_map/pallas_call | solution.py:193
  84.9 8.5 %collective-permute-done.9.right_ref = f32[24,8,128]{2,1,0:T(8,128)S(1)} collective-permute-done((f32[24,8,128]{2,1,0:T(8,128)}, f32[24,8,128]{2,1,0:T(8,128)S(1)}, u32[]{:S(2)}, u32[]{:S(2)}) %collective-permute-start.9) | collective-permute-done | bytes 98336 | tf_op jit(solution)/shard_map/ppermute | solution.py:332
  94.0 4.6 %shard_map.66.own_ref = f32[24,8,128]{2,1,0:T(8,128)} custom-call(s32[2]{0:T(128)} %pad_add_fusion.1.depth_ref, f32[24,8,128]{2,1,0:T(8,128)} %copy-done.19, f32[24,8,128]{2,1,0:T(8,128)} %shard_map.65.own_ref, f32[24,8,128]{2,1,0:T(8,128)} %copy-done.25, f32[24,24,128]{2,1,0:T(8,128)} %copy-done.6, f32[24,24,128]{2,1,0:T(8,128)} %copy-done.5, ...), custom_call_target="tpu_custom_call" | custom-call | tf_op jit(solution)/shard_map/pallas_call | solution.py:193
  103.4 8.3 %collective-permute-done.11.right_ref = f32[24,8,128]{2,1,0:T(8,128)S(1)} collective-permute-done((f32[24,8,128]{2,1,0:T(8,128)}, f32[24,8,128]{2,1,0:T(8,128)S(1)}, u32[]{:S(2)}, u32[]{:S(2)}) %collective-permute-start.11) | collective-permute-done | bytes 98336 | tf_op jit(solution)/shard_map/ppermute | solution.py:332
  112.3 4.4 %shard_map.67 = f32[24,24,128]{2,1,0:T(8,128)} custom-call(s32[2]{0:T(128)} %pad_add_fusion.1.depth_ref, f32[24,8,128]{2,1,0:T(8,128)} %copy-done.17, f32[24,8,128]{2,1,0:T(8,128)} %shard_map.66.own_ref, f32[24,8,128]{2,1,0:T(8,128)} %copy-done.23, f32[24,24,128]{2,1,0:T(8,128)} %copy-done.6, f32[24,24,128]{2,1,0:T(8,128)} %copy-done.5, ...), custom_call_target="tpu_custom_call" | custom-call | tf_op jit(solution)/shard_map/pallas_call | solution.py:193
  117.7 5.4 %collective-permute-start.12 = (f32[9,24,128]{2,1,0:T(8,128)S(1)}, f32[9,24,128]{2,1,0:T(8,128)S(1)}, u32[]{:S(2)}, u32[]{:S(2)}) collective-permute-start(f32[9,24,128]{2,1,0:T(8,128)S(1)} %get-tuple-element.29), channel_id=1, source_target_pairs={{0,16},{16,32},{32,48},{48,64},{64,80},{80,96},{96,112},{112,128},... | collective-permute-start | bytes 331784 | tf_op jit(solution)/shard_map/ppermute | solution.py:351
  125.1 6.3 %collective-permute-done.13 = f32[9,24,128]{2,1,0:T(8,128)S(1)} collective-permute-done((f32[9,24,128]{2,1,0:T(8,128)S(1)}, f32[9,24,128]{2,1,0:T(8,128)S(1)}, u32[]{:S(2)}, u32[]{:S(2)}) %collective-permute-start.13) | collective-permute-done | bytes 110624 | tf_op jit(solution)/shard_map/ppermute | solution.py:354
  134.5 3.5 %collective-permute-start.14 = (f32[24,8,128]{2,1,0:T(8,128)S(1)}, f32[24,8,128]{2,1,0:T(8,128)S(1)}, u32[]{:S(2)}, u32[]{:S(2)}) collective-permute-start(f32[24,8,128]{2,1,0:T(8,128)S(1)} %multiply_multiply_fusion.own_ref), channel_id=1, source_target_pairs={{0,1},{1,2},{2,3},{3,4},{4,5},{5,6},{6,7},{7,8},{8,9},{9,10},{10,1... | collective-permute-start | bytes 294920 | tf_op jit(solution)/shard_map/ppermute | solution.py:330
  140.0 8.8 %collective-permute-done.15.right_ref = f32[24,8,128]{2,1,0:T(8,128)S(1)} collective-permute-done((f32[24,8,128]{2,1,0:T(8,128)S(1)}, f32[24,8,128]{2,1,0:T(8,128)S(1)}, u32[]{:S(2)}, u32[]{:S(2)}) %collective-permute-start.15) | collective-permute-done | bytes 98336 | tf_op jit(solution)/shard_map/ppermute | solution.py:332
  149.4 4.6 %shard_map.68.own_ref = f32[24,8,128]{2,1,0:T(8,128)} custom-call(s32[2]{0:T(128)} %pad_add_fusion.1.depth_ref, f32[24,8,128]{2,1,0:T(8,128)} %copy-done.20, f32[24,8,128]{2,1,0:T(8,128)} %copy-done.12, f32[24,8,128]{2,1,0:T(8,128)} %copy-done.26, f32[24,24,128]{2,1,0:T(8,128)} %copy-done.7, f32[24,24,128]{2,1,0:T(8,128)} %copy-done.5, ...), custom_call_target="tpu_custom_call" | custom-call | tf_op jit(solution)/shard_map/pallas_call | solution.py:193
  158.4 8.5 %collective-permute-done.17.right_ref = f32[24,8,128]{2,1,0:T(8,128)S(1)} collective-permute-done((f32[24,8,128]{2,1,0:T(8,128)}, f32[24,8,128]{2,1,0:T(8,128)S(1)}, u32[]{:S(2)}, u32[]{:S(2)}) %collective-permute-start.17) | collective-permute-done | bytes 98336 | tf_op jit(solution)/shard_map/ppermute | solution.py:332
  167.5 4.6 %shard_map.69.own_ref = f32[24,8,128]{2,1,0:T(8,128)} custom-call(s32[2]{0:T(128)} %pad_add_fusion.1.depth_ref, f32[24,8,128]{2,1,0:T(8,128)} %copy-done.21, f32[24,8,128]{2,1,0:T(8,128)} %shard_map.68.own_ref, f32[24,8,128]{2,1,0:T(8,128)} %copy-done.27, f32[24,24,128]{2,1,0:T(8,128)} %copy-done.7, f32[24,24,128]{2,1,0:T(8,128)} %copy-done.5, ...), custom_call_target="tpu_custom_call" | custom-call | tf_op jit(solution)/shard_map/pallas_call | solution.py:193
  176.4 8.5 %collective-permute-done.19.right_ref = f32[24,8,128]{2,1,0:T(8,128)S(1)} collective-permute-done((f32[24,8,128]{2,1,0:T(8,128)}, f32[24,8,128]{2,1,0:T(8,128)S(1)}, u32[]{:S(2)}, u32[]{:S(2)}) %collective-permute-start.19) | collective-permute-done | bytes 98336 | tf_op jit(solution)/shard_map/ppermute | solution.py:332
  185.6 4.6 %shard_map.70.own_ref = f32[24,8,128]{2,1,0:T(8,128)} custom-call(s32[2]{0:T(128)} %pad_add_fusion.1.depth_ref, f32[24,8,128]{2,1,0:T(8,128)} %copy-done.22, f32[24,8,128]{2,1,0:T(8,128)} %shard_map.69.own_ref, f32[24,8,128]{2,1,0:T(8,128)} %copy-done.28, f32[24,24,128]{2,1,0:T(8,128)} %copy-done.7, f32[24,24,128]{2,1,0:T(8,128)} %copy-done.5, ...), custom_call_target="tpu_custom_call" | custom-call | tf_op jit(solution)/shard_map/pallas_call | solution.py:193
  194.5 8.5 %collective-permute-done.21.right_ref = f32[24,8,128]{2,1,0:T(8,128)S(1)} collective-permute-done((f32[24,8,128]{2,1,0:T(8,128)}, f32[24,8,128]{2,1,0:T(8,128)S(1)}, u32[]{:S(2)}, u32[]{:S(2)}) %collective-permute-start.21) | collective-permute-done | bytes 98336 | tf_op jit(solution)/shard_map/ppermute | solution.py:332
  203.7 4.4 %shard_map.71 = f32[24,24,128]{2,1,0:T(8,128)} custom-call(s32[2]{0:T(128)} %pad_add_fusion.1.depth_ref, f32[24,8,128]{2,1,0:T(8,128)} %copy-done.15, f32[24,8,128]{2,1,0:T(8,128)} %shard_map.70.own_ref, f32[24,8,128]{2,1,0:T(8,128)} %copy-done.16, f32[24,24,128]{2,1,0:T(8,128)} %copy-done.7, f32[24,24,128]{2,1,0:T(8,128)} %copy-done.5, ...), custom_call_target="tpu_custom_call" | custom-call | tf_op jit(solution)/shard_map/pallas_call | solution.py:193
  208.8 4.2 %collective-permute-start.22 = (f32[4,8,128]{2,1,0:T(8,128)S(1)}, f32[4,8,128]{2,1,0:T(8,128)S(1)}, u32[]{:S(2)}, u32[]{:S(2)}) collective-permute-start(f32[4,8,128]{2,1,0:T(8,128)S(1)} %get-tuple-element.27), channel_id=1, source_target_pairs={{0,16},{16,32},{32,48},{48,64},{64,80},{80,96},{96,112},{112,128},... | collective-permute-start | bytes 49160 | tf_op jit(solution)/shard_map/ppermute | solution.py:366
  215.0 5.2 %collective-permute-done.23 = f32[4,8,128]{2,1,0:T(8,128)S(1)} collective-permute-done((f32[4,8,128]{2,1,0:T(8,128)S(1)}, f32[4,8,128]{2,1,0:T(8,128)S(1)}, u32[]{:S(2)}, u32[]{:S(2)}) %collective-permute-start.23) | collective-permute-done | bytes 16416 | tf_op jit(solution)/shard_map/ppermute | solution.py:369
  (190 shorter events, 73.8 us)
Async XLA Ops:
  1.9 11.2 %collective-permute-start = (f32[3,5,8,128]{3,2,1,0:T(8,128)S(1)}, f32[3,5,8,128]{3,2,1,0:T(8,128)S(1)}, u32[]{:S(2)}, u32[]{:S(2)}) collective-permute-start(f32[3,5,8,128]{3,2,1,0:T(8,128)S(1)} %get-tuple-element.42), channel_id=1, source_target_pairs={{0,16},{16,32},{32,48},{48,64},{64,80},{80,96},{96,112},{112,128},... | collective-permute-start | bytes 184328 | tf_op jit(solution)/shard_map/ppermute | solution.py:215
  6.5 7.7 %collective-permute-start.1 = (f32[3,5,8,128]{3,2,1,0:T(8,128)S(1)}, f32[3,5,8,128]{3,2,1,0:T(8,128)S(1)}, u32[]{:S(2)}, u32[]{:S(2)}) collective-permute-start(f32[3,5,8,128]{3,2,1,0:T(8,128)S(1)} %get-tuple-element.43), channel_id=1, source_target_pairs={{16,0},{32,16},{48,32},{64,48},{80,64},{96,80},{112,96},{128,112},... | collective-permute-start | bytes 184328 | tf_op jit(solution)/shard_map/ppermute | solution.py:218
  14.1 10.6 %collective-permute-start.2 = (f32[3,26,8,128]{3,2,1,0:T(8,128)S(1)}, f32[3,26,8,128]{3,2,1,0:T(8,128)S(1)}, u32[]{:S(2)}, u32[]{:S(2)}) collective-permute-start(f32[3,26,8,128]{3,2,1,0:T(8,128)S(1)} %pad_maximum_fusion.1), channel_id=1, source_target_pairs={{0,1},{1,2},{2,3},{3,4},{4,5},{5,6},{6,7},{7,8},{8,9},{9,10},{10,1... | collective-permute-start | bytes 958472 | tf_op jit(solution)/shard_map/ppermute | solution.py:208
  17.4 18.5 %collective-permute-start.3 = (f32[3,26,8,128]{3,2,1,0:T(8,128)S(1)}, f32[3,26,8,128]{3,2,1,0:T(8,128)S(1)}, u32[]{:S(2)}, u32[]{:S(2)}) collective-permute-start(f32[3,26,8,128]{3,2,1,0:T(8,128)S(1)} %pad_maximum_fusion.1), channel_id=1, source_target_pairs={{1,0},{2,1},{3,2},{4,3},{5,4},{6,5},{7,6},{8,7},{9,8},{10,9},{11,1... | collective-permute-start | bytes 958472 | tf_op jit(solution)/shard_map/ppermute | solution.py:209
  40.9 10.2 %collective-permute-start.4 = (f32[24,8,128]{2,1,0:T(8,128)S(1)}, f32[24,8,128]{2,1,0:T(8,128)S(1)}, u32[]{:S(2)}, u32[]{:S(2)}) collective-permute-start(f32[24,8,128]{2,1,0:T(8,128)S(1)} %multiply_multiply_fusion.1.own_ref), channel_id=1, source_target_pairs={{0,1},{1,2},{2,3},{3,4},{4,5},{5,6},{6,7},{7,8},{8,9},{9,10},{10,1... | collective-permute-start | bytes 294920 | tf_op jit(solution)/shard_map/ppermute | solution.py:330
  42.8 10.7 %collective-permute-start.5 = (f32[24,8,128]{2,1,0:T(8,128)S(1)}, f32[24,8,128]{2,1,0:T(8,128)S(1)}, u32[]{:S(2)}, u32[]{:S(2)}) collective-permute-start(f32[24,8,128]{2,1,0:T(8,128)S(1)} %multiply_multiply_fusion.1.own_ref), channel_id=1, source_target_pairs={{1,0},{2,1},{3,2},{4,3},{5,4},{6,5},{7,6},{8,7},{9,8},{10,9},{11,1... | collective-permute-start | bytes 294920 | tf_op jit(solution)/shard_map/ppermute | solution.py:332
  58.8 8.7 %collective-permute-start.6 = (f32[24,8,128]{2,1,0:T(8,128)}, f32[24,8,128]{2,1,0:T(8,128)S(1)}, u32[]{:S(2)}, u32[]{:S(2)}) collective-permute-start(f32[24,8,128]{2,1,0:T(8,128)} %shard_map.64.own_ref), channel_id=1, source_target_pairs={{0,1},{1,2},{2,3},{3,4},{4,5},{5,6},{6,7},{7,8},{8,9},{9,10},{10,1... | collective-permute-start | bytes 294920 | tf_op jit(solution)/shard_map/ppermute | solution.py:330
  64.3 11.0 %collective-permute-start.7 = (f32[24,8,128]{2,1,0:T(8,128)}, f32[24,8,128]{2,1,0:T(8,128)S(1)}, u32[]{:S(2)}, u32[]{:S(2)}) collective-permute-start(f32[24,8,128]{2,1,0:T(8,128)} %shard_map.64.own_ref), channel_id=1, source_target_pairs={{1,0},{2,1},{3,2},{4,3},{5,4},{6,5},{7,6},{8,7},{9,8},{10,9},{11,1... | collective-permute-start | bytes 294920 | tf_op jit(solution)/shard_map/ppermute | solution.py:332
  80.5 4.4 %collective-permute-start.8 = (f32[24,8,128]{2,1,0:T(8,128)}, f32[24,8,128]{2,1,0:T(8,128)S(1)}, u32[]{:S(2)}, u32[]{:S(2)}) collective-permute-start(f32[24,8,128]{2,1,0:T(8,128)} %shard_map.65.own_ref), channel_id=1, source_target_pairs={{0,1},{1,2},{2,3},{3,4},{4,5},{5,6},{6,7},{7,8},{8,9},{9,10},{10,1... | collective-permute-start | bytes 294920 | tf_op jit(solution)/shard_map/ppermute | solution.py:330
  82.4 11.0 %collective-permute-start.9 = (f32[24,8,128]{2,1,0:T(8,128)}, f32[24,8,128]{2,1,0:T(8,128)S(1)}, u32[]{:S(2)}, u32[]{:S(2)}) collective-permute-start(f32[24,8,128]{2,1,0:T(8,128)} %shard_map.65.own_ref), channel_id=1, source_target_pairs={{1,0},{2,1},{3,2},{4,3},{5,4},{6,5},{7,6},{8,7},{9,8},{10,9},{11,1... | collective-permute-start | bytes 294920 | tf_op jit(solution)/shard_map/ppermute | solution.py:332
  98.6 4.8 %collective-permute-start.10 = (f32[24,8,128]{2,1,0:T(8,128)}, f32[24,8,128]{2,1,0:T(8,128)S(1)}, u32[]{:S(2)}, u32[]{:S(2)}) collective-permute-start(f32[24,8,128]{2,1,0:T(8,128)} %shard_map.66.own_ref), channel_id=1, source_target_pairs={{0,1},{1,2},{2,3},{3,4},{4,5},{5,6},{6,7},{7,8},{8,9},{9,10},{10,1... | collective-permute-start | bytes 294920 | tf_op jit(solution)/shard_map/ppermute | solution.py:330
  100.7 11.0 %collective-permute-start.11 = (f32[24,8,128]{2,1,0:T(8,128)}, f32[24,8,128]{2,1,0:T(8,128)S(1)}, u32[]{:S(2)}, u32[]{:S(2)}) collective-permute-start(f32[24,8,128]{2,1,0:T(8,128)} %shard_map.66.own_ref), channel_id=1, source_target_pairs={{1,0},{2,1},{3,2},{4,3},{5,4},{6,5},{7,6},{8,7},{9,8},{10,9},{11,1... | collective-permute-start | bytes 294920 | tf_op jit(solution)/shard_map/ppermute | solution.py:332
  117.7 7.4 %collective-permute-start.12 = (f32[9,24,128]{2,1,0:T(8,128)S(1)}, f32[9,24,128]{2,1,0:T(8,128)S(1)}, u32[]{:S(2)}, u32[]{:S(2)}) collective-permute-start(f32[9,24,128]{2,1,0:T(8,128)S(1)} %get-tuple-element.29), channel_id=1, source_target_pairs={{0,16},{16,32},{32,48},{48,64},{64,80},{80,96},{96,112},{112,128},... | collective-permute-start | bytes 331784 | tf_op jit(solution)/shard_map/ppermute | solution.py:351
  123.2 8.2 %collective-permute-start.13 = (f32[9,24,128]{2,1,0:T(8,128)S(1)}, f32[9,24,128]{2,1,0:T(8,128)S(1)}, u32[]{:S(2)}, u32[]{:S(2)}) collective-permute-start(f32[9,24,128]{2,1,0:T(8,128)S(1)} %get-tuple-element.30), channel_id=1, source_target_pairs={{16,0},{32,16},{48,32},{64,48},{80,64},{96,80},{112,96},{128,112},... | collective-permute-start | bytes 331784 | tf_op jit(solution)/shard_map/ppermute | solution.py:354
  134.5 5.5 %collective-permute-start.14 = (f32[24,8,128]{2,1,0:T(8,128)S(1)}, f32[24,8,128]{2,1,0:T(8,128)S(1)}, u32[]{:S(2)}, u32[]{:S(2)}) collective-permute-start(f32[24,8,128]{2,1,0:T(8,128)S(1)} %multiply_multiply_fusion.own_ref), channel_id=1, source_target_pairs={{0,1},{1,2},{2,3},{3,4},{4,5},{5,6},{6,7},{7,8},{8,9},{9,10},{10,1... | collective-permute-start | bytes 294920 | tf_op jit(solution)/shard_map/ppermute | solution.py:330
  138.1 10.7 %collective-permute-start.15 = (f32[24,8,128]{2,1,0:T(8,128)S(1)}, f32[24,8,128]{2,1,0:T(8,128)S(1)}, u32[]{:S(2)}, u32[]{:S(2)}) collective-permute-start(f32[24,8,128]{2,1,0:T(8,128)S(1)} %multiply_multiply_fusion.own_ref), channel_id=1, source_target_pairs={{1,0},{2,1},{3,2},{4,3},{5,4},{6,5},{7,6},{8,7},{9,8},{10,9},{11,1... | collective-permute-start | bytes 294920 | tf_op jit(solution)/shard_map/ppermute | solution.py:332
  154.0 4.3 %collective-permute-start.16 = (f32[24,8,128]{2,1,0:T(8,128)}, f32[24,8,128]{2,1,0:T(8,128)S(1)}, u32[]{:S(2)}, u32[]{:S(2)}) collective-permute-start(f32[24,8,128]{2,1,0:T(8,128)} %shard_map.68.own_ref), channel_id=1, source_target_pairs={{0,1},{1,2},{2,3},{3,4},{4,5},{5,6},{6,7},{7,8},{8,9},{9,10},{10,1... | collective-permute-start | bytes 294920 | tf_op jit(solution)/shard_map/ppermute | solution.py:330
  155.9 11.0 %collective-permute-start.17 = (f32[24,8,128]{2,1,0:T(8,128)}, f32[24,8,128]{2,1,0:T(8,128)S(1)}, u32[]{:S(2)}, u32[]{:S(2)}) collective-permute-start(f32[24,8,128]{2,1,0:T(8,128)} %shard_map.68.own_ref), channel_id=1, source_target_pairs={{1,0},{2,1},{3,2},{4,3},{5,4},{6,5},{7,6},{8,7},{9,8},{10,9},{11,1... | collective-permute-start | bytes 294920 | tf_op jit(solution)/shard_map/ppermute | solution.py:332
  172.1 4.3 %collective-permute-start.18 = (f32[24,8,128]{2,1,0:T(8,128)}, f32[24,8,128]{2,1,0:T(8,128)S(1)}, u32[]{:S(2)}, u32[]{:S(2)}) collective-permute-start(f32[24,8,128]{2,1,0:T(8,128)} %shard_map.69.own_ref), channel_id=1, source_target_pairs={{0,1},{1,2},{2,3},{3,4},{4,5},{5,6},{6,7},{7,8},{8,9},{9,10},{10,1... | collective-permute-start | bytes 294920 | tf_op jit(solution)/shard_map/ppermute | solution.py:330
  174.0 11.0 %collective-permute-start.19 = (f32[24,8,128]{2,1,0:T(8,128)}, f32[24,8,128]{2,1,0:T(8,128)S(1)}, u32[]{:S(2)}, u32[]{:S(2)}) collective-permute-start(f32[24,8,128]{2,1,0:T(8,128)} %shard_map.69.own_ref), channel_id=1, source_target_pairs={{1,0},{2,1},{3,2},{4,3},{5,4},{6,5},{7,6},{8,7},{9,8},{10,9},{11,1... | collective-permute-start | bytes 294920 | tf_op jit(solution)/shard_map/ppermute | solution.py:332
  190.1 4.3 %collective-permute-start.20 = (f32[24,8,128]{2,1,0:T(8,128)}, f32[24,8,128]{2,1,0:T(8,128)S(1)}, u32[]{:S(2)}, u32[]{:S(2)}) collective-permute-start(f32[24,8,128]{2,1,0:T(8,128)} %shard_map.70.own_ref), channel_id=1, source_target_pairs={{0,1},{1,2},{2,3},{3,4},{4,5},{5,6},{6,7},{7,8},{8,9},{9,10},{10,1... | collective-permute-start | bytes 294920 | tf_op jit(solution)/shard_map/ppermute | solution.py:330
  192.1 11.0 %collective-permute-start.21 = (f32[24,8,128]{2,1,0:T(8,128)}, f32[24,8,128]{2,1,0:T(8,128)S(1)}, u32[]{:S(2)}, u32[]{:S(2)}) collective-permute-start(f32[24,8,128]{2,1,0:T(8,128)} %shard_map.70.own_ref), channel_id=1, source_target_pairs={{1,0},{2,1},{3,2},{4,3},{5,4},{6,5},{7,6},{8,7},{9,8},{10,9},{11,1... | collective-permute-start | bytes 294920 | tf_op jit(solution)/shard_map/ppermute | solution.py:332
  208.8 6.1 %collective-permute-start.22 = (f32[4,8,128]{2,1,0:T(8,128)S(1)}, f32[4,8,128]{2,1,0:T(8,128)S(1)}, u32[]{:S(2)}, u32[]{:S(2)}) collective-permute-start(f32[4,8,128]{2,1,0:T(8,128)S(1)} %get-tuple-element.27), channel_id=1, source_target_pairs={{0,16},{16,32},{32,48},{48,64},{64,80},{80,96},{96,112},{112,128},... | collective-permute-start | bytes 49160 | tf_op jit(solution)/shard_map/ppermute | solution.py:366
  213.0 7.2 %collective-permute-start.23 = (f32[4,8,128]{2,1,0:T(8,128)S(1)}, f32[4,8,128]{2,1,0:T(8,128)S(1)}, u32[]{:S(2)}, u32[]{:S(2)}) collective-permute-start(f32[4,8,128]{2,1,0:T(8,128)S(1)} %get-tuple-element.28), channel_id=1, source_target_pairs={{16,0},{32,16},{48,32},{64,48},{80,64},{96,80},{112,96},{128,112},... | collective-permute-start | bytes 49160 | tf_op jit(solution)/shard_map/ppermute | solution.py:369
  (31 other events, 120.1 us)
